TPU v7x, 512 devices: a whole 4x4x16 slice. The times are simulated.
512 devices in a mesh: xb: 16 (over x, y), zs: 32 (over z, core).
Axes of the slice: x: 4, y: 4, z: 16, core: 2. Of those that a mesh axis runs over, the one named last changes fastest.
Arguments:
- partials: bfloat16 [16384, 32768], P(('xb', 'zs')), may hold values from -6 to 6
- routes: int32 [512, 32], P(('xb', 'zs')), may hold values from 0 to 255, as said below
- taps: float32 [3, 129], replicated, may hold values from 0.25 to 2.5
Outputs:
- gradient: float32 [1024, 1024, 128], P('xb', 'zs')
- smoothed: float32 [1024, 1024, 128], P('xb', 'zs')
Inputs may be any that keep to these rules, and one draw needn't show every extreme that they name: `routes`: an entry v of a device's list names local block v % (8) of the device with zs index v // 8 in the same xb group; the entries of one list that name the same owner all name the same block, and no owner is named by more than two entries of one list.
All inputs are finite; a program needn't handle non-finite values.
Results may differ from a plain program's by a relative error of at most 0.0077.
Values may be sent and summed in bfloat16 or wider, within the bound.
No kernel may reach another device: no remote copies, remote signals or barrier semaphores. Data moves between devices by JAX's collectives and lax.ppermute only.
A program may use at most 64 MiB of HBM per device.

v0:
```python
import jax
import jax.numpy as jnp
from jax import lax
from jax.sharding import PartitionSpec as P

BLK = 32
YBLOCKS = 4
CELLS = 32768
CX = 64
CZ = 32
REACH = 64
NY = 128


def extended_2(x, sides, width):
    for axis, dim in sides:
        count, length = (lax.axis_size(axis), x.shape[dim])
        up = [(i, (i + 1) % count) for i in range(count - 1)]
        down = [(j, i) for i, j in up]
        last = lax.slice_in_dim(x, length - width, length, axis=dim)
        initial = lax.slice_in_dim(x, 0, width, axis=dim)
        before = lax.ppermute(last, axis, up)
        after = lax.ppermute(initial, axis, down)
        x = jnp.concatenate([before, x, after], axis=dim)
    return x


def band_matrix(kern_row, rows, cols, offset):
    border = rows + cols
    widened = jnp.pad(kern_row, ((border, border),))
    front = widened[offset + border : offset + border + cols]
    behind = widened[offset + border - rows : offset + border]
    cycle = jnp.concatenate([front, behind])
    period = rows + cols - 1
    tiled = jnp.tile(cycle, rows)[: rows * period]
    return tiled.reshape(rows, period)[:, :cols]


def body(partials, routes, taps):
    owners_count = lax.axis_size("zs")
    blocks_local = 2 * YBLOCKS
    entries = routes[0]
    owner = entries // blocks_local
    block_id = entries % blocks_local
    owner_hit = owner[:, None] == jnp.arange(owners_count)[None, :]
    hit_count = owner_hit.astype(jnp.int32)
    earlier = jnp.cumsum(hit_count, axis=0) - hit_count
    rank = jnp.sum(earlier * hit_count, axis=1)
    target = owner * 2 + rank
    select = target[None, :] == jnp.arange(2 * owners_count)[:, None]
    packed = jnp.dot(select.astype(jnp.bfloat16), partials, preferred_element_type=jnp.float32)
    packed = packed.astype(jnp.bfloat16).reshape(owners_count, 2, CELLS)
    packed_ids = jnp.sum(jnp.where(select, block_id[None, :], 0), axis=1).reshape(owners_count, 2)
    arrived, arrived_ids = (
        lax.all_to_all(packed, "zs", split_axis=0, concat_axis=0, tiled=True),
        lax.all_to_all(packed_ids, "zs", split_axis=0, concat_axis=0, tiled=True),
    )
    contrib = (arrived[:, 0].astype(jnp.float32) + arrived[:, 1].astype(jnp.float32)).astype(
        jnp.bfloat16
    )
    source_ids = arrived_ids[:, 0]
    placing = (source_ids[None, :] == jnp.arange(blocks_local)[:, None]).astype(jnp.bfloat16)
    assembled = jnp.dot(placing, contrib, preferred_element_type=jnp.float32)
    assembled = assembled.reshape(2, YBLOCKS, BLK, BLK, BLK).transpose(0, 2, 4, 1, 3)
    gradient = assembled.reshape(CX, CZ, NY)
    norms = jnp.sqrt(jnp.sum(taps * taps, axis=1, keepdims=True))
    kernel = (taps / norms).astype(jnp.bfloat16)
    field = gradient.astype(jnp.bfloat16)
    padded = extended_2(field, (("xb", 0),), CX)
    x_matrix = band_matrix(kernel[0], CX, 3 * CX, 0)
    along_x = jnp.dot(x_matrix, padded.reshape(3 * CX, CZ * NY), preferred_element_type=jnp.float32)
    along_x = along_x.astype(jnp.bfloat16).reshape(CX, CZ, NY)
    y_matrix = band_matrix(kernel[1], NY, NY, REACH)
    along_y = jnp.einsum(
        "ab,xzb->xza", y_matrix, along_x, preferred_element_type=jnp.float32
    ).astype(jnp.bfloat16)
    line_length = CZ * owners_count
    columns = CX * NY // owners_count
    z_major = along_y.transpose(1, 0, 2).reshape(CZ, owners_count, columns)
    z_matrix = band_matrix(kernel[2], REACH, 3 * REACH, 0)
    lines = lax.all_to_all(z_major, "zs", split_axis=1, concat_axis=0, tiled=True)
    flat = lines.reshape(line_length, lines.shape[2])
    extended = jnp.pad(flat, ((REACH, REACH), (0, 0)))
    pieces = extended.reshape(line_length // REACH + 2, REACH, flat.shape[1])
    windows = jnp.concatenate([pieces[:-2], pieces[1:-1], pieces[2:]], axis=1)
    filtered = jnp.einsum("ij,bjm->bim", z_matrix, windows, preferred_element_type=jnp.float32)
    filtered = filtered.reshape(line_length, 1, flat.shape[1])
    returned = lax.all_to_all(filtered, "zs", split_axis=0, concat_axis=1, tiled=True)
    smoothed = returned.reshape(CZ, CX, NY).transpose(1, 0, 2)
    return (gradient, smoothed)


def solution(mesh):
    placed = (P(("xb", "zs"), None), P(("xb", "zs"), None), P())
    return jax.shard_map(
        body,
        mesh=mesh,
        in_specs=placed,
        out_specs=(P("xb", "zs", None), P("xb", "zs", None)),
        check_vma=False,
    )
```

profile of v0, /device:TPU:7, one launch (start us, length us, event | category | flops | bytes accessed | tf_op | source)
XLA Modules:
  0.0 407.5 jit_solution(13148397627251615303)
XLA Ops:
  0.6 0.8 and_select_fusion.1
  1.5 0.1 fusion.14
  1.5 0.1 reduce_window_sum.11
  1.6 0.2 select_reduce_fusion.1
  1.8 0.7 fusion.20
  2.4 0.1 select_reduce_fusion
  2.5 0.7 all_to_all.33
  3.3 15.9 %all-to-all-start = ((s32[32,1,2]{2,1,0:T(1,128)}), s32[32,1,2]{2,1,0:T(1,128)S(1)}, u32[]{:S(2)}, u32[]{:S(2)}) async-start(s32[32,1,2]{2,1,0:T(1,128)} %bitcast.4), calls=%async_computation | async-start | bytes 32768 | tf_op jit(solution)/shard_map/all_to_all | solution.py:56
  19.2 3.3 convolution_convert_fusion
  22.5 7.6 %reshape.109 = bf16[32,2,32768]{2,1,0:T(2,128)(2,1)} reshape(bf16[64,32768]{1,0:T(8,128)(2,1)} %convolution_convert_fusion) | data formatting | bytes 8388608 | tf_op jit(solution)/shard_map/reshape | solution.py:52
  30.1 0.8 all-to-all-done
  30.9 11.6 %all-to-all-start.1 = ((bf16[32,2,32768]{2,1,0:T(2,128)(2,1)}), bf16[32,2,32768]{2,1,0:T(2,128)(2,1)}, u32[]{:S(2)}, u32[]{:S(2)}) async-start(bf16[32,2,32768]{2,1,0:T(2,128)(2,1)} %reshape.109), calls=%async_computation.1 | async-start | bytes 8388608 | tf_op jit(solution)/shard_map/all_to_all | solution.py:55
  42.5 0.1 multiply_reduce_fusion
  42.7 0.1 divide_convert_fusion
  42.8 0.1 copy.35
  42.9 182.9 %all-to-all-done.1 = bf16[32,2,32768]{2,1,0:T(2,128)(2,1)} async-done(((bf16[32,2,32768]{2,1,0:T(2,128)(2,1)}), bf16[32,2,32768]{2,1,0:T(2,128)(2,1)}, u32[]{:S(2)}, u32[]{:S(2)}) %all-to-all-start.1) | async-done | bytes 4194336 | tf_op jit(solution)/shard_map/all_to_all | solution.py:55
  225.8 9.0 %fusion.23 = (bf16[32,1,32768]{2,1,0:T(2,128)(2,1)S(1)}, bf16[32,1,32768]{2,1,0:T(2,128)(2,1)S(1)}) fusion(bf16[32,2,32768]{2,1,0:T(2,128)(2,1)} %all-to-all-done.1), kind=kLoop, calls=%fused_computation.61 | loop fusion | bytes 8388608 | tf_op jit(solution)/shard_map/slice | solution.py:58
  234.8 5.9 %fusion = bf16[32768,32]{0,1:T(8,128)(2,1)} fusion(bf16[32,1,32768]{2,1,0:T(2,128)(2,1)S(1)} %get-tuple-element.14, bf16[32,1,32768]{2,1,0:T(2,128)(2,1)S(1)} %get-tuple-element.13), kind=kLoop, calls=%fused_computation.4 | loop fusion | flops 4194304 | bytes 6291456 | tf_op jit(solution)/shard_map/dot_general | solution.py:63
  240.6 7.4 %copy.46 = bf16[32768,32]{1,0:T(8,128)(2,1)} copy(bf16[32768,32]{0,1:T(8,128)(2,1)} %fusion) | data formatting | bytes 4194304 | tf_op jit(solution)/shard_map/dot_general | solution.py:63
  248.0 16.3 %convolution_bitcast_fusion = f32[2,32,32,4,32]{2,3,4,1,0:T(4,128)} fusion(bf16[32,32,32,32,1]{3,2,1,0,4:T(8,128)(2,1)} %bitcast.86, s32[2,4]{1,0:T(2,128)S(1)} %multiply_add_fusion, s32[32]{0:T(128)S(1)} %slice_bitcast_fusion.4), kind=kOutput, calls=%fused_computation.3 | convolution fusion | flops 16777472 | bytes 3145888 | tf_op jit(solution)/shard_map/dot_general | solution.py:63
  264.3 6.3 %copy.39 = f32[2,32,32,4,32]{4,3,2,1,0:T(4,128)} copy(f32[2,32,32,4,32]{2,3,4,1,0:T(4,128)} %convolution_bitcast_fusion) | data formatting | bytes 2097152 | tf_op jit(solution)/shard_map/transpose | solution.py:64
  270.5 3.7 reshape.110
  274.3 1.0 convert_element_type.51
  275.3 3.2 collective-permute-start
  278.5 4.4 %collective-permute-start.1 = (bf16[64,32,128]{2,1,0:T(8,128)(2,1)}, bf16[64,32,128]{2,1,0:T(8,128)(2,1)}, u32[]{:S(2)}, u32[]{:S(2)}) collective-permute-start(bf16[64,32,128]{2,1,0:T(8,128)(2,1)} %convert_element_type.51), channel_id=1, source_target_pairs={{32,0},{64,32},{96,64},{128,96},{160,128},{192,160},{224,192},{256... | collective-permute-start | bytes 1572872 | tf_op jit(solution)/shard_map/ppermute | solution.py:23
  283.0 0.2 reshape.111
  283.2 0.1 pad_slice_fusion.3
  283.3 0.3 reshape.114
  283.7 8.6 %collective-permute-done = bf16[64,32,128]{2,1,0:T(8,128)(2,1)} collective-permute-done((bf16[64,32,128]{2,1,0:T(8,128)(2,1)}, bf16[64,32,128]{2,1,0:T(8,128)(2,1)}, u32[]{:S(2)}, u32[]{:S(2)}) %collective-permute-start) | collective-permute-done | bytes 524320 | tf_op jit(solution)/shard_map/ppermute | solution.py:22
  292.2 0.9 collective-permute-done.1
  293.1 1.5 pad_maximum_fusion
  294.6 0.6 fusion.10
  295.3 0.1 copy.53
  295.4 0.3 fusion.9
  295.7 0.2 copy.40
  295.9 0.2 reshape.115
  296.1 1.1 copy.41
  297.2 11.8 %all-to-all-start.2 = ((bf16[32,32,256]{2,0,1:T(8,128)(2,1)}), bf16[32,32,256]{2,0,1:T(8,128)(2,1)S(1)}, u32[]{:S(2)}, u32[]{:S(2)}) async-start(bf16[32,32,256]{2,0,1:T(8,128)(2,1)} %copy.41), calls=%async_computation.2 | async-start | bytes 1048576 | tf_op jit(solution)/shard_map/all_to_all | solution.py:81
  309.0 0.2 reshape.117
  309.2 33.3 %all-to-all-done.2 = bf16[32,32,256]{2,0,1:T(8,128)(2,1)S(1)} async-done(((bf16[32,32,256]{2,0,1:T(8,128)(2,1)}), bf16[32,32,256]{2,0,1:T(8,128)(2,1)S(1)}, u32[]{:S(2)}, u32[]{:S(2)}) %all-to-all-start.2) | async-done | bytes 524320 | tf_op jit(solution)/shard_map/all_to_all | solution.py:81
  342.4 0.1 pad_slice_fusion.1
  342.5 0.4 fusion.3
  342.9 1.1 copy.42
  344.0 59.0 %all_to_all.47 = f32[1024,1,256]{2,1,0:T(1,128)S(1)} all-to-all(f32[1024,1,256]{2,1,0:T(1,128)S(1)} %copy.42), channel_id=1, replica_groups=mesh['xb'=16,'zs'=32] {'zs'}, dimensions={0} | all-to-all | bytes 2097152 | tf_op jit(solution)/shard_map/all_to_all | solution.py:88
  403.0 0.1 copy.47
  403.0 0.6 copy.43
  403.7 1.1 reshape.119
  404.7 2.8 copy.44
  (20 shorter events, 0.2 us)
Async XLA Ops:
  0.6 18.6 %copy-start = (bf16[32,32768]{1,0:T(8,128)(2,1)S(1)}, bf16[32,32768]{1,0:T(8,128)(2,1)}, u32[]{:S(2)}) copy-start(bf16[32,32768]{1,0:T(8,128)(2,1)} %param.3) | copy-start | bytes 6291460
  3.3 27.6 %all-to-all-start = ((s32[32,1,2]{2,1,0:T(1,128)}), s32[32,1,2]{2,1,0:T(1,128)S(1)}, u32[]{:S(2)}, u32[]{:S(2)}) async-start(s32[32,1,2]{2,1,0:T(1,128)} %bitcast.4), calls=%async_computation | async-start | bytes 32768 | tf_op jit(solution)/shard_map/all_to_all | solution.py:56
  30.1 12.4 %copy-start.2 = (f32[3,129]{1,0:T(4,128)S(1)}, f32[3,129]{1,0:T(4,128)}, u32[]{:S(2)}) copy-start(f32[3,129]{1,0:T(4,128)} %param.5) | copy-start | bytes 4648
  30.9 194.9 %all-to-all-start.1 = ((bf16[32,2,32768]{2,1,0:T(2,128)(2,1)}), bf16[32,2,32768]{2,1,0:T(2,128)(2,1)}, u32[]{:S(2)}, u32[]{:S(2)}) async-start(bf16[32,2,32768]{2,1,0:T(2,128)(2,1)} %reshape.109), calls=%async_computation.1 | async-start | bytes 8388608 | tf_op jit(solution)/shard_map/all_to_all | solution.py:55
  274.3 21.0 %copy-start.1 = (f32[64,32,128]{2,1,0:T(8,128)}, f32[64,32,128]{2,1,0:T(8,128)S(1)}, u32[]{:S(2)}) copy-start(f32[64,32,128]{2,1,0:T(8,128)S(1)} %reshape.110) | copy-start | bytes 3145732
  275.3 16.9 %collective-permute-start = (bf16[64,32,128]{2,1,0:T(8,128)(2,1)}, bf16[64,32,128]{2,1,0:T(8,128)(2,1)}, u32[]{:S(2)}, u32[]{:S(2)}) collective-permute-start(bf16[64,32,128]{2,1,0:T(8,128)(2,1)} %convert_element_type.51), channel_id=1, source_target_pairs={{0,32},{32,64},{64,96},{96,128},{128,160},{160,192},{192,224},{224... | collective-permute-start | bytes 1572872 | tf_op jit(solution)/shard_map/ppermute | solution.py:22
  278.5 14.6 %collective-permute-start.1 = (bf16[64,32,128]{2,1,0:T(8,128)(2,1)}, bf16[64,32,128]{2,1,0:T(8,128)(2,1)}, u32[]{:S(2)}, u32[]{:S(2)}) collective-permute-start(bf16[64,32,128]{2,1,0:T(8,128)(2,1)} %convert_element_type.51), channel_id=1, source_target_pairs={{32,0},{64,32},{96,64},{128,96},{160,128},{192,160},{224,192},{256... | collective-permute-start | bytes 1572872 | tf_op jit(solution)/shard_map/ppermute | solution.py:23
  297.2 45.3 %all-to-all-start.2 = ((bf16[32,32,256]{2,0,1:T(8,128)(2,1)}), bf16[32,32,256]{2,0,1:T(8,128)(2,1)S(1)}, u32[]{:S(2)}, u32[]{:S(2)}) async-start(bf16[32,32,256]{2,0,1:T(8,128)(2,1)} %copy.41), calls=%async_computation.2 | async-start | bytes 1048576 | tf_op jit(solution)/shard_map/all_to_all | solution.py:81
where the time goes:
time: 410 us; the launch traced here: 408 us
  waiting for transfers between devices  226 us (55%)
  blocking collectives  59 us (14%)
  starting transfers between devices  46.9 us (11%)
  local copies, waits for them, and re-layouts  43 us (10%)
  matrix products  21 us (5%)
  other arithmetic  10.5 us (3%)
    all_to_all x1, waiting for transfers between devices, body(): lax.all_to_all(packed, 'zs', split_axis=0, concat_axis=0, tiled=True)  183 us
    all_to_all x1, blocking collectives, body(): lax.all_to_all(filtered, 'zs', split_axis=0, concat_axis=1, tiled=True)  59 us
    all_to_all x1, waiting for transfers between devices, body(): lax.all_to_all(z_major, 'zs', split_axis=1, concat_axis=0, tiled=True)  33.3 us
    dot_general x1, matrix products, body(): assembled = jnp.dot(placing, contrib, preferred_element_type=jnp.float32)  16.3 us
    all_to_all x1, starting transfers between devices, body(): lax.all_to_all(packed_ids, 'zs', split_axis=0, concat_axis=0, tiled=True)  15.9 us
    all_to_all x1, starting transfers between devices, body(): lax.all_to_all(z_major, 'zs', split_axis=1, concat_axis=0, tiled=True)  11.8 us
    all_to_all x1, starting transfers between devices, body(): lax.all_to_all(packed, 'zs', split_axis=0, concat_axis=0, tiled=True)  11.6 us
    slice x1, local copies, waits for them, and re-layouts, body(): arrived[:, 0].astype(jnp.float32) + arrived[:, 1].astype(jnp.float32)  8.97 us
  transfers between devices with their start and end apart: 5, of which 5 were waited for; matrix products, arithmetic and copies ran while one was open for 3% of the time, Pallas kernels for 0%

commit v1 on v0

v1 whole, which is shorter than its diff:
```python
import jax
import jax.numpy as jnp
from jax import lax
from jax.sharding import PartitionSpec as P

BLK = 32
YBLOCKS = 4
CELLS = 32768
CX = 64
CZ = 32
REACH = 64
NY = 128


def shifted(x, axis, step):
    count = lax.axis_size(axis)
    pairs = [(i, i + step) for i in range(count) if 0 <= i + step < count]
    return lax.ppermute(x, axis, pairs)


def band_matrix(kern_row, rows, cols, offset):
    border = rows + cols
    widened = jnp.pad(kern_row, ((border, border),))
    front = widened[offset + border : offset + border + cols]
    behind = widened[offset + border - rows : offset + border]
    cycle = jnp.concatenate([front, behind])
    period = rows + cols - 1
    tiled = jnp.tile(cycle, rows)[: rows * period]
    return tiled.reshape(rows, period)[:, :cols]


def body(partials, routes, taps):
    owners_count = lax.axis_size("zs")
    blocks_local = 2 * YBLOCKS
    entries = routes[0]
    owner = entries // blocks_local
    block_id = entries % blocks_local
    select = owner[None, :] == jnp.arange(owners_count)[:, None]
    packed = jnp.dot(select.astype(jnp.bfloat16), partials, preferred_element_type=jnp.float32)
    packed = packed.astype(jnp.bfloat16)
    packed_ids = jnp.max(jnp.where(select, block_id[None, :], 0), axis=1).reshape(owners_count, 1)
    arrived = lax.all_to_all(packed, "zs", split_axis=0, concat_axis=0, tiled=True)
    arrived_ids = lax.all_to_all(packed_ids, "zs", split_axis=0, concat_axis=0, tiled=True)
    placing = (arrived_ids[:, 0][None, :] == jnp.arange(blocks_local)[:, None]).astype(jnp.bfloat16)
    assembled = jnp.dot(placing, arrived, preferred_element_type=jnp.float32)
    assembled = assembled.reshape(2, YBLOCKS, BLK, BLK, BLK).transpose(0, 2, 4, 1, 3)
    gradient = assembled.reshape(CX, CZ, NY)
    norms = jnp.sqrt(jnp.sum(taps * taps, axis=1, keepdims=True))
    kernel = (taps / norms).astype(jnp.bfloat16)
    field = gradient.astype(jnp.bfloat16)
    padded = jnp.concatenate(
        [shifted(field, "xb", 1), field, shifted(field, "xb", -1)], axis=0
    )
    x_matrix = band_matrix(kernel[0], CX, 3 * CX, 0)
    along_x = jnp.dot(x_matrix, padded.reshape(3 * CX, CZ * NY), preferred_element_type=jnp.float32)
    along_x = along_x.astype(jnp.bfloat16).reshape(CX, CZ, NY)
    y_matrix = band_matrix(kernel[1], NY, NY, REACH)
    along_y = jnp.einsum(
        "ab,xzb->xza", y_matrix, along_x, preferred_element_type=jnp.float32
    ).astype(jnp.bfloat16)
    reach_slabs = REACH // CZ
    halo_lo = [shifted(along_y, "zs", s) for s in range(reach_slabs, 0, -1)]
    halo_hi = [shifted(along_y, "zs", -s) for s in range(1, reach_slabs + 1)]
    extended = jnp.concatenate(halo_lo + [along_y] + halo_hi, axis=1)
    z_matrix = band_matrix(kernel[2], CZ, CZ + 2 * REACH, 0)
    smoothed = jnp.einsum(
        "zk,xky->xzy", z_matrix, extended, preferred_element_type=jnp.float32
    )
    return (gradient, smoothed)


def solution(mesh):
    placed = (P(("xb", "zs"), None), P(("xb", "zs"), None), P())
    return jax.shard_map(
        body,
        mesh=mesh,
        in_specs=placed,
        out_specs=(P("xb", "zs", None), P("xb", "zs", None)),
        check_vma=False,
    )
```

time: 410 us -> 245 us (0.60)
  the two profiles are of different devices: /device:TPU:7 before, /device:TPU:24 now
where the time goes in v1:
time: 245 us; the launch traced here: 243 us
  waiting for transfers between devices  130 us (53%)
  local copies, waits for them, and re-layouts  43.3 us (18%)
  starting transfers between devices  39.8 us (16%)
  matrix products  20.7 us (8%)
  other arithmetic  8.86 us (4%)
    all_to_all x1, waiting for transfers between devices, body(): lax.all_to_all(packed, 'zs', split_axis=0, concat_axis=0, tiled=True)  98.3 us
    ppermute x6, waiting for transfers between devices, shifted(): return lax.ppermute(x, axis, pairs)  30.6 us
    unnamed x17, local copies, waits for them, and re-layouts  18.6 us
    dot_general x1, matrix products, body(): assembled = jnp.dot(placing, arrived, preferred_element_type=jnp.float32)  16.3 us
    all_to_all x1, starting transfers between devices, body(): lax.all_to_all(packed_ids, 'zs', split_axis=0, concat_axis=0, tiled=True)  15.5 us
    ppermute x6, starting transfers between devices, shifted(): return lax.ppermute(x, axis, pairs)  12.7 us
    dot_general x1, local copies, waits for them, and re-layouts, body(): assembled = jnp.dot(placing, arrived, preferred_element_type=jnp.float32)  12.6 us
    all_to_all x1, starting transfers between devices, body(): lax.all_to_all(packed, 'zs', split_axis=0, concat_axis=0, tiled=True)  11.6 us
  transfers between devices with their start and end apart: 8, of which 6 were waited for; matrix products, arithmetic and copies ran while one was open for 7% of the time, Pallas kernels for 0%

profile of v1, /device:TPU:24, one launch (start us, length us, event | category | flops | bytes accessed | tf_op | source)
XLA Modules:
  0.0 243.2 jit_solution(11649939339041843083)
XLA Ops:
  0.6 0.0 copy-start
  0.6 0.8 fusion.12
  1.5 0.1 select_reduce_fusion
  1.6 0.7 copy.16
  2.3 15.5 %all-to-all-start = ((s32[32,1,1]{2,1,0:T(1,128)}), s32[32,1,1]{2,1,0:T(1,128)S(1)}, u32[]{:S(2)}, u32[]{:S(2)}) async-start(s32[32,1,1]{2,1,0:T(1,128)} %copy.16), calls=%async_computation | async-start | bytes 32768 | tf_op jit(solution)/shard_map/all_to_all | solution.py:43
  17.8 2.0 fusion
  19.8 0.5 broadcast.72
  20.3 4.6 %reduce.7 = bf16[32,32768]{1,0:T(8,128)(2,1)} reduce(bf16[32,1,32768]{2,0,1:T(8,128)(2,1)} %fusion, bf16[]{:T(256)} %broadcast.72), dimensions={1}, to_apply=%copy.17.reduce_sub_computation | reduce | bytes 4194306 | tf_op jit(solution)/shard_map/all_to_all | solution.py:42
  24.8 4.5 %reshape.71 = bf16[32,2,16384]{2,1,0:T(2,128)(2,1)} reshape(bf16[32,32768]{1,0:T(8,128)(2,1)} %reduce.7) | data formatting | bytes 4194304
  29.3 0.8 all-to-all-done
  30.2 11.6 %all-to-all-start.1 = ((bf16[32,2,16384]{2,1,0:T(2,128)(2,1)}), bf16[32,2,16384]{2,1,0:T(2,128)(2,1)}, u32[]{:S(2)}, u32[]{:S(2)}) async-start(bf16[32,2,16384]{2,1,0:T(2,128)(2,1)} %reshape.71), calls=%async_computation.1 | async-start | bytes 4194304 | tf_op jit(solution)/shard_map/all_to_all | solution.py:42
  41.8 0.1 multiply_reduce_fusion
  41.9 0.1 divide_convert_fusion
  42.1 0.7 reduce
  42.7 98.3 %all-to-all-done.1 = bf16[32,2,16384]{2,1,0:T(2,128)(2,1)} async-done(((bf16[32,2,16384]{2,1,0:T(2,128)(2,1)}), bf16[32,2,16384]{2,1,0:T(2,128)(2,1)}, u32[]{:S(2)}, u32[]{:S(2)}) %all-to-all-start.1) | async-done | bytes 2097184 | tf_op jit(solution)/shard_map/all_to_all | solution.py:42
  141.0 10.5 %reshape.72 = bf16[32,1,32768]{2,1,0:T(2,128)(2,1)} reshape(bf16[32,2,16384]{2,1,0:T(2,128)(2,1)} %all-to-all-done.1) | data formatting | bytes 4194304
  151.5 12.6 %copy.22 = bf16[32,1,32768]{0,2,1:T(8,128)(2,1)} copy(bf16[32,1,32768]{2,1,0:T(2,128)(2,1)} %reshape.72) | data formatting | bytes 4194304 | tf_op jit(solution)/shard_map/dot_general | solution.py:45
  164.1 16.3 %convolution_bitcast_fusion = f32[2,32,32,4,32]{2,3,4,1,0:T(4,128)} fusion(bf16[32,32,32,32,1]{3,2,1,0,4:T(8,128)(2,1)} %bitcast.52, s32[2,4]{1,0:T(2,128)S(1)} %multiply_add_fusion, s32[32]{0:T(128)S(1)} %reduce), kind=kOutput, calls=%fused_computation.3 | convolution fusion | flops 16777472 | bytes 3145888 | tf_op jit(solution)/shard_map/dot_general | solution.py:45
  180.3 6.3 %copy.19 = f32[2,32,32,4,32]{4,3,2,1,0:T(4,128)} copy(f32[2,32,32,4,32]{2,3,4,1,0:T(4,128)} %convolution_bitcast_fusion) | data formatting | bytes 2097152 | tf_op jit(solution)/shard_map/transpose | solution.py:46
  186.6 3.7 %reshape.57 = f32[64,32,128]{2,1,0:T(8,128)S(1)} reshape(f32[2,32,32,4,32]{4,3,2,1,0:T(4,128)} %copy.19) | data formatting | bytes 2097152 | tf_op jit(solution)/shard_map/reshape | solution.py:47
  190.4 0.0 copy-start.1
  190.4 1.0 convert_element_type.24
  191.3 3.0 %collective-permute-start = (bf16[64,32,128]{2,1,0:T(8,128)(2,1)}, bf16[64,32,128]{2,1,0:T(8,128)(2,1)}, u32[]{:S(2)}, u32[]{:S(2)}) collective-permute-start(bf16[64,32,128]{2,1,0:T(8,128)(2,1)} %convert_element_type.24), channel_id=1, source_target_pairs={{0,32},{32,64},{64,96},{96,128},{128,160},{160,192},{192,224},{224... | collective-permute-start | bytes 1572872 | tf_op jit(solution)/shard_map/ppermute | solution.py:18
  194.4 2.8 %collective-permute-start.1 = (bf16[64,32,128]{2,1,0:T(8,128)(2,1)}, bf16[64,32,128]{2,1,0:T(8,128)(2,1)}, u32[]{:S(2)}, u32[]{:S(2)}) collective-permute-start(bf16[64,32,128]{2,1,0:T(8,128)(2,1)} %convert_element_type.24), channel_id=1, source_target_pairs={{32,0},{64,32},{96,64},{128,96},{160,128},{192,160},{224,192},{256... | collective-permute-start | bytes 1572872 | tf_op jit(solution)/shard_map/ppermute | solution.py:18
  197.2 0.2 reshape.58
  197.4 0.1 pad_slice_fusion.1
  197.5 0.1 copy.26
  197.6 0.3 reshape.61
  197.9 9.1 %collective-permute-done = bf16[64,32,128]{2,1,0:T(8,128)(2,1)} collective-permute-done((bf16[64,32,128]{2,1,0:T(8,128)(2,1)}, bf16[64,32,128]{2,1,0:T(8,128)(2,1)}, u32[]{:S(2)}, u32[]{:S(2)}) %collective-permute-start) | collective-permute-done | bytes 524320 | tf_op jit(solution)/shard_map/ppermute | solution.py:18
  207.0 4.9 %collective-permute-done.1 = bf16[64,32,128]{2,1,0:T(8,128)(2,1)} collective-permute-done((bf16[64,32,128]{2,1,0:T(8,128)(2,1)}, bf16[64,32,128]{2,1,0:T(8,128)(2,1)}, u32[]{:S(2)}, u32[]{:S(2)}) %collective-permute-start.1) | collective-permute-done | bytes 524320 | tf_op jit(solution)/shard_map/ppermute | solution.py:18
  211.9 1.5 pad_maximum_fusion
  213.4 0.6 fusion.3
  214.1 0.1 copy.25
  214.2 0.3 convolution_convert_fusion.2
  214.5 2.2 collective-permute-start.2
  216.6 2.1 collective-permute-start.3
  218.7 1.3 collective-permute-start.4
  220.0 1.3 collective-permute-start.5
  221.4 0.1 tile.32
  221.5 0.1 reshape.62
  221.6 6.6 %collective-permute-done.2 = bf16[64,32,128]{2,1,0:T(8,128)(2,1)} collective-permute-done((bf16[64,32,128]{2,1,0:T(8,128)(2,1)S(1)}, bf16[64,32,128]{2,1,0:T(8,128)(2,1)}, u32[]{:S(2)}, u32[]{:S(2)}) %collective-permute-start.2) | collective-permute-done | bytes 524320 | tf_op jit(solution)/shard_map/ppermute | solution.py:18
  228.2 1.1 constant_dynamic-update-slice_fusion.4
  229.3 1.1 constant_dynamic-update-slice_fusion.3
  230.4 0.1 constant_dynamic-update-slice_fusion.2
  230.5 1.1 constant_dynamic-update-slice_fusion.1
  231.6 10.0 %collective-permute-done.5 = bf16[64,32,128]{2,1,0:T(8,128)(2,1)S(1)} collective-permute-done((bf16[64,32,128]{2,1,0:T(8,128)(2,1)S(1)}, bf16[64,32,128]{2,1,0:T(8,128)(2,1)S(1)}, u32[]{:S(2)}, u32[]{:S(2)}) %collective-permute-start.5) | collective-permute-done | bytes 524320 | tf_op jit(solution)/shard_map/ppermute | solution.py:18
  241.6 0.1 constant_dynamic-update-slice_fusion
  241.7 1.5 convolution_bitcast_fusion.1
  (18 shorter events, 0.1 us)
Async XLA Ops:
  0.6 17.1 %copy-start = (bf16[32,32768]{1,0:T(8,128)(2,1)S(1)}, bf16[32,32768]{1,0:T(8,128)(2,1)}, u32[]{:S(2)}) copy-start(bf16[32,32768]{1,0:T(8,128)(2,1)} %param.3) | copy-start | bytes 6291460
  2.3 27.9 %all-to-all-start = ((s32[32,1,1]{2,1,0:T(1,128)}), s32[32,1,1]{2,1,0:T(1,128)S(1)}, u32[]{:S(2)}, u32[]{:S(2)}) async-start(s32[32,1,1]{2,1,0:T(1,128)} %copy.16), calls=%async_computation | async-start | bytes 32768 | tf_op jit(solution)/shard_map/all_to_all | solution.py:43
  29.3 12.5 %copy-start.2 = (f32[3,129]{1,0:T(4,128)S(1)}, f32[3,129]{1,0:T(4,128)}, u32[]{:S(2)}) copy-start(f32[3,129]{1,0:T(4,128)} %param.5) | copy-start | bytes 4648
  30.2 110.9 %all-to-all-start.1 = ((bf16[32,2,16384]{2,1,0:T(2,128)(2,1)}), bf16[32,2,16384]{2,1,0:T(2,128)(2,1)}, u32[]{:S(2)}, u32[]{:S(2)}) async-start(bf16[32,2,16384]{2,1,0:T(2,128)(2,1)} %reshape.71), calls=%async_computation.1 | async-start | bytes 4194304 | tf_op jit(solution)/shard_map/all_to_all | solution.py:42
  190.4 23.7 %copy-start.1 = (f32[64,32,128]{2,1,0:T(8,128)}, f32[64,32,128]{2,1,0:T(8,128)S(1)}, u32[]{:S(2)}) copy-start(f32[64,32,128]{2,1,0:T(8,128)S(1)} %reshape.57) | copy-start | bytes 3145732
  191.3 15.7 %collective-permute-start = (bf16[64,32,128]{2,1,0:T(8,128)(2,1)}, bf16[64,32,128]{2,1,0:T(8,128)(2,1)}, u32[]{:S(2)}, u32[]{:S(2)}) collective-permute-start(bf16[64,32,128]{2,1,0:T(8,128)(2,1)} %convert_element_type.24), channel_id=1, source_target_pairs={{0,32},{32,64},{64,96},{96,128},{128,160},{160,192},{192,224},{224... | collective-permute-start | bytes 1572872 | tf_op jit(solution)/shard_map/ppermute | solution.py:18
  194.4 17.5 %collective-permute-start.1 = (bf16[64,32,128]{2,1,0:T(8,128)(2,1)}, bf16[64,32,128]{2,1,0:T(8,128)(2,1)}, u32[]{:S(2)}, u32[]{:S(2)}) collective-permute-start(bf16[64,32,128]{2,1,0:T(8,128)(2,1)} %convert_element_type.24), channel_id=1, source_target_pairs={{32,0},{64,32},{96,64},{128,96},{160,128},{192,160},{224,192},{256... | collective-permute-start | bytes 1572872 | tf_op jit(solution)/shard_map/ppermute | solution.py:18
  214.5 13.7 %collective-permute-start.2 = (bf16[64,32,128]{2,1,0:T(8,128)(2,1)S(1)}, bf16[64,32,128]{2,1,0:T(8,128)(2,1)}, u32[]{:S(2)}, u32[]{:S(2)}) collective-permute-start(bf16[64,32,128]{2,1,0:T(8,128)(2,1)S(1)} %convolution_convert_fusion.2), channel_id=1, source_target_pairs={{0,2},{1,3},{2,4},{3,5},{4,6},{5,7},{6,8},{7,9},{8,10},{9,11},{10,... | collective-permute-start | bytes 1572872 | tf_op jit(solution)/shard_map/ppermute | solution.py:18
  216.6 12.7 %collective-permute-start.3 = (bf16[64,32,128]{2,1,0:T(8,128)(2,1)S(1)}, bf16[64,32,128]{2,1,0:T(8,128)(2,1)}, u32[]{:S(2)}, u32[]{:S(2)}) collective-permute-start(bf16[64,32,128]{2,1,0:T(8,128)(2,1)S(1)} %convolution_convert_fusion.2), channel_id=1, source_target_pairs={{0,1},{1,2},{2,3},{3,4},{4,5},{5,6},{6,7},{7,8},{8,9},{9,10},{10,1... | collective-permute-start | bytes 1572872 | tf_op jit(solution)/shard_map/ppermute | solution.py:18
  218.7 11.8 %collective-permute-start.4 = (bf16[64,32,128]{2,1,0:T(8,128)(2,1)S(1)}, bf16[64,32,128]{2,1,0:T(8,128)(2,1)}, u32[]{:S(2)}, u32[]{:S(2)}) collective-permute-start(bf16[64,32,128]{2,1,0:T(8,128)(2,1)S(1)} %convolution_convert_fusion.2), channel_id=1, source_target_pairs={{1,0},{2,1},{3,2},{4,3},{5,4},{6,5},{7,6},{8,7},{9,8},{10,9},{11,1... | collective-permute-start | bytes 1572872 | tf_op jit(solution)/shard_map/ppermute | solution.py:18
  220.0 21.6 %collective-permute-start.5 = (bf16[64,32,128]{2,1,0:T(8,128)(2,1)S(1)}, bf16[64,32,128]{2,1,0:T(8,128)(2,1)S(1)}, u32[]{:S(2)}, u32[]{:S(2)}) collective-permute-start(bf16[64,32,128]{2,1,0:T(8,128)(2,1)S(1)} %convolution_convert_fusion.2), channel_id=1, source_target_pairs={{2,0},{3,1},{4,2},{5,3},{6,4},{7,5},{8,6},{9,7},{10,8},{11,9},{12,... | collective-permute-start | bytes 1572872 | tf_op jit(solution)/shard_map/ppermute | solution.py:18

commit v2 on v1

--- a/solution.py
+++ b/solution.py
@@ -36,13 +36,16 @@
     owner = entries // blocks_local
     block_id = entries % blocks_local
     select = owner[None, :] == jnp.arange(owners_count)[:, None]
-    packed = jnp.dot(select.astype(jnp.bfloat16), partials, preferred_element_type=jnp.float32)
+    rows = partials.reshape(partials.shape[0], CELLS // 128, 128)
+    packed = jnp.einsum("or,rkc->okc", select.astype(jnp.bfloat16), rows, preferred_element_type=jnp.float32)
     packed = packed.astype(jnp.bfloat16)
-    packed_ids = jnp.max(jnp.where(select, block_id[None, :], 0), axis=1).reshape(owners_count, 1)
     arrived = lax.all_to_all(packed, "zs", split_axis=0, concat_axis=0, tiled=True)
-    arrived_ids = lax.all_to_all(packed_ids, "zs", split_axis=0, concat_axis=0, tiled=True)
-    placing = (arrived_ids[:, 0][None, :] == jnp.arange(blocks_local)[:, None]).astype(jnp.bfloat16)
-    assembled = jnp.dot(placing, arrived, preferred_element_type=jnp.float32)
+    listed = lax.all_gather(entries, "zs")
+    mine = (listed // blocks_local) == lax.axis_index("zs")
+    arrived_ids = jnp.max(jnp.where(mine, listed % blocks_local, 0), axis=1)
+    placing = (arrived_ids[None, :] == jnp.arange(blocks_local)[:, None]).astype(jnp.bfloat16)
+    assembled = jnp.einsum("bs,skc->bkc", placing, arrived, preferred_element_type=jnp.float32)
+    assembled = lax.optimization_barrier(assembled)
     assembled = assembled.reshape(2, YBLOCKS, BLK, BLK, BLK).transpose(0, 2, 4, 1, 3)
     gradient = assembled.reshape(CX, CZ, NY)
     norms = jnp.sqrt(jnp.sum(taps * taps, axis=1, keepdims=True))

time: 245 us -> 206 us (0.84)
  the two profiles are of different devices: /device:TPU:24 before, /device:TPU:120 now
where the time goes in v2:
time: 206 us; the launch traced here: 205 us
  blocking collectives  114 us (55%)
  starting transfers between devices  32.2 us (16%)
  waiting for transfers between devices  29.5 us (14%)
  local copies, waits for them, and re-layouts  19 us (9%)
  matrix products  5.93 us (3%)
  other arithmetic  3.63 us (2%)
    all_gather x1, blocking collectives, body(): listed = lax.all_gather(entries, 'zs')  114 us
    ppermute x6, waiting for transfers between devices, shifted(): return lax.ppermute(x, axis, pairs)  29.5 us
    ppermute x6, starting transfers between devices, shifted(): return lax.ppermute(x, axis, pairs)  17.6 us
    all_to_all x1, starting transfers between devices, body(): lax.all_to_all(packed, 'zs', split_axis=0, concat_axis=0, tiled=True)  14.6 us
    transpose x1, local copies, waits for them, and re-layouts, body(): assembled.reshape(2, YBLOCKS, BLK, BLK, BLK).transpose(0, 2, 4, 1, 3)  5.24 us
    unnamed x17, local copies, waits for them, and re-layouts  4.37 us
  transfers between devices with their start and end apart: 7, of which 5 were waited for; matrix products, arithmetic and copies ran while one was open for 2% of the time, Pallas kernels for 0%

profile of v2, /device:TPU:120, one launch (start us, length us, event | category | flops | bytes accessed | tf_op | source)
XLA Modules:
  0.0 205.5 jit_solution(18202311552593888704)
XLA Ops:
  0.6 0.0 copy-start
  0.6 0.8 fusion.25
  1.5 0.8 copy-done
  2.2 0.7 fusion.5
  2.9 2.1 %copy.10 = bf16[32,256,128]{2,1,0:T(8,128)(2,1)} copy(bf16[32,256,128]{2,0,1:T(8,128)(2,1)S(1)} %fusion.5) | data formatting | bytes 4194304 | tf_op jit(solution)/shard_map/convert_element_type | solution.py:41
  5.0 14.6 %all-to-all-start = ((bf16[32,256,128]{2,1,0:T(8,128)(2,1)}), bf16[32,256,128]{2,1,0:T(8,128)(2,1)}, u32[]{:S(2)}, u32[]{:S(2)}) async-start(bf16[32,256,128]{2,1,0:T(8,128)(2,1)} %copy.10), calls=%async_computation | async-start | bytes 4194304 | tf_op jit(solution)/shard_map/all_to_all | solution.py:42
  19.7 0.0 copy-done.2
  19.7 0.1 multiply_reduce_fusion
  19.8 0.1 divide_convert_fusion
  20.0 0.0 copy-done.3
  20.0 114.3 %all-gather = s32[32,1,32]{2,1,0:T(1,128)S(1)} all-gather(s32[1,1,32]{2,1,0:T(1,128)S(1)} %bitcast.55), channel_id=1, replica_groups=mesh['xb'=16,'zs'=32] {'zs'}, dimensions={0}, use_global_device_ids=true | all-gather | bytes 4224 | tf_op jit(solution)/shard_map/all_gather | solution.py:43
  134.3 0.1 fusion.16
  134.4 0.0 all-to-all-done
  134.4 2.8 %fusion.3 = f32[8,256,128]{2,0,1:T(8,128)S(1)} fusion(bf16[32,256,128]{2,1,0:T(8,128)(2,1)} %all-to-all-done, s32[32]{0:T(128)S(1)} %fusion.16), kind=kOutput, calls=%fused_computation.4 | convolution fusion | flops 16777472 | bytes 3145856 | tf_op jit(solution)/shard_map/bs,skc->bkc/dot_general | solution.py:47
  137.2 0.2 copy.12
  137.4 2.4 %reshape.37 = f32[2,4,32,32,32]{4,3,2,1,0:T(8,128)} reshape(f32[8,256,128]{2,1,0:T(8,128)S(1)} %copy.12) | data formatting | bytes 2097152 | tf_op jit(solution)/shard_map/reshape | solution.py:49
  139.9 5.2 %copy.13 = f32[2,32,32,4,32]{4,3,2,1,0:T(4,128)} copy(f32[2,32,32,4,32]{2,4,1,3,0:T(8,128)} %bitcast.48) | data formatting | bytes 2097152 | tf_op jit(solution)/shard_map/transpose | solution.py:49
  145.1 3.7 %reshape.38 = f32[64,32,128]{2,1,0:T(8,128)S(1)} reshape(f32[2,32,32,4,32]{4,3,2,1,0:T(4,128)} %copy.13) | data formatting | bytes 2097152 | tf_op jit(solution)/shard_map/reshape | solution.py:50
  148.8 0.0 copy-start.1
  148.8 1.0 convert_element_type.24
  149.8 3.0 %collective-permute-start = (bf16[64,32,128]{2,1,0:T(8,128)(2,1)}, bf16[64,32,128]{2,1,0:T(8,128)(2,1)}, u32[]{:S(2)}, u32[]{:S(2)}) collective-permute-start(bf16[64,32,128]{2,1,0:T(8,128)(2,1)} %convert_element_type.24), channel_id=1, source_target_pairs={{0,32},{32,64},{64,96},{96,128},{128,160},{160,192},{192,224},{224... | collective-permute-start | bytes 1572872 | tf_op jit(solution)/shard_map/ppermute | solution.py:18
  152.8 2.8 %collective-permute-start.1 = (bf16[64,32,128]{2,1,0:T(8,128)(2,1)}, bf16[64,32,128]{2,1,0:T(8,128)(2,1)}, u32[]{:S(2)}, u32[]{:S(2)}) collective-permute-start(bf16[64,32,128]{2,1,0:T(8,128)(2,1)} %convert_element_type.24), channel_id=1, source_target_pairs={{32,0},{64,32},{96,64},{128,96},{160,128},{192,160},{224,192},{256... | collective-permute-start | bytes 1572872 | tf_op jit(solution)/shard_map/ppermute | solution.py:18
  155.7 0.2 reshape.39
  155.9 0.1 pad_slice_fusion.1
  156.0 0.1 copy.18
  156.0 0.3 reshape.42
  156.3 9.8 %collective-permute-done = bf16[64,32,128]{2,1,0:T(8,128)(2,1)} collective-permute-done((bf16[64,32,128]{2,1,0:T(8,128)(2,1)}, bf16[64,32,128]{2,1,0:T(8,128)(2,1)}, u32[]{:S(2)}, u32[]{:S(2)}) %collective-permute-start) | collective-permute-done | bytes 524320 | tf_op jit(solution)/shard_map/ppermute | solution.py:18
  166.1 4.9 %collective-permute-done.1 = bf16[64,32,128]{2,1,0:T(8,128)(2,1)} collective-permute-done((bf16[64,32,128]{2,1,0:T(8,128)(2,1)}, bf16[64,32,128]{2,1,0:T(8,128)(2,1)}, u32[]{:S(2)}, u32[]{:S(2)}) %collective-permute-start.1) | collective-permute-done | bytes 524320 | tf_op jit(solution)/shard_map/ppermute | solution.py:18
  171.0 1.5 pad_maximum_fusion
  172.6 0.6 fusion.10
  173.2 0.1 copy.17
  173.3 0.3 convolution_convert_fusion.1
  173.6 4.3 %collective-permute-start.2 = (bf16[64,32,128]{2,1,0:T(8,128)(2,1)S(1)}, bf16[64,32,128]{2,1,0:T(8,128)(2,1)}, u32[]{:S(2)}, u32[]{:S(2)}) collective-permute-start(bf16[64,32,128]{2,1,0:T(8,128)(2,1)S(1)} %convolution_convert_fusion.1), channel_id=1, source_target_pairs={{0,2},{1,3},{2,4},{3,5},{4,6},{5,7},{6,8},{7,9},{8,10},{9,11},{10,... | collective-permute-start | bytes 1572872 | tf_op jit(solution)/shard_map/ppermute | solution.py:18
  177.9 1.9 collective-permute-start.3
  179.8 3.6 %collective-permute-start.4 = (bf16[64,32,128]{2,1,0:T(8,128)(2,1)S(1)}, bf16[64,32,128]{2,1,0:T(8,128)(2,1)}, u32[]{:S(2)}, u32[]{:S(2)}) collective-permute-start(bf16[64,32,128]{2,1,0:T(8,128)(2,1)S(1)} %convolution_convert_fusion.1), channel_id=1, source_target_pairs={{1,0},{2,1},{3,2},{4,3},{5,4},{6,5},{7,6},{8,7},{9,8},{10,9},{11,1... | collective-permute-start | bytes 1572872 | tf_op jit(solution)/shard_map/ppermute | solution.py:18
  183.5 1.9 collective-permute-start.5
  185.4 0.1 tile.32
  185.5 0.1 reshape.43
  185.7 4.8 %collective-permute-done.2 = bf16[64,32,128]{2,1,0:T(8,128)(2,1)} collective-permute-done((bf16[64,32,128]{2,1,0:T(8,128)(2,1)S(1)}, bf16[64,32,128]{2,1,0:T(8,128)(2,1)}, u32[]{:S(2)}, u32[]{:S(2)}) %collective-permute-start.2) | collective-permute-done | bytes 524320 | tf_op jit(solution)/shard_map/ppermute | solution.py:18
  190.5 1.1 constant_dynamic-update-slice_fusion.4
  191.5 2.7 %collective-permute-done.3 = bf16[64,32,128]{2,1,0:T(8,128)(2,1)} collective-permute-done((bf16[64,32,128]{2,1,0:T(8,128)(2,1)S(1)}, bf16[64,32,128]{2,1,0:T(8,128)(2,1)}, u32[]{:S(2)}, u32[]{:S(2)}) %collective-permute-start.3) | collective-permute-done | bytes 524320 | tf_op jit(solution)/shard_map/ppermute | solution.py:18
  194.2 1.1 constant_dynamic-update-slice_fusion.3
  195.3 0.1 constant_dynamic-update-slice_fusion.2
  195.4 0.0 collective-permute-done.4
  195.4 1.1 constant_dynamic-update-slice_fusion.1
  196.5 7.4 %collective-permute-done.5 = bf16[64,32,128]{2,1,0:T(8,128)(2,1)S(1)} collective-permute-done((bf16[64,32,128]{2,1,0:T(8,128)(2,1)S(1)}, bf16[64,32,128]{2,1,0:T(8,128)(2,1)S(1)}, u32[]{:S(2)}, u32[]{:S(2)}) %collective-permute-start.5) | collective-permute-done | bytes 524320 | tf_op jit(solution)/shard_map/ppermute | solution.py:18
  203.9 0.1 constant_dynamic-update-slice_fusion
  204.0 1.5 convolution_bitcast_fusion
  (14 shorter events, 0.1 us)
Async XLA Ops:
  0.6 1.6 copy-start
  5.0 14.7 %copy-start.2 = (f32[3,129]{1,0:T(4,128)S(1)}, f32[3,129]{1,0:T(4,128)}, u32[]{:S(2)}) copy-start(f32[3,129]{1,0:T(4,128)} %param.5) | copy-start | bytes 4648
  5.0 14.9 %copy-start.3 = (s32[1,32]{1,0:T(1,128)S(1)}, s32[1,32]{1,0:T(1,128)}, u32[]{:S(2)}) copy-start(s32[1,32]{1,0:T(1,128)} %param.4) | copy-start | bytes 388
  5.0 129.4 %all-to-all-start = ((bf16[32,256,128]{2,1,0:T(8,128)(2,1)}), bf16[32,256,128]{2,1,0:T(8,128)(2,1)}, u32[]{:S(2)}, u32[]{:S(2)}) async-start(bf16[32,256,128]{2,1,0:T(8,128)(2,1)} %copy.10), calls=%async_computation | async-start | bytes 4194304 | tf_op jit(solution)/shard_map/all_to_all | solution.py:42
  148.8 23.7 %copy-start.1 = (f32[64,32,128]{2,1,0:T(8,128)}, f32[64,32,128]{2,1,0:T(8,128)S(1)}, u32[]{:S(2)}) copy-start(f32[64,32,128]{2,1,0:T(8,128)S(1)} %reshape.38) | copy-start | bytes 3145732
  149.8 16.3 %collective-permute-start = (bf16[64,32,128]{2,1,0:T(8,128)(2,1)}, bf16[64,32,128]{2,1,0:T(8,128)(2,1)}, u32[]{:S(2)}, u32[]{:S(2)}) collective-permute-start(bf16[64,32,128]{2,1,0:T(8,128)(2,1)} %convert_element_type.24), channel_id=1, source_target_pairs={{0,32},{32,64},{64,96},{96,128},{128,160},{160,192},{192,224},{224... | collective-permute-start | bytes 1572872 | tf_op jit(solution)/shard_map/ppermute | solution.py:18
  152.8 18.2 %collective-permute-start.1 = (bf16[64,32,128]{2,1,0:T(8,128)(2,1)}, bf16[64,32,128]{2,1,0:T(8,128)(2,1)}, u32[]{:S(2)}, u32[]{:S(2)}) collective-permute-start(bf16[64,32,128]{2,1,0:T(8,128)(2,1)} %convert_element_type.24), channel_id=1, source_target_pairs={{32,0},{64,32},{96,64},{128,96},{160,128},{192,160},{224,192},{256... | collective-permute-start | bytes 1572872 | tf_op jit(solution)/shard_map/ppermute | solution.py:18
  173.6 16.9 %collective-permute-start.2 = (bf16[64,32,128]{2,1,0:T(8,128)(2,1)S(1)}, bf16[64,32,128]{2,1,0:T(8,128)(2,1)}, u32[]{:S(2)}, u32[]{:S(2)}) collective-permute-start(bf16[64,32,128]{2,1,0:T(8,128)(2,1)S(1)} %convolution_convert_fusion.1), channel_id=1, source_target_pairs={{0,2},{1,3},{2,4},{3,5},{4,6},{5,7},{6,8},{7,9},{8,10},{9,11},{10,... | collective-permute-start | bytes 1572872 | tf_op jit(solution)/shard_map/ppermute | solution.py:18
  177.9 16.3 %collective-permute-start.3 = (bf16[64,32,128]{2,1,0:T(8,128)(2,1)S(1)}, bf16[64,32,128]{2,1,0:T(8,128)(2,1)}, u32[]{:S(2)}, u32[]{:S(2)}) collective-permute-start(bf16[64,32,128]{2,1,0:T(8,128)(2,1)S(1)} %convolution_convert_fusion.1), channel_id=1, source_target_pairs={{0,1},{1,2},{2,3},{3,4},{4,5},{5,6},{6,7},{7,8},{8,9},{9,10},{10,1... | collective-permute-start | bytes 1572872 | tf_op jit(solution)/shard_map/ppermute | solution.py:18
  179.8 15.6 %collective-permute-start.4 = (bf16[64,32,128]{2,1,0:T(8,128)(2,1)S(1)}, bf16[64,32,128]{2,1,0:T(8,128)(2,1)}, u32[]{:S(2)}, u32[]{:S(2)}) collective-permute-start(bf16[64,32,128]{2,1,0:T(8,128)(2,1)S(1)} %convolution_convert_fusion.1), channel_id=1, source_target_pairs={{1,0},{2,1},{3,2},{4,3},{5,4},{6,5},{7,6},{8,7},{9,8},{10,9},{11,1... | collective-permute-start | bytes 1572872 | tf_op jit(solution)/shard_map/ppermute | solution.py:18
  183.5 20.4 %collective-permute-start.5 = (bf16[64,32,128]{2,1,0:T(8,128)(2,1)S(1)}, bf16[64,32,128]{2,1,0:T(8,128)(2,1)S(1)}, u32[]{:S(2)}, u32[]{:S(2)}) collective-permute-start(bf16[64,32,128]{2,1,0:T(8,128)(2,1)S(1)} %convolution_convert_fusion.1), channel_id=1, source_target_pairs={{2,0},{3,1},{4,2},{5,3},{6,4},{7,5},{8,6},{9,7},{10,8},{11,9},{12,... | collective-permute-start | bytes 1572872 | tf_op jit(solution)/shard_map/ppermute | solution.py:18

commit v3 on v2

--- a/solution.py
+++ b/solution.py
@@ -12,10 +12,11 @@
 NY = 128
 
 
-def shifted(x, axis, step):
+def shifted(x, axis, step, dim, pieces=2):
     count = lax.axis_size(axis)
     pairs = [(i, i + step) for i in range(count) if 0 <= i + step < count]
-    return lax.ppermute(x, axis, pairs)
+    parts = jnp.split(x, pieces, axis=dim)
+    return jnp.concatenate([lax.ppermute(p, axis, pairs) for p in parts], axis=dim)
 
 
 def band_matrix(kern_row, rows, cols, offset):
@@ -52,7 +53,7 @@
     kernel = (taps / norms).astype(jnp.bfloat16)
     field = gradient.astype(jnp.bfloat16)
     padded = jnp.concatenate(
-        [shifted(field, "xb", 1), field, shifted(field, "xb", -1)], axis=0
+        [shifted(field, "xb", 1, 1), field, shifted(field, "xb", -1, 1)], axis=0
     )
     x_matrix = band_matrix(kernel[0], CX, 3 * CX, 0)
     along_x = jnp.dot(x_matrix, padded.reshape(3 * CX, CZ * NY), preferred_element_type=jnp.float32)
@@ -62,8 +63,8 @@
         "ab,xzb->xza", y_matrix, along_x, preferred_element_type=jnp.float32
     ).astype(jnp.bfloat16)
     reach_slabs = REACH // CZ
-    halo_lo = [shifted(along_y, "zs", s) for s in range(reach_slabs, 0, -1)]
-    halo_hi = [shifted(along_y, "zs", -s) for s in range(1, reach_slabs + 1)]
+    halo_lo = [shifted(along_y, "zs", s, 0) for s in range(reach_slabs, 0, -1)]
+    halo_hi = [shifted(along_y, "zs", -s, 0) for s in range(1, reach_slabs + 1)]
     extended = jnp.concatenate(halo_lo + [along_y] + halo_hi, axis=1)
     z_matrix = band_matrix(kernel[2], CZ, CZ + 2 * REACH, 0)
     smoothed = jnp.einsum(

time: 206 us -> 219 us (1.063)
  the two profiles are of different devices: /device:TPU:120 before, /device:TPU:26 now
where the time goes in v3:
time: 219 us; the launch traced here: 218 us
  blocking collectives  114 us (52%)
  starting transfers between devices  49.9 us (23%)
  local copies, waits for them, and re-layouts  24.7 us (11%)
  waiting for transfers between devices  13.8 us (6%)
  other arithmetic  9.62 us (4%)
  matrix products  5.71 us (3%)
    all_gather x1, blocking collectives, body(): listed = lax.all_gather(entries, 'zs')  114 us
    ppermute x12, starting transfers between devices, shifted(): lax.ppermute(p, axis, pairs)  34.1 us
    all_to_all x1, starting transfers between devices, body(): lax.all_to_all(packed, 'zs', split_axis=0, concat_axis=0, tiled=True)  15.7 us
    ppermute x12, waiting for transfers between devices, shifted(): lax.ppermute(p, axis, pairs)  13.8 us
    convert_element_type x2, local copies, waits for them, and re-layouts, body(): field = gradient.astype(jnp.bfloat16)  7.75 us
    transpose x1, local copies, waits for them, and re-layouts, body(): assembled.reshape(2, YBLOCKS, BLK, BLK, BLK).transpose(0, 2, 4, 1, 3)  5.27 us
  transfers between devices with their start and end apart: 13, of which 2 were waited for; matrix products, arithmetic and copies ran while one was open for 7% of the time, Pallas kernels for 0%

profile of v3, /device:TPU:26, one launch (start us, length us, event | category | flops | bytes accessed | tf_op | source)
XLA Modules:
  0.0 218.4 jit_solution(17899155534024138819)
XLA Ops:
  0.6 0.8 fusion.28
  1.5 0.8 copy-done
  2.2 0.7 fusion.5
  2.9 2.1 copy.11
  5.1 15.7 %all-to-all-start = ((bf16[32,256,128]{2,1,0:T(8,128)(2,1)}), bf16[32,256,128]{2,1,0:T(8,128)(2,1)}, u32[]{:S(2)}, u32[]{:S(2)}) async-start(bf16[32,256,128]{2,1,0:T(8,128)(2,1)} %copy.11), calls=%async_computation | async-start | bytes 4194304 | tf_op jit(solution)/shard_map/all_to_all | solution.py:43
  20.8 0.1 multiply_reduce_fusion
  20.9 0.1 divide_convert_fusion
  21.1 0.2 reshape.42
  21.3 0.1 pad_slice_fusion.1
  21.5 0.3 reshape.44
  21.8 113.6 %all-gather = s32[32,1,32]{2,1,0:T(1,128)S(1)} all-gather(s32[1,1,32]{2,1,0:T(1,128)S(1)} %bitcast.57), channel_id=1, replica_groups=mesh['xb'=16,'zs'=32] {'zs'}, dimensions={0}, use_global_device_ids=true | all-gather | bytes 4224 | tf_op jit(solution)/shard_map/all_gather | solution.py:44
  135.5 0.1 fusion.19
  135.6 2.8 %fusion.3 = f32[8,256,128]{2,0,1:T(8,128)S(1)} fusion(bf16[32,256,128]{2,1,0:T(8,128)(2,1)} %all-to-all-done, s32[32]{0:T(128)S(1)} %fusion.19), kind=kOutput, calls=%fused_computation.4 | convolution fusion | flops 16777472 | bytes 3145856 | tf_op jit(solution)/shard_map/bs,skc->bkc/dot_general | solution.py:48
  138.4 0.2 copy.13
  138.6 2.4 %reshape.40 = f32[2,4,32,32,32]{4,3,2,1,0:T(8,128)} reshape(f32[8,256,128]{2,1,0:T(8,128)S(1)} %copy.13) | data formatting | bytes 2097152 | tf_op jit(solution)/shard_map/reshape | solution.py:50
  141.1 5.3 %copy.14 = f32[2,32,32,4,32]{4,3,2,1,0:T(4,128)} copy(f32[2,32,32,4,32]{2,4,1,3,0:T(8,128)} %bitcast.49) | data formatting | bytes 2097152 | tf_op jit(solution)/shard_map/transpose | solution.py:50
  146.3 3.7 %reshape.41 = f32[64,32,128]{2,1,0:T(8,128)S(1)} reshape(f32[2,32,32,4,32]{4,3,2,1,0:T(4,128)} %copy.14) | data formatting | bytes 2097152 | tf_op jit(solution)/shard_map/reshape | solution.py:51
  150.1 0.1 convert_element_type.30
  150.2 0.8 fusion.31
  151.0 2.6 %collective-permute-start.2 = (bf16[64,16,128]{2,1,0:T(8,128)(2,1)}, bf16[64,16,128]{2,1,0:T(8,128)(2,1)}, u32[]{:S(2)}, u32[]{:S(2)}) collective-permute-start(bf16[64,16,128]{2,1,0:T(8,128)(2,1)} %get-tuple-element.7), channel_id=1, source_target_pairs={{32,0},{64,32},{96,64},{128,96},{160,128},{192,160},{224,192},{256... | collective-permute-start | bytes 786440 | tf_op jit(solution)/shard_map/ppermute | solution.py:19
  153.7 5.3 %collective-permute-start = (bf16[64,16,128]{2,1,0:T(8,128)(2,1)}, bf16[64,16,128]{2,1,0:T(8,128)(2,1)}, u32[]{:S(2)}, u32[]{:S(2)}) collective-permute-start(bf16[64,16,128]{2,1,0:T(8,128)(2,1)} %get-tuple-element.7), channel_id=1, source_target_pairs={{0,32},{32,64},{64,96},{96,128},{128,160},{160,192},{192,224},{224... | collective-permute-start | bytes 786440 | tf_op jit(solution)/shard_map/ppermute | solution.py:19
  159.0 1.9 collective-permute-start.3
  160.9 6.0 %collective-permute-start.1 = (bf16[64,16,128]{2,1,0:T(8,128)(2,1)S(1)}, bf16[64,16,128]{2,1,0:T(8,128)(2,1)}, u32[]{:S(2)}, u32[]{:S(2)}) collective-permute-start(bf16[64,16,128]{2,1,0:T(8,128)(2,1)S(1)} %get-tuple-element.8), channel_id=1, source_target_pairs={{0,32},{32,64},{64,96},{96,128},{128,160},{160,192},{192,224},{224... | collective-permute-start | bytes 786440 | tf_op jit(solution)/shard_map/ppermute | solution.py:19
  166.9 4.0 %bitcast_convert_fusion = bf16[2,32,32,4,32]{2,4,1,3,0:T(8,128)(2,1)} fusion(f32[2,4,32,32,32]{4,3,2,1,0:T(8,128)} %reshape.40), kind=kLoop, calls=%fused_computation.62 | loop fusion | flops 262144 | bytes 1572864 | tf_op jit(solution)/shard_map/convert_element_type | solution.py:54
  170.9 4.2 %copy.15 = bf16[2,32,32,4,32]{4,3,2,1,0:T(4,128)(2,1)} copy(bf16[2,32,32,4,32]{2,4,1,3,0:T(8,128)(2,1)} %bitcast_convert_fusion) | data formatting | bytes 1048576 | tf_op jit(solution)/shard_map/convert_element_type | solution.py:54
  175.2 3.5 %convert_element_type.32 = bf16[64,4096]{1,0:T(8,128)(2,1)S(1)} reshape(bf16[2,32,32,4,32]{4,3,2,1,0:T(4,128)(2,1)} %copy.15) | data formatting | bytes 1048576 | tf_op jit(solution)/shard_map/convert_element_type | solution.py:54
  178.7 1.1 pad_maximum_fusion.1
  179.8 1.1 pad_maximum_fusion
  180.9 0.4 copy_bitcast_fusion
  181.3 0.4 fusion.13
  181.7 0.1 copy.20
  181.8 0.3 convolution_convert_fusion.1
  182.2 3.9 %collective-permute-start.4 = (bf16[32,32,128]{2,1,0:T(8,128)(2,1)S(1)}, bf16[32,32,128]{2,1,0:T(8,128)(2,1)}, u32[]{:S(2)}, u32[]{:S(2)}) collective-permute-start(bf16[32,32,128]{2,1,0:T(8,128)(2,1)S(1)} %get-tuple-element.5), channel_id=1, source_target_pairs={{0,2},{1,3},{2,4},{3,5},{4,6},{5,7},{6,8},{7,9},{8,10},{9,11},{10,... | collective-permute-start | bytes 786440 | tf_op jit(solution)/shard_map/ppermute | solution.py:19
  186.1 3.1 %collective-permute-start.5 = (bf16[32,32,128]{2,1,0:T(8,128)(2,1)S(1)}, bf16[32,32,128]{2,1,0:T(8,128)(2,1)}, u32[]{:S(2)}, u32[]{:S(2)}) collective-permute-start(bf16[32,32,128]{2,1,0:T(8,128)(2,1)S(1)} %get-tuple-element.6), channel_id=1, source_target_pairs={{0,2},{1,3},{2,4},{3,5},{4,6},{5,7},{6,8},{7,9},{8,10},{9,11},{10,... | collective-permute-start | bytes 786440 | tf_op jit(solution)/shard_map/ppermute | solution.py:19
  189.2 1.3 collective-permute-start.6
  190.5 4.7 %collective-permute-start.7 = (bf16[32,32,128]{2,1,0:T(8,128)(2,1)S(1)}, bf16[32,32,128]{2,1,0:T(8,128)(2,1)}, u32[]{:S(2)}, u32[]{:S(2)}) collective-permute-start(bf16[32,32,128]{2,1,0:T(8,128)(2,1)S(1)} %get-tuple-element.6), channel_id=1, source_target_pairs={{0,1},{1,2},{2,3},{3,4},{4,5},{5,6},{6,7},{7,8},{8,9},{9,10},{10,1... | collective-permute-start | bytes 786440 | tf_op jit(solution)/shard_map/ppermute | solution.py:19
  195.3 0.1 tile.32
  195.4 0.1 reshape.45
  195.5 1.3 collective-permute-start.10
  196.8 1.3 collective-permute-start.8
  198.1 1.3 collective-permute-start.9
  199.4 1.1 maximum_dynamic-update-slice_fusion.3
  200.5 1.3 collective-permute-start.11
  201.8 1.0 maximum_dynamic-update-slice_fusion.2
  202.8 0.1 constant_dynamic-update-slice_fusion
  203.0 2.6 %collective-permute-done.10 = bf16[32,32,128]{2,1,0:T(8,128)(2,1)S(1)} collective-permute-done((bf16[32,32,128]{2,1,0:T(8,128)(2,1)S(1)}, bf16[32,32,128]{2,1,0:T(8,128)(2,1)S(1)}, u32[]{:S(2)}, u32[]{:S(2)}) %collective-permute-start.10) | collective-permute-done | bytes 262176 | tf_op jit(solution)/shard_map/ppermute | solution.py:19
  205.6 11.2 %collective-permute-done.11 = bf16[32,32,128]{2,1,0:T(8,128)(2,1)S(1)} collective-permute-done((bf16[32,32,128]{2,1,0:T(8,128)(2,1)S(1)}, bf16[32,32,128]{2,1,0:T(8,128)(2,1)S(1)}, u32[]{:S(2)}, u32[]{:S(2)}) %collective-permute-start.11) | collective-permute-done | bytes 262176 | tf_op jit(solution)/shard_map/ppermute | solution.py:19
  216.9 1.5 convolution_bitcast_fusion
  (33 shorter events, 0.4 us)
Async XLA Ops:
  0.6 1.6 copy-start
  5.1 15.8 %copy-start.2 = (f32[3,129]{1,0:T(4,128)S(1)}, f32[3,129]{1,0:T(4,128)}, u32[]{:S(2)}) copy-start(f32[3,129]{1,0:T(4,128)} %param.5) | copy-start | bytes 4648
  5.1 16.8 %copy-start.3 = (s32[1,32]{1,0:T(1,128)S(1)}, s32[1,32]{1,0:T(1,128)}, u32[]{:S(2)}) copy-start(s32[1,32]{1,0:T(1,128)} %param.4) | copy-start | bytes 388
  5.1 130.5 %all-to-all-start = ((bf16[32,256,128]{2,1,0:T(8,128)(2,1)}), bf16[32,256,128]{2,1,0:T(8,128)(2,1)}, u32[]{:S(2)}, u32[]{:S(2)}) async-start(bf16[32,256,128]{2,1,0:T(8,128)(2,1)} %copy.11), calls=%async_computation | async-start | bytes 4194304 | tf_op jit(solution)/shard_map/all_to_all | solution.py:43
  150.0 20.9 %copy-start.1 = (f32[64,32,128]{2,1,0:T(8,128)}, f32[64,32,128]{2,1,0:T(8,128)S(1)}, u32[]{:S(2)}) copy-start(f32[64,32,128]{2,1,0:T(8,128)S(1)} %reshape.41) | copy-start | bytes 3145732
  151.0 27.7 %collective-permute-start.2 = (bf16[64,16,128]{2,1,0:T(8,128)(2,1)}, bf16[64,16,128]{2,1,0:T(8,128)(2,1)}, u32[]{:S(2)}, u32[]{:S(2)}) collective-permute-start(bf16[64,16,128]{2,1,0:T(8,128)(2,1)} %get-tuple-element.7), channel_id=1, source_target_pairs={{32,0},{64,32},{96,64},{128,96},{160,128},{192,160},{224,192},{256... | collective-permute-start | bytes 786440 | tf_op jit(solution)/shard_map/ppermute | solution.py:19
  153.7 26.2 %collective-permute-start = (bf16[64,16,128]{2,1,0:T(8,128)(2,1)}, bf16[64,16,128]{2,1,0:T(8,128)(2,1)}, u32[]{:S(2)}, u32[]{:S(2)}) collective-permute-start(bf16[64,16,128]{2,1,0:T(8,128)(2,1)} %get-tuple-element.7), channel_id=1, source_target_pairs={{0,32},{32,64},{64,96},{96,128},{128,160},{160,192},{192,224},{224... | collective-permute-start | bytes 786440 | tf_op jit(solution)/shard_map/ppermute | solution.py:19
  159.0 19.8 %collective-permute-start.3 = (bf16[64,16,128]{2,1,0:T(8,128)(2,1)S(1)}, bf16[64,16,128]{2,1,0:T(8,128)(2,1)}, u32[]{:S(2)}, u32[]{:S(2)}) collective-permute-start(bf16[64,16,128]{2,1,0:T(8,128)(2,1)S(1)} %get-tuple-element.8), channel_id=1, source_target_pairs={{32,0},{64,32},{96,64},{128,96},{160,128},{192,160},{224,192},{256... | collective-permute-start | bytes 786440 | tf_op jit(solution)/shard_map/ppermute | solution.py:19
  160.9 18.9 %collective-permute-start.1 = (bf16[64,16,128]{2,1,0:T(8,128)(2,1)S(1)}, bf16[64,16,128]{2,1,0:T(8,128)(2,1)}, u32[]{:S(2)}, u32[]{:S(2)}) collective-permute-start(bf16[64,16,128]{2,1,0:T(8,128)(2,1)S(1)} %get-tuple-element.8), channel_id=1, source_target_pairs={{0,32},{32,64},{64,96},{96,128},{128,160},{160,192},{192,224},{224... | collective-permute-start | bytes 786440 | tf_op jit(solution)/shard_map/ppermute | solution.py:19
  182.2 14.6 %collective-permute-start.4 = (bf16[32,32,128]{2,1,0:T(8,128)(2,1)S(1)}, bf16[32,32,128]{2,1,0:T(8,128)(2,1)}, u32[]{:S(2)}, u32[]{:S(2)}) collective-permute-start(bf16[32,32,128]{2,1,0:T(8,128)(2,1)S(1)} %get-tuple-element.5), channel_id=1, source_target_pairs={{0,2},{1,3},{2,4},{3,5},{4,6},{5,7},{6,8},{7,9},{8,10},{9,11},{10,... | collective-permute-start | bytes 786440 | tf_op jit(solution)/shard_map/ppermute | solution.py:19
  186.1 12.0 %collective-permute-start.5 = (bf16[32,32,128]{2,1,0:T(8,128)(2,1)S(1)}, bf16[32,32,128]{2,1,0:T(8,128)(2,1)}, u32[]{:S(2)}, u32[]{:S(2)}) collective-permute-start(bf16[32,32,128]{2,1,0:T(8,128)(2,1)S(1)} %get-tuple-element.6), channel_id=1, source_target_pairs={{0,2},{1,3},{2,4},{3,5},{4,6},{5,7},{6,8},{7,9},{8,10},{9,11},{10,... | collective-permute-start | bytes 786440 | tf_op jit(solution)/shard_map/ppermute | solution.py:19
  189.2 11.3 %collective-permute-start.6 = (bf16[32,32,128]{2,1,0:T(8,128)(2,1)S(1)}, bf16[32,32,128]{2,1,0:T(8,128)(2,1)S(1)}, u32[]{:S(2)}, u32[]{:S(2)}) collective-permute-start(bf16[32,32,128]{2,1,0:T(8,128)(2,1)S(1)} %get-tuple-element.5), channel_id=1, source_target_pairs={{0,1},{1,2},{2,3},{3,4},{4,5},{5,6},{6,7},{7,8},{8,9},{9,10},{10,1... | collective-permute-start | bytes 786440 | tf_op jit(solution)/shard_map/ppermute | solution.py:19
  190.5 11.3 %collective-permute-start.7 = (bf16[32,32,128]{2,1,0:T(8,128)(2,1)S(1)}, bf16[32,32,128]{2,1,0:T(8,128)(2,1)}, u32[]{:S(2)}, u32[]{:S(2)}) collective-permute-start(bf16[32,32,128]{2,1,0:T(8,128)(2,1)S(1)} %get-tuple-element.6), channel_id=1, source_target_pairs={{0,1},{1,2},{2,3},{3,4},{4,5},{5,6},{6,7},{7,8},{8,9},{9,10},{10,1... | collective-permute-start | bytes 786440 | tf_op jit(solution)/shard_map/ppermute | solution.py:19
  195.5 10.1 %collective-permute-start.10 = (bf16[32,32,128]{2,1,0:T(8,128)(2,1)S(1)}, bf16[32,32,128]{2,1,0:T(8,128)(2,1)S(1)}, u32[]{:S(2)}, u32[]{:S(2)}) collective-permute-start(bf16[32,32,128]{2,1,0:T(8,128)(2,1)S(1)} %get-tuple-element.5), channel_id=1, source_target_pairs={{2,0},{3,1},{4,2},{5,3},{6,4},{7,5},{8,6},{9,7},{10,8},{11,9},{12,... | collective-permute-start | bytes 786440 | tf_op jit(solution)/shard_map/ppermute | solution.py:19
  196.8 6.1 %collective-permute-start.8 = (bf16[32,32,128]{2,1,0:T(8,128)(2,1)S(1)}, bf16[32,32,128]{2,1,0:T(8,128)(2,1)S(1)}, u32[]{:S(2)}, u32[]{:S(2)}) collective-permute-start(bf16[32,32,128]{2,1,0:T(8,128)(2,1)S(1)} %get-tuple-element.5), channel_id=1, source_target_pairs={{1,0},{2,1},{3,2},{4,3},{5,4},{6,5},{7,6},{8,7},{9,8},{10,9},{11,1... | collective-permute-start | bytes 786440 | tf_op jit(solution)/shard_map/ppermute | solution.py:19
  198.1 4.8 %collective-permute-start.9 = (bf16[32,32,128]{2,1,0:T(8,128)(2,1)S(1)}, bf16[32,32,128]{2,1,0:T(8,128)(2,1)S(1)}, u32[]{:S(2)}, u32[]{:S(2)}) collective-permute-start(bf16[32,32,128]{2,1,0:T(8,128)(2,1)S(1)} %get-tuple-element.6), channel_id=1, source_target_pairs={{1,0},{2,1},{3,2},{4,3},{5,4},{6,5},{7,6},{8,7},{9,8},{10,9},{11,1... | collective-permute-start | bytes 786440 | tf_op jit(solution)/shard_map/ppermute | solution.py:19
  200.5 16.3 %collective-permute-start.11 = (bf16[32,32,128]{2,1,0:T(8,128)(2,1)S(1)}, bf16[32,32,128]{2,1,0:T(8,128)(2,1)S(1)}, u32[]{:S(2)}, u32[]{:S(2)}) collective-permute-start(bf16[32,32,128]{2,1,0:T(8,128)(2,1)S(1)} %get-tuple-element.6), channel_id=1, source_target_pairs={{2,0},{3,1},{4,2},{5,3},{6,4},{7,5},{8,6},{9,7},{10,8},{11,9},{12,... | collective-permute-start | bytes 786440 | tf_op jit(solution)/shard_map/ppermute | solution.py:19

commit v4 on v2

--- a/solution.py
+++ b/solution.py
@@ -39,10 +39,12 @@
     rows = partials.reshape(partials.shape[0], CELLS // 128, 128)
     packed = jnp.einsum("or,rkc->okc", select.astype(jnp.bfloat16), rows, preferred_element_type=jnp.float32)
     packed = packed.astype(jnp.bfloat16)
-    arrived = lax.all_to_all(packed, "zs", split_axis=0, concat_axis=0, tiled=True)
-    listed = lax.all_gather(entries, "zs")
-    mine = (listed // blocks_local) == lax.axis_index("zs")
-    arrived_ids = jnp.max(jnp.where(mine, listed % blocks_local, 0), axis=1)
+    packed_ids = jnp.max(jnp.where(select, block_id[None, :], 0), axis=1).astype(jnp.bfloat16)
+    id_rows = jnp.broadcast_to(packed_ids[:, None, None], (owners_count, 16, 128))
+    outgoing = jnp.concatenate([packed, id_rows], axis=1)
+    arrived_all = lax.all_to_all(outgoing, "zs", split_axis=0, concat_axis=0, tiled=True)
+    arrived = arrived_all[:, : CELLS // 128]
+    arrived_ids = arrived_all[:, CELLS // 128, 0].astype(jnp.int32)
     placing = (arrived_ids[None, :] == jnp.arange(blocks_local)[:, None]).astype(jnp.bfloat16)
     assembled = jnp.einsum("bs,skc->bkc", placing, arrived, preferred_element_type=jnp.float32)
     assembled = lax.optimization_barrier(assembled)

time: 206 us -> 196 us (0.951)
  the two profiles are of different devices: /device:TPU:120 before, /device:TPU:24 now
where the time goes in v4:
time: 196 us; the launch traced here: 195 us
  waiting for transfers between devices  135 us (69%)
  starting transfers between devices  28.5 us (15%)
  local copies, waits for them, and re-layouts  20.8 us (11%)
  other arithmetic  5.32 us (3%)
  matrix products  4.34 us (2%)
    all_to_all x1, waiting for transfers between devices, body(): lax.all_to_all(outgoing, 'zs', split_axis=0, concat_axis=0, tiled=True)  104 us
    ppermute x6, waiting for transfers between devices, shifted(): return lax.ppermute(x, axis, pairs)  30.9 us
    all_to_all x1, starting transfers between devices, body(): lax.all_to_all(outgoing, 'zs', split_axis=0, concat_axis=0, tiled=True)  15.7 us
    ppermute x6, starting transfers between devices, shifted(): return lax.ppermute(x, axis, pairs)  12.7 us
    transpose x1, local copies, waits for them, and re-layouts, body(): assembled.reshape(2, YBLOCKS, BLK, BLK, BLK).transpose(0, 2, 4, 1, 3)  5.24 us
    unnamed x15, local copies, waits for them, and re-layouts  4.24 us
  transfers between devices with their start and end apart: 7, of which 5 were waited for; matrix products, arithmetic and copies ran while one was open for 2% of the time, Pallas kernels for 0%

profile of v4, /device:TPU:24, one launch (start us, length us, event | category | flops | bytes accessed | tf_op | source)
XLA Modules:
  0.0 195.1 jit_solution(4116920681809937210)
XLA Ops:
  0.6 0.0 copy-start
  0.6 0.8 fusion.22
  1.5 0.1 select_reduce_fusion
  1.6 0.7 copy-done
  2.2 0.7 fusion.5
  2.9 0.1 broadcast_in_dim.29
  3.0 0.2 pad_maximum_fusion
  3.2 2.2 %copy.12 = bf16[32,272,128]{2,1,0:T(8,128)(2,1)} copy(bf16[32,272,128]{2,0,1:T(8,128)(2,1)S(1)} %pad_maximum_fusion) | data formatting | bytes 4456448 | tf_op jit(solution)/shard_map/concatenate | solution.py:44
  5.5 15.7 %all-to-all-start = ((bf16[32,272,128]{2,1,0:T(8,128)(2,1)}), bf16[32,272,128]{2,1,0:T(8,128)(2,1)}, u32[]{:S(2)}, u32[]{:S(2)}) async-start(bf16[32,272,128]{2,1,0:T(8,128)(2,1)} %copy.12), calls=%async_computation | async-start | bytes 4456448 | tf_op jit(solution)/shard_map/all_to_all | solution.py:45
  21.2 0.1 multiply_reduce_fusion
  21.3 0.1 divide_convert_fusion
  21.5 104.3 %all-to-all-done = bf16[32,272,128]{2,1,0:T(8,128)(2,1)} async-done(((bf16[32,272,128]{2,1,0:T(8,128)(2,1)}), bf16[32,272,128]{2,1,0:T(8,128)(2,1)}, u32[]{:S(2)}, u32[]{:S(2)}) %all-to-all-start) | async-done | bytes 2228256 | tf_op jit(solution)/shard_map/all_to_all | solution.py:45
  125.8 1.7 slice.63
  127.5 1.5 fusion.14
  129.0 1.2 fusion.3
  130.3 0.2 copy.14
  130.5 2.4 %reshape.46 = f32[2,4,32,32,32]{4,3,2,1,0:T(8,128)} reshape(f32[8,256,128]{2,1,0:T(8,128)S(1)} %copy.14) | data formatting | bytes 2097152 | tf_op jit(solution)/shard_map/reshape | solution.py:51
  132.9 5.2 %copy.15 = f32[2,32,32,4,32]{4,3,2,1,0:T(4,128)} copy(f32[2,32,32,4,32]{2,4,1,3,0:T(8,128)} %bitcast.48) | data formatting | bytes 2097152 | tf_op jit(solution)/shard_map/transpose | solution.py:51
  138.1 3.7 %reshape.47 = f32[64,32,128]{2,1,0:T(8,128)S(1)} reshape(f32[2,32,32,4,32]{4,3,2,1,0:T(4,128)} %copy.15) | data formatting | bytes 2097152 | tf_op jit(solution)/shard_map/reshape | solution.py:52
  141.9 0.0 copy-start.1
  141.9 1.0 convert_element_type.44
  142.8 3.0 %collective-permute-start = (bf16[64,32,128]{2,1,0:T(8,128)(2,1)}, bf16[64,32,128]{2,1,0:T(8,128)(2,1)}, u32[]{:S(2)}, u32[]{:S(2)}) collective-permute-start(bf16[64,32,128]{2,1,0:T(8,128)(2,1)} %convert_element_type.44), channel_id=1, source_target_pairs={{0,32},{32,64},{64,96},{96,128},{128,160},{160,192},{192,224},{224... | collective-permute-start | bytes 1572872 | tf_op jit(solution)/shard_map/ppermute | solution.py:18
  145.9 2.8 %collective-permute-start.1 = (bf16[64,32,128]{2,1,0:T(8,128)(2,1)}, bf16[64,32,128]{2,1,0:T(8,128)(2,1)}, u32[]{:S(2)}, u32[]{:S(2)}) collective-permute-start(bf16[64,32,128]{2,1,0:T(8,128)(2,1)} %convert_element_type.44), channel_id=1, source_target_pairs={{32,0},{64,32},{96,64},{128,96},{160,128},{192,160},{224,192},{256... | collective-permute-start | bytes 1572872 | tf_op jit(solution)/shard_map/ppermute | solution.py:18
  148.7 0.2 reshape.48
  148.9 0.1 pad_slice_fusion.1
  149.0 0.1 copy.21
  149.1 0.3 reshape.51
  149.4 9.0 %collective-permute-done = bf16[64,32,128]{2,1,0:T(8,128)(2,1)} collective-permute-done((bf16[64,32,128]{2,1,0:T(8,128)(2,1)}, bf16[64,32,128]{2,1,0:T(8,128)(2,1)}, u32[]{:S(2)}, u32[]{:S(2)}) %collective-permute-start) | collective-permute-done | bytes 524320 | tf_op jit(solution)/shard_map/ppermute | solution.py:18
  158.4 4.9 %collective-permute-done.1 = bf16[64,32,128]{2,1,0:T(8,128)(2,1)} collective-permute-done((bf16[64,32,128]{2,1,0:T(8,128)(2,1)}, bf16[64,32,128]{2,1,0:T(8,128)(2,1)}, u32[]{:S(2)}, u32[]{:S(2)}) %collective-permute-start.1) | collective-permute-done | bytes 524320 | tf_op jit(solution)/shard_map/ppermute | solution.py:18
  163.3 1.5 pad_maximum_fusion.1
  164.9 0.6 fusion.10
  165.5 0.1 copy.20
  165.6 0.3 convolution_convert_fusion.1
  165.9 2.2 %collective-permute-start.2 = (bf16[64,32,128]{2,1,0:T(8,128)(2,1)S(1)}, bf16[64,32,128]{2,1,0:T(8,128)(2,1)}, u32[]{:S(2)}, u32[]{:S(2)}) collective-permute-start(bf16[64,32,128]{2,1,0:T(8,128)(2,1)S(1)} %convolution_convert_fusion.1), channel_id=1, source_target_pairs={{0,2},{1,3},{2,4},{3,5},{4,6},{5,7},{6,8},{7,9},{8,10},{9,11},{10,... | collective-permute-start | bytes 1572872 | tf_op jit(solution)/shard_map/ppermute | solution.py:18
  168.2 2.1 %collective-permute-start.3 = (bf16[64,32,128]{2,1,0:T(8,128)(2,1)S(1)}, bf16[64,32,128]{2,1,0:T(8,128)(2,1)}, u32[]{:S(2)}, u32[]{:S(2)}) collective-permute-start(bf16[64,32,128]{2,1,0:T(8,128)(2,1)S(1)} %convolution_convert_fusion.1), channel_id=1, source_target_pairs={{0,1},{1,2},{2,3},{3,4},{4,5},{5,6},{6,7},{7,8},{8,9},{9,10},{10,1... | collective-permute-start | bytes 1572872 | tf_op jit(solution)/shard_map/ppermute | solution.py:18
  170.3 1.3 collective-permute-start.4
  171.5 1.3 collective-permute-start.5
  172.9 0.1 tile.32
  173.0 0.1 reshape.52
  173.1 6.6 %collective-permute-done.2 = bf16[64,32,128]{2,1,0:T(8,128)(2,1)} collective-permute-done((bf16[64,32,128]{2,1,0:T(8,128)(2,1)S(1)}, bf16[64,32,128]{2,1,0:T(8,128)(2,1)}, u32[]{:S(2)}, u32[]{:S(2)}) %collective-permute-start.2) | collective-permute-done | bytes 524320 | tf_op jit(solution)/shard_map/ppermute | solution.py:18
  179.7 1.1 constant_dynamic-update-slice_fusion.4
  180.8 1.1 constant_dynamic-update-slice_fusion.3
  181.9 0.1 constant_dynamic-update-slice_fusion.2
  182.0 0.0 collective-permute-done.4
  182.0 1.1 constant_dynamic-update-slice_fusion.1
  183.1 10.4 %collective-permute-done.5 = bf16[64,32,128]{2,1,0:T(8,128)(2,1)S(1)} collective-permute-done((bf16[64,32,128]{2,1,0:T(8,128)(2,1)S(1)}, bf16[64,32,128]{2,1,0:T(8,128)(2,1)S(1)}, u32[]{:S(2)}, u32[]{:S(2)}) %collective-permute-start.5) | collective-permute-done | bytes 524320 | tf_op jit(solution)/shard_map/ppermute | solution.py:18
  193.5 0.1 constant_dynamic-update-slice_fusion
  193.6 1.5 convolution_bitcast_fusion
  (16 shorter events, 0.1 us)
Async XLA Ops:
  0.6 1.6 copy-start
  5.5 15.7 %copy-start.2 = (f32[3,129]{1,0:T(4,128)S(1)}, f32[3,129]{1,0:T(4,128)}, u32[]{:S(2)}) copy-start(f32[3,129]{1,0:T(4,128)} %param.5) | copy-start | bytes 4648
  5.5 120.3 %all-to-all-start = ((bf16[32,272,128]{2,1,0:T(8,128)(2,1)}), bf16[32,272,128]{2,1,0:T(8,128)(2,1)}, u32[]{:S(2)}, u32[]{:S(2)}) async-start(bf16[32,272,128]{2,1,0:T(8,128)(2,1)} %copy.12), calls=%async_computation | async-start | bytes 4456448 | tf_op jit(solution)/shard_map/all_to_all | solution.py:45
  141.9 23.0 %copy-start.1 = (f32[64,32,128]{2,1,0:T(8,128)}, f32[64,32,128]{2,1,0:T(8,128)S(1)}, u32[]{:S(2)}) copy-start(f32[64,32,128]{2,1,0:T(8,128)S(1)} %reshape.47) | copy-start | bytes 3145732
  142.8 15.6 %collective-permute-start = (bf16[64,32,128]{2,1,0:T(8,128)(2,1)}, bf16[64,32,128]{2,1,0:T(8,128)(2,1)}, u32[]{:S(2)}, u32[]{:S(2)}) collective-permute-start(bf16[64,32,128]{2,1,0:T(8,128)(2,1)} %convert_element_type.44), channel_id=1, source_target_pairs={{0,32},{32,64},{64,96},{96,128},{128,160},{160,192},{192,224},{224... | collective-permute-start | bytes 1572872 | tf_op jit(solution)/shard_map/ppermute | solution.py:18
  145.9 17.4 %collective-permute-start.1 = (bf16[64,32,128]{2,1,0:T(8,128)(2,1)}, bf16[64,32,128]{2,1,0:T(8,128)(2,1)}, u32[]{:S(2)}, u32[]{:S(2)}) collective-permute-start(bf16[64,32,128]{2,1,0:T(8,128)(2,1)} %convert_element_type.44), channel_id=1, source_target_pairs={{32,0},{64,32},{96,64},{128,96},{160,128},{192,160},{224,192},{256... | collective-permute-start | bytes 1572872 | tf_op jit(solution)/shard_map/ppermute | solution.py:18
  165.9 13.8 %collective-permute-start.2 = (bf16[64,32,128]{2,1,0:T(8,128)(2,1)S(1)}, bf16[64,32,128]{2,1,0:T(8,128)(2,1)}, u32[]{:S(2)}, u32[]{:S(2)}) collective-permute-start(bf16[64,32,128]{2,1,0:T(8,128)(2,1)S(1)} %convolution_convert_fusion.1), channel_id=1, source_target_pairs={{0,2},{1,3},{2,4},{3,5},{4,6},{5,7},{6,8},{7,9},{8,10},{9,11},{10,... | collective-permute-start | bytes 1572872 | tf_op jit(solution)/shard_map/ppermute | solution.py:18
  168.2 12.7 %collective-permute-start.3 = (bf16[64,32,128]{2,1,0:T(8,128)(2,1)S(1)}, bf16[64,32,128]{2,1,0:T(8,128)(2,1)}, u32[]{:S(2)}, u32[]{:S(2)}) collective-permute-start(bf16[64,32,128]{2,1,0:T(8,128)(2,1)S(1)} %convolution_convert_fusion.1), channel_id=1, source_target_pairs={{0,1},{1,2},{2,3},{3,4},{4,5},{5,6},{6,7},{7,8},{8,9},{9,10},{10,1... | collective-permute-start | bytes 1572872 | tf_op jit(solution)/shard_map/ppermute | solution.py:18
  170.3 11.8 %collective-permute-start.4 = (bf16[64,32,128]{2,1,0:T(8,128)(2,1)S(1)}, bf16[64,32,128]{2,1,0:T(8,128)(2,1)}, u32[]{:S(2)}, u32[]{:S(2)}) collective-permute-start(bf16[64,32,128]{2,1,0:T(8,128)(2,1)S(1)} %convolution_convert_fusion.1), channel_id=1, source_target_pairs={{1,0},{2,1},{3,2},{4,3},{5,4},{6,5},{7,6},{8,7},{9,8},{10,9},{11,1... | collective-permute-start | bytes 1572872 | tf_op jit(solution)/shard_map/ppermute | solution.py:18
  171.5 22.0 %collective-permute-start.5 = (bf16[64,32,128]{2,1,0:T(8,128)(2,1)S(1)}, bf16[64,32,128]{2,1,0:T(8,128)(2,1)S(1)}, u32[]{:S(2)}, u32[]{:S(2)}) collective-permute-start(bf16[64,32,128]{2,1,0:T(8,128)(2,1)S(1)} %convolution_convert_fusion.1), channel_id=1, source_target_pairs={{2,0},{3,1},{4,2},{5,3},{6,4},{7,5},{8,6},{9,7},{10,8},{11,9},{12,... | collective-permute-start | bytes 1572872 | tf_op jit(solution)/shard_map/ppermute | solution.py:18

commit v5 on v4

--- a/solution.py
+++ b/solution.py
@@ -53,23 +53,28 @@
     norms = jnp.sqrt(jnp.sum(taps * taps, axis=1, keepdims=True))
     kernel = (taps / norms).astype(jnp.bfloat16)
     field = gradient.astype(jnp.bfloat16)
-    padded = jnp.concatenate(
-        [shifted(field, "xb", 1), field, shifted(field, "xb", -1)], axis=0
+    neighbours = (shifted(field, "xb", 1), field, shifted(field, "xb", -1))
+    x_matrix = band_matrix(kernel[0], CX, 3 * CX, 0)
+    along_x = sum(
+        jnp.dot(x_matrix[:, k * CX : (k + 1) * CX], part.reshape(CX, CZ * NY), preferred_element_type=jnp.float32)
+        for k, part in enumerate(neighbours)
     )
-    x_matrix = band_matrix(kernel[0], CX, 3 * CX, 0)
-    along_x = jnp.dot(x_matrix, padded.reshape(3 * CX, CZ * NY), preferred_element_type=jnp.float32)
     along_x = along_x.astype(jnp.bfloat16).reshape(CX, CZ, NY)
     y_matrix = band_matrix(kernel[1], NY, NY, REACH)
     along_y = jnp.einsum(
         "ab,xzb->xza", y_matrix, along_x, preferred_element_type=jnp.float32
     ).astype(jnp.bfloat16)
     reach_slabs = REACH // CZ
-    halo_lo = [shifted(along_y, "zs", s) for s in range(reach_slabs, 0, -1)]
-    halo_hi = [shifted(along_y, "zs", -s) for s in range(1, reach_slabs + 1)]
-    extended = jnp.concatenate(halo_lo + [along_y] + halo_hi, axis=1)
     z_matrix = band_matrix(kernel[2], CZ, CZ + 2 * REACH, 0)
-    smoothed = jnp.einsum(
-        "zk,xky->xzy", z_matrix, extended, preferred_element_type=jnp.float32
+    slabs = [(reach_slabs, along_y)]
+    for s in range(1, reach_slabs + 1):
+        slabs.append((reach_slabs - s, shifted(along_y, "zs", s)))
+        slabs.append((reach_slabs + s, shifted(along_y, "zs", -s)))
+    smoothed = sum(
+        jnp.einsum(
+            "zk,xky->xzy", z_matrix[:, k * CZ : (k + 1) * CZ], slab, preferred_element_type=jnp.float32
+        )
+        for k, slab in slabs
     )
     return (gradient, smoothed)
 

time: 196 us -> 197 us (level)
  the two profiles are of different devices: /device:TPU:24 before, /device:TPU:7 now
where the time goes in v5:
time: 197 us; the launch traced here: 195 us
  waiting for transfers between devices  120 us (61%)
  starting transfers between devices  33.4 us (17%)
  local copies, waits for them, and re-layouts  25.1 us (13%)
  matrix products  7.81 us (4%)
  other arithmetic  7.8 us (4%)
    all_to_all x1, waiting for transfers between devices, body(): lax.all_to_all(outgoing, 'zs', split_axis=0, concat_axis=0, tiled=True)  103 us
    ppermute x6, waiting for transfers between devices, shifted(): return lax.ppermute(x, axis, pairs)  17.4 us
    ppermute x6, starting transfers between devices, shifted(): return lax.ppermute(x, axis, pairs)  17.3 us
    all_to_all x1, starting transfers between devices, body(): lax.all_to_all(outgoing, 'zs', split_axis=0, concat_axis=0, tiled=True)  16.1 us
    convert_element_type x2, local copies, waits for them, and re-layouts, body(): field = gradient.astype(jnp.bfloat16)  7.75 us
    transpose x1, local copies, waits for them, and re-layouts, body(): assembled.reshape(2, YBLOCKS, BLK, BLK, BLK).transpose(0, 2, 4, 1, 3)  5.24 us
    convert_element_type x2, other arithmetic, body(): field = gradient.astype(jnp.bfloat16)  4.97 us
  transfers between devices with their start and end apart: 7, of which 4 were waited for; matrix products, arithmetic and copies ran while one was open for 8% of the time, Pallas kernels for 0%

profile of v5, /device:TPU:7, one launch (start us, length us, event | category | flops | bytes accessed | tf_op | source)
XLA Modules:
  0.0 195.4 jit_solution(17361504131556086989)
XLA Ops:
  0.6 0.0 copy-start
  0.6 0.8 fusion.34
  1.5 0.1 select_reduce_fusion
  1.6 0.7 copy-done
  2.2 0.7 fusion.7
  2.9 0.1 broadcast_in_dim.29
  3.0 0.2 pad_maximum_fusion
  3.2 2.2 %copy.13 = bf16[32,272,128]{2,1,0:T(8,128)(2,1)} copy(bf16[32,272,128]{2,0,1:T(8,128)(2,1)S(1)} %pad_maximum_fusion) | data formatting | bytes 4456448 | tf_op jit(solution)/shard_map/concatenate | solution.py:44
  5.5 16.1 %all-to-all-start = ((bf16[32,272,128]{2,1,0:T(8,128)(2,1)}), bf16[32,272,128]{2,1,0:T(8,128)(2,1)}, u32[]{:S(2)}, u32[]{:S(2)}) async-start(bf16[32,272,128]{2,1,0:T(8,128)(2,1)} %copy.13), calls=%async_computation | async-start | bytes 4456448 | tf_op jit(solution)/shard_map/all_to_all | solution.py:45
  21.6 0.1 multiply_reduce_fusion
  21.7 0.1 divide_convert_fusion
  21.9 0.2 reshape.54
  22.1 0.1 pad_slice_fusion.1
  22.2 0.1 copy.24
  22.2 0.3 reshape.58
  22.6 103.0 %all-to-all-done = bf16[32,272,128]{2,1,0:T(8,128)(2,1)} async-done(((bf16[32,272,128]{2,1,0:T(8,128)(2,1)}), bf16[32,272,128]{2,1,0:T(8,128)(2,1)}, u32[]{:S(2)}, u32[]{:S(2)}) %all-to-all-start) | async-done | bytes 2228256 | tf_op jit(solution)/shard_map/all_to_all | solution.py:45
  125.5 1.7 slice.97
  127.3 1.5 fusion.23
  128.8 1.2 fusion.5
  130.0 0.2 copy.15
  130.2 2.4 %reshape.52 = f32[2,4,32,32,32]{4,3,2,1,0:T(8,128)} reshape(f32[8,256,128]{2,1,0:T(8,128)S(1)} %copy.15) | data formatting | bytes 2097152 | tf_op jit(solution)/shard_map/reshape | solution.py:51
  132.6 5.2 %copy.16 = f32[2,32,32,4,32]{4,3,2,1,0:T(4,128)} copy(f32[2,32,32,4,32]{2,4,1,3,0:T(8,128)} %bitcast.68) | data formatting | bytes 2097152 | tf_op jit(solution)/shard_map/transpose | solution.py:51
  137.9 3.7 %reshape.53 = f32[64,32,128]{2,1,0:T(8,128)S(1)} reshape(f32[2,32,32,4,32]{4,3,2,1,0:T(4,128)} %copy.16) | data formatting | bytes 2097152 | tf_op jit(solution)/shard_map/reshape | solution.py:52
  141.6 1.0 convert_element_type.50
  142.6 4.9 %collective-permute-start.1 = (bf16[64,32,128]{2,1,0:T(8,128)(2,1)}, bf16[64,32,128]{2,1,0:T(8,128)(2,1)}, u32[]{:S(2)}, u32[]{:S(2)}) collective-permute-start(bf16[64,32,128]{2,1,0:T(8,128)(2,1)} %convert_element_type.50), channel_id=1, source_target_pairs={{32,0},{64,32},{96,64},{128,96},{160,128},{192,160},{224,192},{256... | collective-permute-start | bytes 1572872 | tf_op jit(solution)/shard_map/ppermute | solution.py:18
  147.5 1.9 collective-permute-start
  149.4 4.0 %bitcast_convert_fusion = bf16[2,32,32,4,32]{2,4,1,3,0:T(8,128)(2,1)} fusion(f32[2,4,32,32,32]{4,3,2,1,0:T(8,128)} %reshape.52), kind=kLoop, calls=%fused_computation.63 | loop fusion | flops 262144 | bytes 1572864 | tf_op jit(solution)/shard_map/convert_element_type | solution.py:55
  153.4 4.3 %copy.17 = bf16[2,32,32,4,32]{4,3,2,1,0:T(4,128)(2,1)} copy(bf16[2,32,32,4,32]{2,4,1,3,0:T(8,128)(2,1)} %bitcast_convert_fusion) | data formatting | bytes 1048576 | tf_op jit(solution)/shard_map/convert_element_type | solution.py:55
  157.7 3.5 %convert_element_type.52 = bf16[64,4096]{1,0:T(8,128)(2,1)S(1)} reshape(bf16[2,32,32,4,32]{4,3,2,1,0:T(4,128)(2,1)} %copy.17) | data formatting | bytes 1048576 | tf_op jit(solution)/shard_map/convert_element_type | solution.py:55
  161.2 0.3 fusion.20
  161.5 1.3 fusion.14
  162.9 1.1 collective-permute-done
  164.0 1.4 fusion.13
  165.4 0.1 copy.23
  165.5 0.3 convolution_convert_fusion
  165.8 1.3 collective-permute-start.4
  167.1 0.1 tile.32
  167.2 0.1 reshape.59
  167.4 6.0 %collective-permute-start.2 = (bf16[64,32,128]{2,1,0:T(8,128)(2,1)S(1)}, bf16[64,32,128]{2,1,0:T(8,128)(2,1)S(1)}, u32[]{:S(2)}, u32[]{:S(2)}) collective-permute-start(bf16[64,32,128]{2,1,0:T(8,128)(2,1)S(1)} %convolution_convert_fusion), channel_id=1, source_target_pairs={{0,1},{1,2},{2,3},{3,4},{4,5},{5,6},{6,7},{7,8},{8,9},{9,10},{10,1... | collective-permute-start | bytes 1572872 | tf_op jit(solution)/shard_map/ppermute | solution.py:18
  173.3 1.3 collective-permute-start.5
  174.6 1.9 collective-permute-start.3
  176.6 0.3 fusion.28
  176.9 0.3 fusion.27
  177.2 11.6 %collective-permute-done.5 = bf16[64,32,128]{2,1,0:T(8,128)(2,1)S(1)} collective-permute-done((bf16[64,32,128]{2,1,0:T(8,128)(2,1)S(1)}, bf16[64,32,128]{2,1,0:T(8,128)(2,1)S(1)}, u32[]{:S(2)}, u32[]{:S(2)}) %collective-permute-start.5) | collective-permute-done | bytes 524320 | tf_op jit(solution)/shard_map/ppermute | solution.py:18
  188.8 0.3 fusion.26
  189.1 0.3 convolution_add_fusion.2
  189.4 4.7 %collective-permute-done.3 = bf16[64,32,128]{2,1,0:T(8,128)(2,1)S(1)} collective-permute-done((bf16[64,32,128]{2,1,0:T(8,128)(2,1)S(1)}, bf16[64,32,128]{2,1,0:T(8,128)(2,1)S(1)}, u32[]{:S(2)}, u32[]{:S(2)}) %collective-permute-start.3) | collective-permute-done | bytes 524320 | tf_op jit(solution)/shard_map/ppermute | solution.py:18
  194.1 1.3 fusion.12
  (19 shorter events, 0.2 us)
Async XLA Ops:
  0.6 1.6 copy-start
  5.5 16.1 %copy-start.2 = (f32[3,129]{1,0:T(4,128)S(1)}, f32[3,129]{1,0:T(4,128)}, u32[]{:S(2)}) copy-start(f32[3,129]{1,0:T(4,128)} %param.5) | copy-start | bytes 4648
  5.5 120.1 %all-to-all-start = ((bf16[32,272,128]{2,1,0:T(8,128)(2,1)}), bf16[32,272,128]{2,1,0:T(8,128)(2,1)}, u32[]{:S(2)}, u32[]{:S(2)}) async-start(bf16[32,272,128]{2,1,0:T(8,128)(2,1)} %copy.13), calls=%async_computation | async-start | bytes 4456448 | tf_op jit(solution)/shard_map/all_to_all | solution.py:45
  141.6 11.8 %copy-start.1 = (f32[64,32,128]{2,1,0:T(8,128)}, f32[64,32,128]{2,1,0:T(8,128)S(1)}, u32[]{:S(2)}) copy-start(f32[64,32,128]{2,1,0:T(8,128)S(1)} %reshape.53) | copy-start | bytes 3145732
  142.6 19.0 %collective-permute-start.1 = (bf16[64,32,128]{2,1,0:T(8,128)(2,1)}, bf16[64,32,128]{2,1,0:T(8,128)(2,1)}, u32[]{:S(2)}, u32[]{:S(2)}) collective-permute-start(bf16[64,32,128]{2,1,0:T(8,128)(2,1)} %convert_element_type.50), channel_id=1, source_target_pairs={{32,0},{64,32},{96,64},{128,96},{160,128},{192,160},{224,192},{256... | collective-permute-start | bytes 1572872 | tf_op jit(solution)/shard_map/ppermute | solution.py:18
  147.5 16.5 %collective-permute-start = (bf16[64,32,128]{2,1,0:T(8,128)(2,1)}, bf16[64,32,128]{2,1,0:T(8,128)(2,1)}, u32[]{:S(2)}, u32[]{:S(2)}) collective-permute-start(bf16[64,32,128]{2,1,0:T(8,128)(2,1)} %convert_element_type.50), channel_id=1, source_target_pairs={{0,32},{32,64},{64,96},{96,128},{128,160},{160,192},{192,224},{224... | collective-permute-start | bytes 1572872 | tf_op jit(solution)/shard_map/ppermute | solution.py:18
  165.8 11.2 %collective-permute-start.4 = (bf16[64,32,128]{2,1,0:T(8,128)(2,1)S(1)}, bf16[64,32,128]{2,1,0:T(8,128)(2,1)S(1)}, u32[]{:S(2)}, u32[]{:S(2)}) collective-permute-start(bf16[64,32,128]{2,1,0:T(8,128)(2,1)S(1)} %convolution_convert_fusion), channel_id=1, source_target_pairs={{0,2},{1,3},{2,4},{3,5},{4,6},{5,7},{6,8},{7,9},{8,10},{9,11},{10,... | collective-permute-start | bytes 1572872 | tf_op jit(solution)/shard_map/ppermute | solution.py:18
  167.4 21.7 %collective-permute-start.2 = (bf16[64,32,128]{2,1,0:T(8,128)(2,1)S(1)}, bf16[64,32,128]{2,1,0:T(8,128)(2,1)S(1)}, u32[]{:S(2)}, u32[]{:S(2)}) collective-permute-start(bf16[64,32,128]{2,1,0:T(8,128)(2,1)S(1)} %convolution_convert_fusion), channel_id=1, source_target_pairs={{0,1},{1,2},{2,3},{3,4},{4,5},{5,6},{6,7},{7,8},{8,9},{9,10},{10,1... | collective-permute-start | bytes 1572872 | tf_op jit(solution)/shard_map/ppermute | solution.py:18
  173.3 15.5 %collective-permute-start.5 = (bf16[64,32,128]{2,1,0:T(8,128)(2,1)S(1)}, bf16[64,32,128]{2,1,0:T(8,128)(2,1)S(1)}, u32[]{:S(2)}, u32[]{:S(2)}) collective-permute-start(bf16[64,32,128]{2,1,0:T(8,128)(2,1)S(1)} %convolution_convert_fusion), channel_id=1, source_target_pairs={{2,0},{3,1},{4,2},{5,3},{6,4},{7,5},{8,6},{9,7},{10,8},{11,9},{12,... | collective-permute-start | bytes 1572872 | tf_op jit(solution)/shard_map/ppermute | solution.py:18
  174.6 19.4 %collective-permute-start.3 = (bf16[64,32,128]{2,1,0:T(8,128)(2,1)S(1)}, bf16[64,32,128]{2,1,0:T(8,128)(2,1)S(1)}, u32[]{:S(2)}, u32[]{:S(2)}) collective-permute-start(bf16[64,32,128]{2,1,0:T(8,128)(2,1)S(1)} %convolution_convert_fusion), channel_id=1, source_target_pairs={{1,0},{2,1},{3,2},{4,3},{5,4},{6,5},{7,6},{8,7},{9,8},{10,9},{11,1... | collective-permute-start | bytes 1572872 | tf_op jit(solution)/shard_map/ppermute | solution.py:18

commit v6 on v5

--- a/solution.py
+++ b/solution.py
@@ -1,6 +1,8 @@
 import jax
 import jax.numpy as jnp
 from jax import lax
+from jax.experimental import pallas as pl
+from jax.experimental.pallas import tpu as pltpu
 from jax.sharding import PartitionSpec as P
 
 BLK = 32
@@ -16,6 +18,45 @@
     count = lax.axis_size(axis)
     pairs = [(i, i + step) for i in range(count) if 0 <= i + step < count]
     return lax.ppermute(x, axis, pairs)
+
+
+def place_kernel(ids_ref, arrived_ref, gradient_ref, field_ref, acc_ref):
+    sources = arrived_ref.shape[0]
+    acc_ref[...] = jnp.zeros_like(acc_ref)
+    for s in range(sources):
+        acc_ref[ids_ref[s]] += arrived_ref[s].astype(jnp.float32)
+    planes = acc_ref.shape[1] // 8
+    for b in range(2 * YBLOCKS):
+        lx, ly = b // YBLOCKS, b % YBLOCKS
+        cube = acc_ref[b].reshape(planes, 8, 128 // BLK, BLK)
+        cube = jnp.transpose(cube, (0, 3, 1, 2)).reshape(planes, BLK, BLK)
+        gradient_ref[lx, :, :, ly * BLK : (ly + 1) * BLK] = cube
+        field_ref[lx, :, :, ly * BLK : (ly + 1) * BLK] = cube.astype(jnp.bfloat16)
+
+
+def place(ids, arrived):
+    sources = arrived.shape[0]
+    planes = 8
+    steps = BLK // planes
+    grid_spec = pltpu.PrefetchScalarGridSpec(
+        num_scalar_prefetch=1,
+        grid=(steps,),
+        in_specs=[pl.BlockSpec((sources, planes * 8, 128), lambda i, ids: (0, i, 0))],
+        out_specs=[
+            pl.BlockSpec((2, planes, BLK, NY), lambda i, ids: (0, i, 0, 0)),
+            pl.BlockSpec((2, planes, BLK, NY), lambda i, ids: (0, i, 0, 0)),
+        ],
+        scratch_shapes=[pltpu.VMEM((2 * YBLOCKS, planes * 8, 128), jnp.float32)],
+    )
+    gradient, field = pl.pallas_call(
+        place_kernel,
+        grid_spec=grid_spec,
+        out_shape=[
+            jax.ShapeDtypeStruct((2, BLK, BLK, NY), jnp.float32),
+            jax.ShapeDtypeStruct((2, BLK, BLK, NY), jnp.bfloat16),
+        ],
+    )(ids, arrived)
+    return gradient.reshape(CX, CZ, NY), field.reshape(CX, CZ, NY)
 
 
 def band_matrix(kern_row, rows, cols, offset):
@@ -43,16 +84,10 @@
     id_rows = jnp.broadcast_to(packed_ids[:, None, None], (owners_count, 16, 128))
     outgoing = jnp.concatenate([packed, id_rows], axis=1)
     arrived_all = lax.all_to_all(outgoing, "zs", split_axis=0, concat_axis=0, tiled=True)
-    arrived = arrived_all[:, : CELLS // 128]
-    arrived_ids = arrived_all[:, CELLS // 128, 0].astype(jnp.int32)
-    placing = (arrived_ids[None, :] == jnp.arange(blocks_local)[:, None]).astype(jnp.bfloat16)
-    assembled = jnp.einsum("bs,skc->bkc", placing, arrived, preferred_element_type=jnp.float32)
-    assembled = lax.optimization_barrier(assembled)
-    assembled = assembled.reshape(2, YBLOCKS, BLK, BLK, BLK).transpose(0, 2, 4, 1, 3)
-    gradient = assembled.reshape(CX, CZ, NY)
+    arrived_ids = jnp.clip(arrived_all[:, CELLS // 128, 0].astype(jnp.int32), 0, blocks_local - 1)
+    gradient, field = place(arrived_ids, arrived_all)
     norms = jnp.sqrt(jnp.sum(taps * taps, axis=1, keepdims=True))
     kernel = (taps / norms).astype(jnp.bfloat16)
-    field = gradient.astype(jnp.bfloat16)
     neighbours = (shifted(field, "xb", 1), field, shifted(field, "xb", -1))
     x_matrix = band_matrix(kernel[0], CX, 3 * CX, 0)
     along_x = sum(

time: 197 us -> 209 us (1.061)
  Pallas kernels: 0 us -> 33.1 us
  local copies, waits for them, and re-layouts: 25.1 us -> 2.64 us
  waiting for transfers between devices: 120 us -> 127 us
  other arithmetic: 7.8 us -> 4.76 us
  matrix products: 7.81 us -> 5.54 us
    pallas_call x0 -> x1, Pallas kernels: none -> 33.1 us  [place(): pl.pallas_call(place_kernel, grid_spec=grid_spec, out_shape=[jax.ShapeDty...]
    convert_element_type x2 -> x0, local copies, waits for them, and re-layouts: 7.75 us -> none  [body(): field = gradient.astype(jnp.bfloat16)]
    convert_element_type x3 -> x0, other arithmetic: 6.47 us -> none  [the longest x2 4.97 us: body(): field = gradient.astype(jnp.bfloat16)]
    reshape x2 -> x0, local copies, waits for them, and re-layouts: 6.13 us -> none  [the longest x1 3.71 us: body(): gradient = assembled.reshape(CX, CZ, NY)]
    ppermute x6, waiting for transfers between devices: 17.4 us -> 23.1 us  [shifted(): return lax.ppermute(x, axis, pairs)]
    transpose x1 -> x0, local copies, waits for them, and re-layouts: 5.24 us -> none  [body(): assembled.reshape(2, YBLOCKS, BLK, BLK, BLK).transpose(0, 2, 4, 1, 3)]
    concatenate x1 -> x0, local copies, waits for them, and re-layouts: 2.23 us -> none  [body(): outgoing = jnp.concatenate([packed, id_rows], axis=1)]
  transfers between devices with their start and end apart: 7 -> 7, of which waited for: 4 -> 6; matrix products, arithmetic and copies ran while one was open for 8% -> 2% of each run, Pallas kernels for 0% -> 0%
where the time goes in v6:
time: 209 us; the launch traced here: 208 us
  waiting for transfers between devices  127 us (61%)
  starting transfers between devices  34.4 us (16%)
  Pallas kernels  33.1 us (16%)
  matrix products  5.54 us (3%)
  other arithmetic  4.76 us (2%)
  local copies, waits for them, and re-layouts  2.64 us (1%)
    all_to_all x1, waiting for transfers between devices, body(): lax.all_to_all(outgoing, 'zs', split_axis=0, concat_axis=0, tiled=True)  104 us
    pallas_call x1, Pallas kernels, place(): pl.pallas_call(place_kernel, grid_spec=grid_spec, out_shape=[jax.ShapeDty...  33.1 us
    ppermute x6, waiting for transfers between devices, shifted(): return lax.ppermute(x, axis, pairs)  23.1 us
    ppermute x6, starting transfers between devices, shifted(): return lax.ppermute(x, axis, pairs)  18.3 us
    all_to_all x1, starting transfers between devices, body(): lax.all_to_all(outgoing, 'zs', split_axis=0, concat_axis=0, tiled=True)  16.1 us
  transfers between devices with their start and end apart: 7, of which 6 were waited for; matrix products, arithmetic and copies ran while one was open for 2% of the time, Pallas kernels for 0%

profile of v6, /device:TPU:7, one launch (start us, length us, event | category | flops | bytes accessed | tf_op | source)
XLA Modules:
  0.0 208.0 jit_solution(2052130416076034927)
XLA Ops:
  0.6 0.0 copy-start
  0.6 0.8 fusion.29
  1.5 0.1 select_reduce_fusion
  1.6 0.7 copy-done
  2.2 0.7 fusion.2
  2.9 0.8 copy.33
  3.8 0.1 broadcast_in_dim.27
  3.9 1.5 pad_maximum_fusion
  5.4 0.0 copy-start.1
  5.4 16.1 %all-to-all-start = ((bf16[32,272,128]{2,1,0:T(8,128)(2,1)}), bf16[32,272,128]{2,1,0:T(8,128)(2,1)}, u32[]{:S(2)}, u32[]{:S(2)}) async-start(bf16[32,272,128]{2,1,0:T(8,128)(2,1)} %pad_maximum_fusion), calls=%async_computation | async-start | bytes 4456448 | tf_op jit(solution)/shard_map/all_to_all | solution.py:86
  21.5 0.0 copy-done.1
  21.5 0.1 multiply_reduce_fusion
  21.6 0.1 divide_convert_fusion
  21.8 0.1 pad_slice_fusion.1
  21.9 103.6 %all-to-all-done.arrived_ref = bf16[32,272,128]{2,1,0:T(8,128)(2,1)} async-done(((bf16[32,272,128]{2,1,0:T(8,128)(2,1)}), bf16[32,272,128]{2,1,0:T(8,128)(2,1)}, u32[]{:S(2)}, u32[]{:S(2)}) %all-to-all-start) | async-done | bytes 2228256 | tf_op jit(solution)/shard_map/all_to_all | solution.py:86
  125.5 2.1 %fusion.22.ids_ref = s32[32]{0:T(128)} fusion(bf16[32,272,128]{2,1,0:T(8,128)(2,1)} %all-to-all-done.arrived_ref), kind=kLoop, calls=%fused_computation.34 | loop fusion | flops 64 | bytes 192 | tf_op jit(solution)/shard_map/jit(clip)/min | solution.py:87
  127.6 33.1 %shard_map.50 = (f32[2,32,32,128]{3,2,1,0:T(8,128)}, bf16[2,32,32,128]{3,2,1,0:T(8,128)(2,1)}) custom-call(s32[32]{0:T(128)} %fusion.22.ids_ref, bf16[32,272,128]{2,1,0:T(8,128)(2,1)} %all-to-all-done.arrived_ref), custom_call_target="tpu_custom_call" | custom-call | tf_op jit(solution)/shard_map/pallas_call | solution.py:51
  160.7 4.9 %collective-permute-start.1 = (bf16[64,32,128]{2,1,0:T(8,128)(2,1)}, bf16[64,32,128]{2,1,0:T(8,128)(2,1)S(1)}, u32[]{:S(2)}, u32[]{:S(2)}) collective-permute-start(bf16[64,32,128]{2,1,0:T(8,128)(2,1)} %bitcast.68), channel_id=1, source_target_pairs={{32,0},{64,32},{96,64},{128,96},{160,128},{192,160},{224,192},{256... | collective-permute-start | bytes 1572872 | tf_op jit(solution)/shard_map/ppermute | solution.py:20
  165.6 0.2 reshape.47
  165.9 0.1 copy.15
  165.9 0.3 reshape.52
  166.2 1.9 collective-permute-start
  168.2 1.4 fusion.12
  169.6 6.6 %collective-permute-done.1 = bf16[64,32,128]{2,1,0:T(8,128)(2,1)S(1)} collective-permute-done((bf16[64,32,128]{2,1,0:T(8,128)(2,1)}, bf16[64,32,128]{2,1,0:T(8,128)(2,1)S(1)}, u32[]{:S(2)}, u32[]{:S(2)}) %collective-permute-start.1) | collective-permute-done | bytes 524320 | tf_op jit(solution)/shard_map/ppermute | solution.py:20
  176.2 0.3 fusion.9
  176.5 6.1 %collective-permute-done = bf16[64,32,128]{2,1,0:T(8,128)(2,1)S(1)} collective-permute-done((bf16[64,32,128]{2,1,0:T(8,128)(2,1)}, bf16[64,32,128]{2,1,0:T(8,128)(2,1)S(1)}, u32[]{:S(2)}, u32[]{:S(2)}) %collective-permute-start) | collective-permute-done | bytes 524320 | tf_op jit(solution)/shard_map/ppermute | solution.py:20
  182.6 0.3 fusion.8
  183.0 0.1 copy.14
  183.1 0.3 convolution_convert_fusion
  183.4 1.3 collective-permute-start.5
  184.7 0.1 tile.32
  184.8 0.1 reshape.53
  184.9 4.0 %collective-permute-start.4 = (bf16[64,32,128]{2,1,0:T(8,128)(2,1)S(1)}, bf16[64,32,128]{2,1,0:T(8,128)(2,1)S(1)}, u32[]{:S(2)}, u32[]{:S(2)}) collective-permute-start(bf16[64,32,128]{2,1,0:T(8,128)(2,1)S(1)} %convolution_convert_fusion), channel_id=1, source_target_pairs={{0,2},{1,3},{2,4},{3,5},{4,6},{5,7},{6,8},{7,9},{8,10},{9,11},{10,... | collective-permute-start | bytes 1572872 | tf_op jit(solution)/shard_map/ppermute | solution.py:20
  189.0 4.2 %collective-permute-start.2 = (bf16[64,32,128]{2,1,0:T(8,128)(2,1)S(1)}, bf16[64,32,128]{2,1,0:T(8,128)(2,1)S(1)}, u32[]{:S(2)}, u32[]{:S(2)}) collective-permute-start(bf16[64,32,128]{2,1,0:T(8,128)(2,1)S(1)} %convolution_convert_fusion), channel_id=1, source_target_pairs={{0,1},{1,2},{2,3},{3,4},{4,5},{5,6},{6,7},{7,8},{8,9},{9,10},{10,1... | collective-permute-start | bytes 1572872 | tf_op jit(solution)/shard_map/ppermute | solution.py:20
  193.2 1.9 collective-permute-start.3
  195.1 0.3 fusion.26
  195.4 1.1 collective-permute-done.5
  196.5 0.3 fusion.24
  196.8 0.9 collective-permute-done.4
  197.7 0.3 fusion.25
  198.0 8.3 %collective-permute-done.2 = bf16[64,32,128]{2,1,0:T(8,128)(2,1)S(1)} collective-permute-done((bf16[64,32,128]{2,1,0:T(8,128)(2,1)S(1)}, bf16[64,32,128]{2,1,0:T(8,128)(2,1)S(1)}, u32[]{:S(2)}, u32[]{:S(2)}) %collective-permute-start.2) | collective-permute-done | bytes 524320 | tf_op jit(solution)/shard_map/ppermute | solution.py:20
  206.3 0.3 convolution_add_fusion.2
  206.6 0.0 collective-permute-done.3
  206.6 1.3 fusion.7
  (12 shorter events, 0.1 us)
Async XLA Ops:
  0.6 1.6 copy-start
  5.4 16.1 %copy-start.1 = (f32[3,129]{1,0:T(4,128)S(1)}, f32[3,129]{1,0:T(4,128)}, u32[]{:S(2)}) copy-start(f32[3,129]{1,0:T(4,128)} %param.5) | copy-start | bytes 4648
  5.4 120.1 %all-to-all-start = ((bf16[32,272,128]{2,1,0:T(8,128)(2,1)}), bf16[32,272,128]{2,1,0:T(8,128)(2,1)}, u32[]{:S(2)}, u32[]{:S(2)}) async-start(bf16[32,272,128]{2,1,0:T(8,128)(2,1)} %pad_maximum_fusion), calls=%async_computation | async-start | bytes 4456448 | tf_op jit(solution)/shard_map/all_to_all | solution.py:86
  160.7 15.5 %collective-permute-start.1 = (bf16[64,32,128]{2,1,0:T(8,128)(2,1)}, bf16[64,32,128]{2,1,0:T(8,128)(2,1)S(1)}, u32[]{:S(2)}, u32[]{:S(2)}) collective-permute-start(bf16[64,32,128]{2,1,0:T(8,128)(2,1)} %bitcast.68), channel_id=1, source_target_pairs={{32,0},{64,32},{96,64},{128,96},{160,128},{192,160},{224,192},{256... | collective-permute-start | bytes 1572872 | tf_op jit(solution)/shard_map/ppermute | solution.py:20
  166.2 16.4 %collective-permute-start = (bf16[64,32,128]{2,1,0:T(8,128)(2,1)}, bf16[64,32,128]{2,1,0:T(8,128)(2,1)S(1)}, u32[]{:S(2)}, u32[]{:S(2)}) collective-permute-start(bf16[64,32,128]{2,1,0:T(8,128)(2,1)} %bitcast.69), channel_id=1, source_target_pairs={{0,32},{32,64},{64,96},{96,128},{128,160},{160,192},{192,224},{224... | collective-permute-start | bytes 1572872 | tf_op jit(solution)/shard_map/ppermute | solution.py:20
  183.4 13.2 %collective-permute-start.5 = (bf16[64,32,128]{2,1,0:T(8,128)(2,1)S(1)}, bf16[64,32,128]{2,1,0:T(8,128)(2,1)S(1)}, u32[]{:S(2)}, u32[]{:S(2)}) collective-permute-start(bf16[64,32,128]{2,1,0:T(8,128)(2,1)S(1)} %convolution_convert_fusion), channel_id=1, source_target_pairs={{2,0},{3,1},{4,2},{5,3},{6,4},{7,5},{8,6},{9,7},{10,8},{11,9},{12,... | collective-permute-start | bytes 1572872 | tf_op jit(solution)/shard_map/ppermute | solution.py:20
  184.9 12.8 %collective-permute-start.4 = (bf16[64,32,128]{2,1,0:T(8,128)(2,1)S(1)}, bf16[64,32,128]{2,1,0:T(8,128)(2,1)S(1)}, u32[]{:S(2)}, u32[]{:S(2)}) collective-permute-start(bf16[64,32,128]{2,1,0:T(8,128)(2,1)S(1)} %convolution_convert_fusion), channel_id=1, source_target_pairs={{0,2},{1,3},{2,4},{3,5},{4,6},{5,7},{6,8},{7,9},{8,10},{9,11},{10,... | collective-permute-start | bytes 1572872 | tf_op jit(solution)/shard_map/ppermute | solution.py:20
  189.0 17.3 %collective-permute-start.2 = (bf16[64,32,128]{2,1,0:T(8,128)(2,1)S(1)}, bf16[64,32,128]{2,1,0:T(8,128)(2,1)S(1)}, u32[]{:S(2)}, u32[]{:S(2)}) collective-permute-start(bf16[64,32,128]{2,1,0:T(8,128)(2,1)S(1)} %convolution_convert_fusion), channel_id=1, source_target_pairs={{0,1},{1,2},{2,3},{3,4},{4,5},{5,6},{6,7},{7,8},{8,9},{9,10},{10,1... | collective-permute-start | bytes 1572872 | tf_op jit(solution)/shard_map/ppermute | solution.py:20
  193.2 13.5 %collective-permute-start.3 = (bf16[64,32,128]{2,1,0:T(8,128)(2,1)S(1)}, bf16[64,32,128]{2,1,0:T(8,128)(2,1)S(1)}, u32[]{:S(2)}, u32[]{:S(2)}) collective-permute-start(bf16[64,32,128]{2,1,0:T(8,128)(2,1)S(1)} %convolution_convert_fusion), channel_id=1, source_target_pairs={{1,0},{2,1},{3,2},{4,3},{5,4},{6,5},{7,6},{8,7},{9,8},{10,9},{11,1... | collective-permute-start | bytes 1572872 | tf_op jit(solution)/shard_map/ppermute | solution.py:20

commit v7 on v5

--- a/solution.py
+++ b/solution.py
@@ -43,17 +43,26 @@
     id_rows = jnp.broadcast_to(packed_ids[:, None, None], (owners_count, 16, 128))
     outgoing = jnp.concatenate([packed, id_rows], axis=1)
     arrived_all = lax.all_to_all(outgoing, "zs", split_axis=0, concat_axis=0, tiled=True)
-    arrived = arrived_all[:, : CELLS // 128]
     arrived_ids = arrived_all[:, CELLS // 128, 0].astype(jnp.int32)
-    placing = (arrived_ids[None, :] == jnp.arange(blocks_local)[:, None]).astype(jnp.bfloat16)
-    assembled = jnp.einsum("bs,skc->bkc", placing, arrived, preferred_element_type=jnp.float32)
-    assembled = lax.optimization_barrier(assembled)
-    assembled = assembled.reshape(2, YBLOCKS, BLK, BLK, BLK).transpose(0, 2, 4, 1, 3)
-    gradient = assembled.reshape(CX, CZ, NY)
+    order = jnp.arange(blocks_local)
+    slot = (order % 2) * YBLOCKS + order // 2
+    placing = (arrived_ids[None, :] == slot[:, None]).astype(jnp.bfloat16)
+    summed = jnp.einsum("bs,skc->bkc", placing, arrived_all, preferred_element_type=jnp.float32)
+    summed = summed[:, : CELLS // 128]
+    lanes = 128 // BLK
+    rows = CELLS // 128 // BLK
+    field_u = summed.astype(jnp.bfloat16).reshape(YBLOCKS, CX, rows, 128)
+    halo_u = (shifted(field_u, "xb", 1), shifted(field_u, "xb", -1))
+
+    def to_xzy(u):
+        u = u.reshape(YBLOCKS, CX, rows, lanes, BLK).transpose(1, 4, 0, 2, 3)
+        return u.reshape(CX, CZ, NY)
+
+    gradient = to_xzy(summed)
     norms = jnp.sqrt(jnp.sum(taps * taps, axis=1, keepdims=True))
     kernel = (taps / norms).astype(jnp.bfloat16)
     field = gradient.astype(jnp.bfloat16)
-    neighbours = (shifted(field, "xb", 1), field, shifted(field, "xb", -1))
+    neighbours = (to_xzy(halo_u[0]), field, to_xzy(halo_u[1]))
     x_matrix = band_matrix(kernel[0], CX, 3 * CX, 0)
     along_x = sum(
         jnp.dot(x_matrix[:, k * CX : (k + 1) * CX], part.reshape(CX, CZ * NY), preferred_element_type=jnp.float32)

time: 197 us -> 208 us (1.056)
  matrix products: 7.81 us -> 20.8 us
  waiting for transfers between devices: 120 us -> 111 us
  local copies, waits for them, and re-layouts: 25.1 us -> 33.2 us
  other arithmetic: 7.8 us -> 2.84 us
  starting transfers between devices: 33.4 us -> 37.5 us
    slice x0 -> x1, matrix products: none -> 15.7 us  [body(): summed = summed[:, :CELLS // 128]]
    ppermute x6, waiting for transfers between devices: 17.4 us -> 7.84 us  [shifted(): return lax.ppermute(x, axis, pairs)]
    convert_element_type x2 -> x1, local copies, waits for them, and re-layouts: 7.75 us -> 0.55 us  [body(): field = gradient.astype(jnp.bfloat16)]
    convert_element_type x2 -> x0, other arithmetic: 4.97 us -> none  [body(): field = gradient.astype(jnp.bfloat16)]
    ppermute x0 -> x2, local copies, waits for them, and re-layouts: none -> 4.76 us  [shifted(): return lax.ppermute(x, axis, pairs)]
    transpose x1 -> x3, local copies, waits for them, and re-layouts: 5.24 us -> 9.81 us  [to_xzy(): u = u.reshape(YBLOCKS, CX, rows, lanes, BLK).transpose(1, 4, 0, 2, 3)]
    unnamed x11 -> x12, local copies, waits for them, and re-layouts: 0.86 us -> 4.75 us
    ppermute x6, starting transfers between devices: 17.3 us -> 21.2 us  [shifted(): return lax.ppermute(x, axis, pairs)]
  transfers between devices with their start and end apart: 7 -> 7, of which waited for: 4 -> 2; matrix products, arithmetic and copies ran while one was open for 8% -> 13% of each run, Pallas kernels for 0% -> 0%
where the time goes in v7:
time: 208 us; the launch traced here: 207 us
  waiting for transfers between devices  111 us (53%)
  starting transfers between devices  37.5 us (18%)
  local copies, waits for them, and re-layouts  33.2 us (16%)
  matrix products  20.8 us (10%)
  other arithmetic  2.84 us (1%)
    all_to_all x1, waiting for transfers between devices, body(): lax.all_to_all(outgoing, 'zs', split_axis=0, concat_axis=0, tiled=True)  103 us
    ppermute x6, starting transfers between devices, shifted(): return lax.ppermute(x, axis, pairs)  21.2 us
    all_to_all x1, starting transfers between devices, body(): lax.all_to_all(outgoing, 'zs', split_axis=0, concat_axis=0, tiled=True)  16.3 us
    slice x1, matrix products, body(): summed = summed[:, :CELLS // 128]  15.7 us
    transpose x3, local copies, waits for them, and re-layouts, to_xzy(): u = u.reshape(YBLOCKS, CX, rows, lanes, BLK).transpose(1, 4, 0, 2, 3)  9.81 us
    reshape x2, local copies, waits for them, and re-layouts, to_xzy(): u = u.reshape(YBLOCKS, CX, rows, lanes, BLK).transpose(1, 4, 0, 2, 3)  7.9 us
    ppermute x6, waiting for transfers between devices, shifted(): return lax.ppermute(x, axis, pairs)  7.84 us
    ppermute x2, local copies, waits for them, and re-layouts, shifted(): return lax.ppermute(x, axis, pairs)  4.76 us
  transfers between devices with their start and end apart: 7, of which 2 were waited for; matrix products, arithmetic and copies ran while one was open for 13% of the time, Pallas kernels for 0%

profile of v7, /device:TPU:7, one launch (start us, length us, event | category | flops | bytes accessed | tf_op | source)
XLA Modules:
  0.0 206.6 jit_solution(1032149794019637903)
XLA Ops:
  0.6 0.0 copy-start
  0.6 0.8 fusion.31
  1.5 0.1 select_reduce_fusion
  1.6 0.7 copy-done
  2.2 0.7 fusion.6
  2.9 0.1 broadcast_in_dim.29
  3.0 0.2 pad_maximum_fusion
  3.2 2.2 %copy.29 = bf16[32,272,128]{2,1,0:T(8,128)(2,1)} copy(bf16[32,272,128]{2,0,1:T(8,128)(2,1)S(1)} %pad_maximum_fusion) | data formatting | bytes 4456448 | tf_op jit(solution)/shard_map/concatenate | solution.py:44
  5.5 16.3 %all-to-all-start = ((bf16[32,272,128]{2,1,0:T(8,128)(2,1)}), bf16[32,272,128]{2,1,0:T(8,128)(2,1)}, u32[]{:S(2)}, u32[]{:S(2)}) async-start(bf16[32,272,128]{2,1,0:T(8,128)(2,1)} %copy.29), calls=%async_computation | async-start | bytes 4456448 | tf_op jit(solution)/shard_map/all_to_all | solution.py:45
  21.8 0.1 multiply_reduce_fusion
  21.9 0.1 divide_convert_fusion
  22.0 0.1 pad_slice_fusion.1
  22.1 103.4 %all-to-all-done = bf16[32,272,128]{2,1,0:T(8,128)(2,1)} async-done(((bf16[32,272,128]{2,1,0:T(8,128)(2,1)}), bf16[32,272,128]{2,1,0:T(8,128)(2,1)}, u32[]{:S(2)}, u32[]{:S(2)}) %all-to-all-start) | async-done | bytes 2228256 | tf_op jit(solution)/shard_map/all_to_all | solution.py:45
  125.5 1.5 fusion.17
  127.0 15.7 %fusion.32 = (bf16[8,256,128]{2,0,1:T(8,128)(2,1)S(1)}, f32[8,256,128]{2,0,1:T(8,128)}) fusion(bf16[32,272,128]{2,1,0:T(8,128)(2,1)} %all-to-all-done, s32[32]{0:T(128)S(1)} %fusion.17, s32[8]{0:T(128)S(1)} %fusion.29), kind=kOutput, calls=%fused_computation.67 | convolution fusion | flops 17039616 | bytes 3801248 | tf_op jit(solution)/shard_map/slice | solution.py:51
  142.7 0.9 copy.34
  143.6 3.2 %collective-permute-start = (bf16[4,64,8,128]{3,2,1,0:T(8,128)(2,1)}, bf16[4,64,8,128]{3,2,1,0:T(8,128)(2,1)}, u32[]{:S(2)}, u32[]{:S(2)}) collective-permute-start(bf16[4,64,8,128]{3,2,1,0:T(8,128)(2,1)} %bitcast.7), channel_id=1, source_target_pairs={{0,32},{32,64},{64,96},{96,128},{128,160},{160,192},{192,224},{224... | collective-permute-start | bytes 1572872 | tf_op jit(solution)/shard_map/ppermute | solution.py:18
  146.8 4.2 %collective-permute-start.1 = (bf16[4,64,8,128]{3,2,1,0:T(8,128)(2,1)}, bf16[4,64,8,128]{3,2,1,0:T(8,128)(2,1)}, u32[]{:S(2)}, u32[]{:S(2)}) collective-permute-start(bf16[4,64,8,128]{3,2,1,0:T(8,128)(2,1)} %bitcast.7), channel_id=1, source_target_pairs={{32,0},{64,32},{96,64},{128,96},{160,128},{192,160},{224,192},{256... | collective-permute-start | bytes 1572872 | tf_op jit(solution)/shard_map/ppermute | solution.py:18
  151.1 0.2 reshape.79
  151.3 0.1 copy.45
  151.3 0.3 reshape.84
  151.7 1.4 copy.31
  153.1 3.2 %reshape.77 = f32[4,64,8,4,32]{4,3,2,1,0:T(4,128)} reshape(f32[8,256,128]{2,1,0:T(8,128)S(1)} %copy.31) | data formatting | bytes 2097152 | tf_op jit(solution)/shard_map/reshape | solution.py:58
  156.3 4.7 %copy.32 = bf16[4,64,8,4,32]{1,2,3,0,4:T(8,128)(2,1)S(1)} copy(f32[4,64,8,4,32]{4,3,2,1,0:T(4,128)} %reshape.77) | data formatting | bytes 1572864 | tf_op jit(solution)/shard_map/reshape | solution.py:58
  161.0 0.5 copy.37
  161.6 0.5 fusion.14
  162.1 2.4 %copy.35 = bf16[4,64,8,128]{1,3,2,0:T(8,128)(2,1)} copy(bf16[4,64,8,128]{3,2,1,0:T(8,128)(2,1)} %collective-permute-done) | data formatting | bytes 1048576 | tf_op jit(solution)/shard_map/ppermute | solution.py:18
  164.5 2.7 %copy.36 = bf16[64,32,4,8,4]{0,4,3,2,1:T(4,128)(2,1)} copy(bf16[64,32,4,8,4]{0,1,4,3,2:T(8,128)(2,1)} %bitcast.83) | data formatting | bytes 1048576 | tf_op jit(solution)/shard_map/transpose | solution.py:58
  167.2 2.4 %copy.38 = bf16[4,64,8,128]{1,3,2,0:T(8,128)(2,1)} copy(bf16[4,64,8,128]{3,2,1,0:T(8,128)(2,1)} %collective-permute-done.1) | data formatting | bytes 1048576 | tf_op jit(solution)/shard_map/ppermute | solution.py:18
  169.6 1.9 copy.39
  171.4 0.5 convolution_add_fusion.1
  171.9 0.5 fusion.12
  172.4 0.1 copy.44
  172.5 0.3 convolution_convert_fusion
  172.8 1.3 collective-permute-start.5
  174.2 0.1 tile.32
  174.3 0.1 reshape.85
  174.4 5.2 %copy.41 = f32[4,64,8,4,32]{1,4,3,2,0:T(8,128)} copy(f32[4,64,8,4,32]{4,3,2,1,0:T(4,128)} %reshape.77) | data formatting | bytes 2097152 | tf_op jit(solution)/shard_map/transpose | solution.py:58
  179.6 3.9 %copy.40 = f32[64,32,128]{2,1,0:T(8,128)} copy(f32[64,32,128]{0,1,2:T(8,128)} %bitcast.78) | data formatting | bytes 2097152
  183.5 4.0 %collective-permute-start.4 = (bf16[64,32,128]{2,1,0:T(8,128)(2,1)S(1)}, bf16[64,32,128]{2,1,0:T(8,128)(2,1)S(1)}, u32[]{:S(2)}, u32[]{:S(2)}) collective-permute-start(bf16[64,32,128]{2,1,0:T(8,128)(2,1)S(1)} %convolution_convert_fusion), channel_id=1, source_target_pairs={{0,2},{1,3},{2,4},{3,5},{4,6},{5,7},{6,8},{7,9},{8,10},{9,11},{10,... | collective-permute-start | bytes 1572872 | tf_op jit(solution)/shard_map/ppermute | solution.py:18
  187.5 6.6 %collective-permute-start.2 = (bf16[64,32,128]{2,1,0:T(8,128)(2,1)S(1)}, bf16[64,32,128]{2,1,0:T(8,128)(2,1)S(1)}, u32[]{:S(2)}, u32[]{:S(2)}) collective-permute-start(bf16[64,32,128]{2,1,0:T(8,128)(2,1)S(1)} %convolution_convert_fusion), channel_id=1, source_target_pairs={{0,1},{1,2},{2,3},{3,4},{4,5},{5,6},{6,7},{7,8},{8,9},{9,10},{10,1... | collective-permute-start | bytes 1572872 | tf_op jit(solution)/shard_map/ppermute | solution.py:18
  194.1 1.9 collective-permute-start.3
  196.1 0.4 fusion.22
  196.4 0.3 fusion.20
  196.7 0.3 fusion.21
  197.0 7.8 %collective-permute-done.2 = bf16[64,32,128]{2,1,0:T(8,128)(2,1)S(1)} collective-permute-done((bf16[64,32,128]{2,1,0:T(8,128)(2,1)S(1)}, bf16[64,32,128]{2,1,0:T(8,128)(2,1)S(1)}, u32[]{:S(2)}, u32[]{:S(2)}) %collective-permute-start.2) | collective-permute-done | bytes 524320 | tf_op jit(solution)/shard_map/ppermute | solution.py:18
  204.8 0.3 convolution_add_fusion.3
  205.2 1.4 fusion.11
  (22 shorter events, 0.2 us)
Async XLA Ops:
  0.6 1.6 copy-start
  5.5 16.3 %copy-start.2 = (f32[3,129]{1,0:T(4,128)S(1)}, f32[3,129]{1,0:T(4,128)}, u32[]{:S(2)}) copy-start(f32[3,129]{1,0:T(4,128)} %param.5) | copy-start | bytes 4648
  5.5 120.1 %all-to-all-start = ((bf16[32,272,128]{2,1,0:T(8,128)(2,1)}), bf16[32,272,128]{2,1,0:T(8,128)(2,1)}, u32[]{:S(2)}, u32[]{:S(2)}) async-start(bf16[32,272,128]{2,1,0:T(8,128)(2,1)} %copy.29), calls=%async_computation | async-start | bytes 4456448 | tf_op jit(solution)/shard_map/all_to_all | solution.py:45
  143.6 18.4 %collective-permute-start = (bf16[4,64,8,128]{3,2,1,0:T(8,128)(2,1)}, bf16[4,64,8,128]{3,2,1,0:T(8,128)(2,1)}, u32[]{:S(2)}, u32[]{:S(2)}) collective-permute-start(bf16[4,64,8,128]{3,2,1,0:T(8,128)(2,1)} %bitcast.7), channel_id=1, source_target_pairs={{0,32},{32,64},{64,96},{96,128},{128,160},{160,192},{192,224},{224... | collective-permute-start | bytes 1572872 | tf_op jit(solution)/shard_map/ppermute | solution.py:18
  146.8 20.4 %collective-permute-start.1 = (bf16[4,64,8,128]{3,2,1,0:T(8,128)(2,1)}, bf16[4,64,8,128]{3,2,1,0:T(8,128)(2,1)}, u32[]{:S(2)}, u32[]{:S(2)}) collective-permute-start(bf16[4,64,8,128]{3,2,1,0:T(8,128)(2,1)} %bitcast.7), channel_id=1, source_target_pairs={{32,0},{64,32},{96,64},{128,96},{160,128},{192,160},{224,192},{256... | collective-permute-start | bytes 1572872 | tf_op jit(solution)/shard_map/ppermute | solution.py:18
  169.6 1.9 copy-start.1
  172.8 23.6 %collective-permute-start.5 = (bf16[64,32,128]{2,1,0:T(8,128)(2,1)S(1)}, bf16[64,32,128]{2,1,0:T(8,128)(2,1)S(1)}, u32[]{:S(2)}, u32[]{:S(2)}) collective-permute-start(bf16[64,32,128]{2,1,0:T(8,128)(2,1)S(1)} %convolution_convert_fusion), channel_id=1, source_target_pairs={{2,0},{3,1},{4,2},{5,3},{6,4},{7,5},{8,6},{9,7},{10,8},{11,9},{12,... | collective-permute-start | bytes 1572872 | tf_op jit(solution)/shard_map/ppermute | solution.py:18
  183.5 13.2 %collective-permute-start.4 = (bf16[64,32,128]{2,1,0:T(8,128)(2,1)S(1)}, bf16[64,32,128]{2,1,0:T(8,128)(2,1)S(1)}, u32[]{:S(2)}, u32[]{:S(2)}) collective-permute-start(bf16[64,32,128]{2,1,0:T(8,128)(2,1)S(1)} %convolution_convert_fusion), channel_id=1, source_target_pairs={{0,2},{1,3},{2,4},{3,5},{4,6},{5,7},{6,8},{7,9},{8,10},{9,11},{10,... | collective-permute-start | bytes 1572872 | tf_op jit(solution)/shard_map/ppermute | solution.py:18
  187.5 17.3 %collective-permute-start.2 = (bf16[64,32,128]{2,1,0:T(8,128)(2,1)S(1)}, bf16[64,32,128]{2,1,0:T(8,128)(2,1)S(1)}, u32[]{:S(2)}, u32[]{:S(2)}) collective-permute-start(bf16[64,32,128]{2,1,0:T(8,128)(2,1)S(1)} %convolution_convert_fusion), channel_id=1, source_target_pairs={{0,1},{1,2},{2,3},{3,4},{4,5},{5,6},{6,7},{7,8},{8,9},{9,10},{10,1... | collective-permute-start | bytes 1572872 | tf_op jit(solution)/shard_map/ppermute | solution.py:18
  194.1 11.0 %collective-permute-start.3 = (bf16[64,32,128]{2,1,0:T(8,128)(2,1)S(1)}, bf16[64,32,128]{2,1,0:T(8,128)(2,1)S(1)}, u32[]{:S(2)}, u32[]{:S(2)}) collective-permute-start(bf16[64,32,128]{2,1,0:T(8,128)(2,1)S(1)} %convolution_convert_fusion), channel_id=1, source_target_pairs={{1,0},{2,1},{3,2},{4,3},{5,4},{6,5},{7,6},{8,7},{9,8},{10,9},{11,1... | collective-permute-start | bytes 1572872 | tf_op jit(solution)/shard_map/ppermute | solution.py:18

commit v8 on v4

--- a/solution.py
+++ b/solution.py
@@ -63,10 +63,26 @@
     along_y = jnp.einsum(
         "ab,xzb->xza", y_matrix, along_x, preferred_element_type=jnp.float32
     ).astype(jnp.bfloat16)
-    reach_slabs = REACH // CZ
-    halo_lo = [shifted(along_y, "zs", s) for s in range(reach_slabs, 0, -1)]
-    halo_hi = [shifted(along_y, "zs", -s) for s in range(1, reach_slabs + 1)]
-    extended = jnp.concatenate(halo_lo + [along_y] + halo_hi, axis=1)
+    zs_count = lax.axis_size("zs")
+
+    def pairs(step, parity):
+        return [
+            (i, i + step)
+            for i in range(zs_count)
+            if 0 <= i + step < zs_count and (parity is None or (i + step) % 2 == parity)
+        ]
+
+    prev1 = lax.ppermute(along_y, "zs", pairs(1, None))
+    next1 = lax.ppermute(along_y, "zs", pairs(-1, None))
+    prev2_even = lax.ppermute(along_y, "zs", pairs(2, 0))
+    next2_odd = lax.ppermute(along_y, "zs", pairs(-2, 1))
+    even = lax.axis_index("zs") % 2 == 0
+    relayed = lax.ppermute(
+        jnp.where(even, prev1, next1), "zs", [(i, i ^ 1) for i in range(zs_count)]
+    )
+    prev2 = jnp.where(even, prev2_even, relayed)
+    next2 = jnp.where(even, relayed, next2_odd)
+    extended = jnp.concatenate([prev2, prev1, along_y, next1, next2], axis=1)
     z_matrix = band_matrix(kernel[2], CZ, CZ + 2 * REACH, 0)
     smoothed = jnp.einsum(
         "zk,xky->xzy", z_matrix, extended, preferred_element_type=jnp.float32

time: 196 us -> 194 us (0.990)
  the two profiles are of different devices: /device:TPU:24 before, /device:TPU:7 now
where the time goes in v8:
time: 194 us; the launch traced here: 192 us
  waiting for transfers between devices  126 us (65%)
  starting transfers between devices  34.3 us (18%)
  local copies, waits for them, and re-layouts  18.6 us (10%)
  other arithmetic  7.52 us (4%)
  matrix products  4.35 us (2%)
    all_to_all x1, waiting for transfers between devices, body(): lax.all_to_all(outgoing, 'zs', split_axis=0, concat_axis=0, tiled=True)  104 us
    all_to_all x1, starting transfers between devices, body(): lax.all_to_all(outgoing, 'zs', split_axis=0, concat_axis=0, tiled=True)  16.1 us
    ppermute x2, waiting for transfers between devices, shifted(): return lax.ppermute(x, axis, pairs)  9.57 us
    ppermute x2, starting transfers between devices, shifted(): return lax.ppermute(x, axis, pairs)  7.38 us
    ppermute x1, waiting for transfers between devices, body(): next2_odd = lax.ppermute(along_y, 'zs', pairs(-2, 1))  6.42 us
    transpose x1, local copies, waits for them, and re-layouts, body(): assembled.reshape(2, YBLOCKS, BLK, BLK, BLK).transpose(0, 2, 4, 1, 3)  5.24 us
    ppermute x1, waiting for transfers between devices, body(): next1 = lax.ppermute(along_y, 'zs', pairs(-1, None))  4.4 us
  transfers between devices with their start and end apart: 8, of which 7 were waited for; matrix products, arithmetic and copies ran while one was open for 2% of the time, Pallas kernels for 0%

profile of v8, /device:TPU:7, one launch (start us, length us, event | category | flops | bytes accessed | tf_op | source)
XLA Modules:
  0.0 192.0 jit_solution(13723321675353750011)
XLA Ops:
  0.6 0.8 fusion.22
  1.5 0.1 select_reduce_fusion
  1.6 0.7 copy-done
  2.2 0.7 fusion.5
  2.9 0.1 broadcast_in_dim.29
  3.0 0.2 pad_maximum_fusion
  3.2 2.2 %copy.12 = bf16[32,272,128]{2,1,0:T(8,128)(2,1)} copy(bf16[32,272,128]{2,0,1:T(8,128)(2,1)S(1)} %pad_maximum_fusion) | data formatting | bytes 4456448 | tf_op jit(solution)/shard_map/concatenate | solution.py:44
  5.5 16.1 %all-to-all-start = ((bf16[32,272,128]{2,1,0:T(8,128)(2,1)}), bf16[32,272,128]{2,1,0:T(8,128)(2,1)}, u32[]{:S(2)}, u32[]{:S(2)}) async-start(bf16[32,272,128]{2,1,0:T(8,128)(2,1)} %copy.12), calls=%async_computation | async-start | bytes 4456448 | tf_op jit(solution)/shard_map/all_to_all | solution.py:45
  21.6 0.1 multiply_reduce_fusion
  21.7 0.1 divide_convert_fusion
  21.8 103.7 %all-to-all-done = bf16[32,272,128]{2,1,0:T(8,128)(2,1)} async-done(((bf16[32,272,128]{2,1,0:T(8,128)(2,1)}), bf16[32,272,128]{2,1,0:T(8,128)(2,1)}, u32[]{:S(2)}, u32[]{:S(2)}) %all-to-all-start) | async-done | bytes 2228256 | tf_op jit(solution)/shard_map/all_to_all | solution.py:45
  125.5 1.7 slice.63
  127.3 1.5 fusion.14
  128.8 1.2 fusion.3
  130.0 0.2 copy.14
  130.2 2.4 %reshape.46 = f32[2,4,32,32,32]{4,3,2,1,0:T(8,128)} reshape(f32[8,256,128]{2,1,0:T(8,128)S(1)} %copy.14) | data formatting | bytes 2097152 | tf_op jit(solution)/shard_map/reshape | solution.py:51
  132.6 5.2 %copy.15 = f32[2,32,32,4,32]{4,3,2,1,0:T(4,128)} copy(f32[2,32,32,4,32]{2,4,1,3,0:T(8,128)} %bitcast.48) | data formatting | bytes 2097152 | tf_op jit(solution)/shard_map/transpose | solution.py:51
  137.9 3.7 %reshape.47 = f32[64,32,128]{2,1,0:T(8,128)S(1)} reshape(f32[2,32,32,4,32]{4,3,2,1,0:T(4,128)} %copy.15) | data formatting | bytes 2097152 | tf_op jit(solution)/shard_map/reshape | solution.py:52
  141.6 1.0 convert_element_type.44
  142.6 3.2 %collective-permute-start = (bf16[64,32,128]{2,1,0:T(8,128)(2,1)}, bf16[64,32,128]{2,1,0:T(8,128)(2,1)}, u32[]{:S(2)}, u32[]{:S(2)}) collective-permute-start(bf16[64,32,128]{2,1,0:T(8,128)(2,1)} %convert_element_type.44), channel_id=1, source_target_pairs={{0,32},{32,64},{64,96},{96,128},{128,160},{160,192},{192,224},{224... | collective-permute-start | bytes 1572872 | tf_op jit(solution)/shard_map/ppermute | solution.py:18
  145.8 4.2 %collective-permute-start.1 = (bf16[64,32,128]{2,1,0:T(8,128)(2,1)}, bf16[64,32,128]{2,1,0:T(8,128)(2,1)}, u32[]{:S(2)}, u32[]{:S(2)}) collective-permute-start(bf16[64,32,128]{2,1,0:T(8,128)(2,1)} %convert_element_type.44), channel_id=1, source_target_pairs={{32,0},{64,32},{96,64},{128,96},{160,128},{192,160},{224,192},{256... | collective-permute-start | bytes 1572872 | tf_op jit(solution)/shard_map/ppermute | solution.py:18
  150.0 0.2 reshape.48
  150.2 0.1 pad_slice_fusion.1
  150.4 0.3 reshape.51
  150.7 8.7 %collective-permute-done = bf16[64,32,128]{2,1,0:T(8,128)(2,1)} collective-permute-done((bf16[64,32,128]{2,1,0:T(8,128)(2,1)}, bf16[64,32,128]{2,1,0:T(8,128)(2,1)}, u32[]{:S(2)}, u32[]{:S(2)}) %collective-permute-start) | collective-permute-done | bytes 524320 | tf_op jit(solution)/shard_map/ppermute | solution.py:18
  159.4 0.9 collective-permute-done.1
  160.3 1.5 pad_maximum_fusion.1
  161.8 0.6 fusion.10
  162.5 0.1 copy.20
  162.6 0.3 convolution_convert_fusion.1
  162.9 3.2 %collective-permute-start.3 = (bf16[64,32,128]{2,1,0:T(8,128)(2,1)S(1)}, bf16[64,32,128]{2,1,0:T(8,128)(2,1)}, u32[]{:S(2)}, u32[]{:S(2)}) collective-permute-start(bf16[64,32,128]{2,1,0:T(8,128)(2,1)S(1)} %convolution_convert_fusion.1), channel_id=1, source_target_pairs={{0,1},{1,2},{2,3},{3,4},{4,5},{5,6},{6,7},{7,8},{8,9},{9,10},{10,1... | collective-permute-start | bytes 1572872 | tf_op jit(solution)/shard_map/ppermute | solution.py:75
  166.0 3.0 %collective-permute-start.4 = (bf16[64,32,128]{2,1,0:T(8,128)(2,1)S(1)}, bf16[64,32,128]{2,1,0:T(8,128)(2,1)S(1)}, u32[]{:S(2)}, u32[]{:S(2)}) collective-permute-start(bf16[64,32,128]{2,1,0:T(8,128)(2,1)S(1)} %convolution_convert_fusion.1), channel_id=1, source_target_pairs={{1,0},{2,1},{3,2},{4,3},{5,4},{6,5},{7,6},{8,7},{9,8},{10,9},{11,1... | collective-permute-start | bytes 1572872 | tf_op jit(solution)/shard_map/ppermute | solution.py:76
  169.0 1.5 collective-permute-start.2
  170.5 1.6 collective-permute-done.3
  172.1 4.4 %collective-permute-done.4 = bf16[64,32,128]{2,1,0:T(8,128)(2,1)S(1)} collective-permute-done((bf16[64,32,128]{2,1,0:T(8,128)(2,1)S(1)}, bf16[64,32,128]{2,1,0:T(8,128)(2,1)S(1)}, u32[]{:S(2)}, u32[]{:S(2)}) %collective-permute-start.4) | collective-permute-done | bytes 524320 | tf_op jit(solution)/shard_map/ppermute | solution.py:76
  176.5 0.9 broadcast_select_fusion
  177.4 1.9 collective-permute-start.5
  179.3 0.1 tile.32
  179.4 0.1 reshape.52
  179.6 1.3 collective-permute-start.6
  180.9 0.6 collective-permute-done.5
  181.5 1.2 select_dynamic-update-slice_fusion.1
  182.7 1.1 constant_dynamic-update-slice_fusion.2
  183.8 0.1 constant_dynamic-update-slice_fusion.1
  183.9 0.1 constant_dynamic-update-slice_fusion
  184.0 6.4 %collective-permute-done.6 = bf16[64,32,128]{2,1,0:T(8,128)(2,1)S(1)} collective-permute-done((bf16[64,32,128]{2,1,0:T(8,128)(2,1)S(1)}, bf16[64,32,128]{2,1,0:T(8,128)(2,1)S(1)}, u32[]{:S(2)}, u32[]{:S(2)}) %collective-permute-start.6) | collective-permute-done | bytes 524320 | tf_op jit(solution)/shard_map/ppermute | solution.py:78
  190.4 0.2 select_dynamic-update-slice_fusion
  190.6 1.5 convolution_bitcast_fusion
  (19 shorter events, 0.2 us)
Async XLA Ops:
  0.6 1.6 copy-start
  5.5 16.1 %copy-start.2 = (f32[3,129]{1,0:T(4,128)S(1)}, f32[3,129]{1,0:T(4,128)}, u32[]{:S(2)}) copy-start(f32[3,129]{1,0:T(4,128)} %param.5) | copy-start | bytes 4648
  5.5 120.1 %all-to-all-start = ((bf16[32,272,128]{2,1,0:T(8,128)(2,1)}), bf16[32,272,128]{2,1,0:T(8,128)(2,1)}, u32[]{:S(2)}, u32[]{:S(2)}) async-start(bf16[32,272,128]{2,1,0:T(8,128)(2,1)} %copy.12), calls=%async_computation | async-start | bytes 4456448 | tf_op jit(solution)/shard_map/all_to_all | solution.py:45
  141.6 20.2 %copy-start.1 = (f32[64,32,128]{2,1,0:T(8,128)}, f32[64,32,128]{2,1,0:T(8,128)S(1)}, u32[]{:S(2)}) copy-start(f32[64,32,128]{2,1,0:T(8,128)S(1)} %reshape.47) | copy-start | bytes 3145732
  142.6 16.8 %collective-permute-start = (bf16[64,32,128]{2,1,0:T(8,128)(2,1)}, bf16[64,32,128]{2,1,0:T(8,128)(2,1)}, u32[]{:S(2)}, u32[]{:S(2)}) collective-permute-start(bf16[64,32,128]{2,1,0:T(8,128)(2,1)} %convert_element_type.44), channel_id=1, source_target_pairs={{0,32},{32,64},{64,96},{96,128},{128,160},{160,192},{192,224},{224... | collective-permute-start | bytes 1572872 | tf_op jit(solution)/shard_map/ppermute | solution.py:18
  145.8 14.5 %collective-permute-start.1 = (bf16[64,32,128]{2,1,0:T(8,128)(2,1)}, bf16[64,32,128]{2,1,0:T(8,128)(2,1)}, u32[]{:S(2)}, u32[]{:S(2)}) collective-permute-start(bf16[64,32,128]{2,1,0:T(8,128)(2,1)} %convert_element_type.44), channel_id=1, source_target_pairs={{32,0},{64,32},{96,64},{128,96},{160,128},{192,160},{224,192},{256... | collective-permute-start | bytes 1572872 | tf_op jit(solution)/shard_map/ppermute | solution.py:18
  162.9 9.3 %collective-permute-start.3 = (bf16[64,32,128]{2,1,0:T(8,128)(2,1)S(1)}, bf16[64,32,128]{2,1,0:T(8,128)(2,1)}, u32[]{:S(2)}, u32[]{:S(2)}) collective-permute-start(bf16[64,32,128]{2,1,0:T(8,128)(2,1)S(1)} %convolution_convert_fusion.1), channel_id=1, source_target_pairs={{0,1},{1,2},{2,3},{3,4},{4,5},{5,6},{6,7},{7,8},{8,9},{9,10},{10,1... | collective-permute-start | bytes 1572872 | tf_op jit(solution)/shard_map/ppermute | solution.py:75
  166.0 10.5 %collective-permute-start.4 = (bf16[64,32,128]{2,1,0:T(8,128)(2,1)S(1)}, bf16[64,32,128]{2,1,0:T(8,128)(2,1)S(1)}, u32[]{:S(2)}, u32[]{:S(2)}) collective-permute-start(bf16[64,32,128]{2,1,0:T(8,128)(2,1)S(1)} %convolution_convert_fusion.1), channel_id=1, source_target_pairs={{1,0},{2,1},{3,2},{4,3},{5,4},{6,5},{7,6},{8,7},{9,8},{10,9},{11,1... | collective-permute-start | bytes 1572872 | tf_op jit(solution)/shard_map/ppermute | solution.py:76
  169.0 11.9 %collective-permute-start.2 = (bf16[64,32,128]{2,1,0:T(8,128)(2,1)S(1)}, bf16[64,32,128]{2,1,0:T(8,128)(2,1)}, u32[]{:S(2)}, u32[]{:S(2)}) collective-permute-start(bf16[64,32,128]{2,1,0:T(8,128)(2,1)S(1)} %convolution_convert_fusion.1), channel_id=1, source_target_pairs={{0,2},{2,4},{4,6},{6,8},{8,10},{10,12},{12,14},{14,16},{16,18},{18... | collective-permute-start | bytes 1572872 | tf_op jit(solution)/shard_map/ppermute | solution.py:77
  177.4 4.1 %collective-permute-start.5 = (bf16[64,32,128]{2,1,0:T(8,128)(2,1)}, bf16[64,32,128]{2,1,0:T(8,128)(2,1)}, u32[]{:S(2)}, u32[]{:S(2)}) collective-permute-start(bf16[64,32,128]{2,1,0:T(8,128)(2,1)} %broadcast_select_fusion), channel_id=1, source_target_pairs={{0,1},{1,0},{2,3},{3,2},{4,5},{5,4},{6,7},{7,6},{8,9},{9,8},{10,11... | collective-permute-start | bytes 1572872 | tf_op jit(solution)/shard_map/ppermute | solution.py:80
  179.6 10.8 %collective-permute-start.6 = (bf16[64,32,128]{2,1,0:T(8,128)(2,1)S(1)}, bf16[64,32,128]{2,1,0:T(8,128)(2,1)S(1)}, u32[]{:S(2)}, u32[]{:S(2)}) collective-permute-start(bf16[64,32,128]{2,1,0:T(8,128)(2,1)S(1)} %convolution_convert_fusion.1), channel_id=1, source_target_pairs={{3,1},{5,3},{7,5},{9,7},{11,9},{13,11},{15,13},{17,15},{19,17},{21... | collective-permute-start | bytes 1572872 | tf_op jit(solution)/shard_map/ppermute | solution.py:78

commit v9 on v8

--- a/solution.py
+++ b/solution.py
@@ -82,10 +82,12 @@
     )
     prev2 = jnp.where(even, prev2_even, relayed)
     next2 = jnp.where(even, relayed, next2_odd)
-    extended = jnp.concatenate([prev2, prev1, along_y, next1, next2], axis=1)
     z_matrix = band_matrix(kernel[2], CZ, CZ + 2 * REACH, 0)
-    smoothed = jnp.einsum(
-        "zk,xky->xzy", z_matrix, extended, preferred_element_type=jnp.float32
+    smoothed = sum(
+        jnp.einsum(
+            "zk,xky->xzy", z_matrix[:, k * CZ : (k + 1) * CZ], slab, preferred_element_type=jnp.float32
+        )
+        for k, slab in ((2, along_y), (1, prev1), (3, next1), (0, prev2), (4, next2))
     )
     return (gradient, smoothed)
 

time: 194 us -> 188 us (0.969)
  waiting for transfers between devices: 126 us -> 121 us
  matrix products: 4.35 us -> 6.5 us
  other arithmetic: 7.52 us -> 5.38 us
    ppermute x1, waiting for transfers between devices: 6.42 us -> 0.01 us  [body(): next2_odd = lax.ppermute(along_y, 'zs', pairs(-2, 1))]
    ppermute x1, waiting for transfers between devices: 4.4 us -> 6.56 us  [body(): next1 = lax.ppermute(along_y, 'zs', pairs(-1, None))]
    dot_general x1 -> x5, matrix products: 1.48 us -> 3.63 us  [body(): jnp.einsum('zk,xky->xzy', z_matrix[:, k * CZ:(k + 1) * CZ], slab, preferr...]
  transfers between devices with their start and end apart: 8 -> 8, of which waited for: 7 -> 6; matrix products, arithmetic and copies ran while one was open for 2% -> 2% of each run, Pallas kernels for 0% -> 0%
where the time goes in v9:
time: 188 us; the launch traced here: 184 us
  waiting for transfers between devices  121 us (64%)
  starting transfers between devices  33.5 us (18%)
  local copies, waits for them, and re-layouts  17.4 us (9%)
  matrix products  6.5 us (3%)
  other arithmetic  5.38 us (3%)
    all_to_all x1, waiting for transfers between devices, body(): lax.all_to_all(outgoing, 'zs', split_axis=0, concat_axis=0, tiled=True)  104 us
    all_to_all x1, starting transfers between devices, body(): lax.all_to_all(outgoing, 'zs', split_axis=0, concat_axis=0, tiled=True)  16.1 us
    ppermute x2, waiting for transfers between devices, shifted(): return lax.ppermute(x, axis, pairs)  9.57 us
    ppermute x2, starting transfers between devices, shifted(): return lax.ppermute(x, axis, pairs)  7.38 us
    ppermute x1, waiting for transfers between devices, body(): next1 = lax.ppermute(along_y, 'zs', pairs(-1, None))  6.56 us
    transpose x1, local copies, waits for them, and re-layouts, body(): assembled.reshape(2, YBLOCKS, BLK, BLK, BLK).transpose(0, 2, 4, 1, 3)  5.24 us
  transfers between devices with their start and end apart: 8, of which 6 were waited for; matrix products, arithmetic and copies ran while one was open for 2% of the time, Pallas kernels for 0%

profile of v9, /device:TPU:7, one launch (start us, length us, event | category | flops | bytes accessed | tf_op | source)
XLA Modules:
  0.0 184.5 jit_solution(7611555180890272306)
XLA Ops:
  0.6 0.0 copy-start
  0.6 0.8 fusion.32
  1.5 0.1 select_reduce_fusion
  1.6 0.7 copy-done
  2.2 0.7 fusion.5
  2.9 0.1 broadcast_in_dim.29
  3.0 0.2 pad_maximum_fusion
  3.2 2.2 %copy.12 = bf16[32,272,128]{2,1,0:T(8,128)(2,1)} copy(bf16[32,272,128]{2,0,1:T(8,128)(2,1)S(1)} %pad_maximum_fusion) | data formatting | bytes 4456448 | tf_op jit(solution)/shard_map/concatenate | solution.py:44
  5.5 16.1 %all-to-all-start = ((bf16[32,272,128]{2,1,0:T(8,128)(2,1)}), bf16[32,272,128]{2,1,0:T(8,128)(2,1)}, u32[]{:S(2)}, u32[]{:S(2)}) async-start(bf16[32,272,128]{2,1,0:T(8,128)(2,1)} %copy.12), calls=%async_computation | async-start | bytes 4456448 | tf_op jit(solution)/shard_map/all_to_all | solution.py:45
  21.6 0.1 multiply_reduce_fusion
  21.7 0.1 divide_convert_fusion
  21.8 103.7 %all-to-all-done = bf16[32,272,128]{2,1,0:T(8,128)(2,1)} async-done(((bf16[32,272,128]{2,1,0:T(8,128)(2,1)}), bf16[32,272,128]{2,1,0:T(8,128)(2,1)}, u32[]{:S(2)}, u32[]{:S(2)}) %all-to-all-start) | async-done | bytes 2228256 | tf_op jit(solution)/shard_map/all_to_all | solution.py:45
  125.5 1.7 slice.85
  127.3 1.5 fusion.23
  128.8 1.2 fusion.3
  130.0 0.2 copy.14
  130.2 2.4 %reshape.46 = f32[2,4,32,32,32]{4,3,2,1,0:T(8,128)} reshape(f32[8,256,128]{2,1,0:T(8,128)S(1)} %copy.14) | data formatting | bytes 2097152 | tf_op jit(solution)/shard_map/reshape | solution.py:51
  132.6 5.2 %copy.15 = f32[2,32,32,4,32]{4,3,2,1,0:T(4,128)} copy(f32[2,32,32,4,32]{2,4,1,3,0:T(8,128)} %bitcast.62) | data formatting | bytes 2097152 | tf_op jit(solution)/shard_map/transpose | solution.py:51
  137.9 3.7 %reshape.47 = f32[64,32,128]{2,1,0:T(8,128)S(1)} reshape(f32[2,32,32,4,32]{4,3,2,1,0:T(4,128)} %copy.15) | data formatting | bytes 2097152 | tf_op jit(solution)/shard_map/reshape | solution.py:52
  141.6 1.0 convert_element_type.44
  142.6 3.2 %collective-permute-start = (bf16[64,32,128]{2,1,0:T(8,128)(2,1)}, bf16[64,32,128]{2,1,0:T(8,128)(2,1)}, u32[]{:S(2)}, u32[]{:S(2)}) collective-permute-start(bf16[64,32,128]{2,1,0:T(8,128)(2,1)} %convert_element_type.44), channel_id=1, source_target_pairs={{0,32},{32,64},{64,96},{96,128},{128,160},{160,192},{192,224},{224... | collective-permute-start | bytes 1572872 | tf_op jit(solution)/shard_map/ppermute | solution.py:18
  145.8 4.2 %collective-permute-start.1 = (bf16[64,32,128]{2,1,0:T(8,128)(2,1)}, bf16[64,32,128]{2,1,0:T(8,128)(2,1)}, u32[]{:S(2)}, u32[]{:S(2)}) collective-permute-start(bf16[64,32,128]{2,1,0:T(8,128)(2,1)} %convert_element_type.44), channel_id=1, source_target_pairs={{32,0},{64,32},{96,64},{128,96},{160,128},{192,160},{224,192},{256... | collective-permute-start | bytes 1572872 | tf_op jit(solution)/shard_map/ppermute | solution.py:18
  150.0 0.2 reshape.48
  150.2 0.1 pad_slice_fusion.1
  150.3 0.1 copy.21
  150.4 0.3 reshape.51
  150.7 8.7 %collective-permute-done = bf16[64,32,128]{2,1,0:T(8,128)(2,1)} collective-permute-done((bf16[64,32,128]{2,1,0:T(8,128)(2,1)}, bf16[64,32,128]{2,1,0:T(8,128)(2,1)}, u32[]{:S(2)}, u32[]{:S(2)}) %collective-permute-start) | collective-permute-done | bytes 524320 | tf_op jit(solution)/shard_map/ppermute | solution.py:18
  159.4 0.9 collective-permute-done.1
  160.3 1.5 pad_maximum_fusion.1
  161.8 0.6 fusion.13
  162.5 0.1 copy.20
  162.6 0.3 convolution_convert_fusion.1
  162.9 3.2 %collective-permute-start.2 = (bf16[64,32,128]{2,1,0:T(8,128)(2,1)S(1)}, bf16[64,32,128]{2,1,0:T(8,128)(2,1)}, u32[]{:S(2)}, u32[]{:S(2)}) collective-permute-start(bf16[64,32,128]{2,1,0:T(8,128)(2,1)S(1)} %convolution_convert_fusion.1), channel_id=1, source_target_pairs={{0,1},{1,2},{2,3},{3,4},{4,5},{5,6},{6,7},{7,8},{8,9},{9,10},{10,1... | collective-permute-start | bytes 1572872 | tf_op jit(solution)/shard_map/ppermute | solution.py:75
  166.0 3.0 %collective-permute-start.3 = (bf16[64,32,128]{2,1,0:T(8,128)(2,1)S(1)}, bf16[64,32,128]{2,1,0:T(8,128)(2,1)S(1)}, u32[]{:S(2)}, u32[]{:S(2)}) collective-permute-start(bf16[64,32,128]{2,1,0:T(8,128)(2,1)S(1)} %convolution_convert_fusion.1), channel_id=1, source_target_pairs={{1,0},{2,1},{3,2},{4,3},{5,4},{6,5},{7,6},{8,7},{9,8},{10,9},{11,1... | collective-permute-start | bytes 1572872 | tf_op jit(solution)/shard_map/ppermute | solution.py:76
  169.0 0.1 tile.32
  169.1 0.1 reshape.52
  169.3 0.7 collective-permute-start.4
  170.0 1.3 collective-permute-start.6
  171.3 0.8 collective-permute-done.2
  172.1 6.6 %collective-permute-done.3 = bf16[64,32,128]{2,1,0:T(8,128)(2,1)S(1)} collective-permute-done((bf16[64,32,128]{2,1,0:T(8,128)(2,1)S(1)}, bf16[64,32,128]{2,1,0:T(8,128)(2,1)S(1)}, u32[]{:S(2)}, u32[]{:S(2)}) %collective-permute-start.3) | collective-permute-done | bytes 524320 | tf_op jit(solution)/shard_map/ppermute | solution.py:76
  178.7 0.1 broadcast_select_fusion
  178.8 1.9 %collective-permute-start.5 = (bf16[64,32,128]{2,1,0:T(8,128)(2,1)S(1)}, bf16[64,32,128]{2,1,0:T(8,128)(2,1)S(1)}, u32[]{:S(2)}, u32[]{:S(2)}) collective-permute-start(bf16[64,32,128]{2,1,0:T(8,128)(2,1)S(1)} %broadcast_select_fusion), channel_id=1, source_target_pairs={{0,1},{1,0},{2,3},{3,2},{4,5},{5,4},{6,7},{7,6},{8,9},{9,8},{10,11... | collective-permute-start | bytes 1572872 | tf_op jit(solution)/shard_map/ppermute | solution.py:80
  180.7 0.3 fusion.26
  181.0 1.4 convolution_add_fusion.1
  182.4 0.1 collective-permute-done.5
  182.6 0.3 fusion.18
  182.9 0.3 fusion.16
  183.2 1.3 fusion.12
  (18 shorter events, 0.2 us)
Async XLA Ops:
  0.6 1.6 copy-start
  5.5 16.1 %copy-start.2 = (f32[3,129]{1,0:T(4,128)S(1)}, f32[3,129]{1,0:T(4,128)}, u32[]{:S(2)}) copy-start(f32[3,129]{1,0:T(4,128)} %param.5) | copy-start | bytes 4648
  5.5 120.1 %all-to-all-start = ((bf16[32,272,128]{2,1,0:T(8,128)(2,1)}), bf16[32,272,128]{2,1,0:T(8,128)(2,1)}, u32[]{:S(2)}, u32[]{:S(2)}) async-start(bf16[32,272,128]{2,1,0:T(8,128)(2,1)} %copy.12), calls=%async_computation | async-start | bytes 4456448 | tf_op jit(solution)/shard_map/all_to_all | solution.py:45
  141.6 20.2 %copy-start.1 = (f32[64,32,128]{2,1,0:T(8,128)}, f32[64,32,128]{2,1,0:T(8,128)S(1)}, u32[]{:S(2)}) copy-start(f32[64,32,128]{2,1,0:T(8,128)S(1)} %reshape.47) | copy-start | bytes 3145732
  142.6 16.8 %collective-permute-start = (bf16[64,32,128]{2,1,0:T(8,128)(2,1)}, bf16[64,32,128]{2,1,0:T(8,128)(2,1)}, u32[]{:S(2)}, u32[]{:S(2)}) collective-permute-start(bf16[64,32,128]{2,1,0:T(8,128)(2,1)} %convert_element_type.44), channel_id=1, source_target_pairs={{0,32},{32,64},{64,96},{96,128},{128,160},{160,192},{192,224},{224... | collective-permute-start | bytes 1572872 | tf_op jit(solution)/shard_map/ppermute | solution.py:18
  145.8 14.5 %collective-permute-start.1 = (bf16[64,32,128]{2,1,0:T(8,128)(2,1)}, bf16[64,32,128]{2,1,0:T(8,128)(2,1)}, u32[]{:S(2)}, u32[]{:S(2)}) collective-permute-start(bf16[64,32,128]{2,1,0:T(8,128)(2,1)} %convert_element_type.44), channel_id=1, source_target_pairs={{32,0},{64,32},{96,64},{128,96},{160,128},{192,160},{224,192},{256... | collective-permute-start | bytes 1572872 | tf_op jit(solution)/shard_map/ppermute | solution.py:18
  162.9 9.3 %collective-permute-start.2 = (bf16[64,32,128]{2,1,0:T(8,128)(2,1)S(1)}, bf16[64,32,128]{2,1,0:T(8,128)(2,1)}, u32[]{:S(2)}, u32[]{:S(2)}) collective-permute-start(bf16[64,32,128]{2,1,0:T(8,128)(2,1)S(1)} %convolution_convert_fusion.1), channel_id=1, source_target_pairs={{0,1},{1,2},{2,3},{3,4},{4,5},{5,6},{6,7},{7,8},{8,9},{9,10},{10,1... | collective-permute-start | bytes 1572872 | tf_op jit(solution)/shard_map/ppermute | solution.py:75
  166.0 12.7 %collective-permute-start.3 = (bf16[64,32,128]{2,1,0:T(8,128)(2,1)S(1)}, bf16[64,32,128]{2,1,0:T(8,128)(2,1)S(1)}, u32[]{:S(2)}, u32[]{:S(2)}) collective-permute-start(bf16[64,32,128]{2,1,0:T(8,128)(2,1)S(1)} %convolution_convert_fusion.1), channel_id=1, source_target_pairs={{1,0},{2,1},{3,2},{4,3},{5,4},{6,5},{7,6},{8,7},{9,8},{10,9},{11,1... | collective-permute-start | bytes 1572872 | tf_op jit(solution)/shard_map/ppermute | solution.py:76
  169.3 13.2 %collective-permute-start.4 = (bf16[64,32,128]{2,1,0:T(8,128)(2,1)S(1)}, bf16[64,32,128]{2,1,0:T(8,128)(2,1)S(1)}, u32[]{:S(2)}, u32[]{:S(2)}) collective-permute-start(bf16[64,32,128]{2,1,0:T(8,128)(2,1)S(1)} %convolution_convert_fusion.1), channel_id=1, source_target_pairs={{0,2},{2,4},{4,6},{6,8},{8,10},{10,12},{12,14},{14,16},{16,18},{18... | collective-permute-start | bytes 1572872 | tf_op jit(solution)/shard_map/ppermute | solution.py:77
  170.0 12.9 %collective-permute-start.6 = (bf16[64,32,128]{2,1,0:T(8,128)(2,1)S(1)}, bf16[64,32,128]{2,1,0:T(8,128)(2,1)S(1)}, u32[]{:S(2)}, u32[]{:S(2)}) collective-permute-start(bf16[64,32,128]{2,1,0:T(8,128)(2,1)S(1)} %convolution_convert_fusion.1), channel_id=1, source_target_pairs={{3,1},{5,3},{7,5},{9,7},{11,9},{13,11},{15,13},{17,15},{19,17},{21... | collective-permute-start | bytes 1572872 | tf_op jit(solution)/shard_map/ppermute | solution.py:78
  178.8 3.8 %collective-permute-start.5 = (bf16[64,32,128]{2,1,0:T(8,128)(2,1)S(1)}, bf16[64,32,128]{2,1,0:T(8,128)(2,1)S(1)}, u32[]{:S(2)}, u32[]{:S(2)}) collective-permute-start(bf16[64,32,128]{2,1,0:T(8,128)(2,1)S(1)} %broadcast_select_fusion), channel_id=1, source_target_pairs={{0,1},{1,0},{2,3},{3,2},{4,5},{5,4},{6,7},{7,6},{8,9},{9,8},{10,11... | collective-permute-start | bytes 1572872 | tf_op jit(solution)/shard_map/ppermute | solution.py:80

commit v10 on v9

--- a/solution.py
+++ b/solution.py
@@ -43,21 +43,21 @@
     id_rows = jnp.broadcast_to(packed_ids[:, None, None], (owners_count, 16, 128))
     outgoing = jnp.concatenate([packed, id_rows], axis=1)
     arrived_all = lax.all_to_all(outgoing, "zs", split_axis=0, concat_axis=0, tiled=True)
-    arrived = arrived_all[:, : CELLS // 128]
     arrived_ids = arrived_all[:, CELLS // 128, 0].astype(jnp.int32)
     placing = (arrived_ids[None, :] == jnp.arange(blocks_local)[:, None]).astype(jnp.bfloat16)
-    assembled = jnp.einsum("bs,skc->bkc", placing, arrived, preferred_element_type=jnp.float32)
-    assembled = lax.optimization_barrier(assembled)
+    assembled = jnp.einsum("bs,skc->bkc", placing, arrived_all, preferred_element_type=jnp.float32)
+    assembled = lax.optimization_barrier(assembled)[:, : CELLS // 128]
     assembled = assembled.reshape(2, YBLOCKS, BLK, BLK, BLK).transpose(0, 2, 4, 1, 3)
     gradient = assembled.reshape(CX, CZ, NY)
     norms = jnp.sqrt(jnp.sum(taps * taps, axis=1, keepdims=True))
     kernel = (taps / norms).astype(jnp.bfloat16)
     field = gradient.astype(jnp.bfloat16)
-    padded = jnp.concatenate(
-        [shifted(field, "xb", 1), field, shifted(field, "xb", -1)], axis=0
+    neighbours = (shifted(field, "xb", 1), field, shifted(field, "xb", -1))
+    x_matrix = band_matrix(kernel[0], CX, 3 * CX, 0)
+    along_x = sum(
+        jnp.dot(x_matrix[:, k * CX : (k + 1) * CX], part.reshape(CX, CZ * NY), preferred_element_type=jnp.float32)
+        for k, part in ((1, field), (0, neighbours[0]), (2, neighbours[2]))
     )
-    x_matrix = band_matrix(kernel[0], CX, 3 * CX, 0)
-    along_x = jnp.dot(x_matrix, padded.reshape(3 * CX, CZ * NY), preferred_element_type=jnp.float32)
     along_x = along_x.astype(jnp.bfloat16).reshape(CX, CZ, NY)
     y_matrix = band_matrix(kernel[1], NY, NY, REACH)
     along_y = jnp.einsum(

time: 188 us -> 192 us (1.021); the launches traced: 184 us -> 191 us
  waiting for transfers between devices: 121 us -> 113 us
  local copies, waits for them, and re-layouts: 17.4 us -> 23.4 us
  matrix products: 6.5 us -> 9.71 us
  other arithmetic: 5.38 us -> 7.86 us
    ppermute x2, waiting for transfers between devices: 9.57 us -> 0.01 us  [shifted(): return lax.ppermute(x, axis, pairs)]
    convert_element_type x0 -> x2, local copies, waits for them, and re-layouts: none -> 7.75 us  [body(): field = gradient.astype(jnp.bfloat16)]
    convert_element_type x1 -> x2, other arithmetic: 0.95 us -> 4.97 us  [body(): field = gradient.astype(jnp.bfloat16)]
    dot_general x2 -> x4, matrix products: 1.88 us -> 5.1 us  [the longest x3 3.02 us: body(): jnp.dot(x_matrix[:, k * CX:(k + 1) * CX], part.reshape(CX, CZ * NY), pref...]
    ppermute x1, starting transfers between devices: 3.16 us -> 6.06 us  [body(): prev1 = lax.ppermute(along_y, 'zs', pairs(1, None))]
  transfers between devices with their start and end apart: 8 -> 8, of which waited for: 6 -> 4; matrix products, arithmetic and copies ran while one was open for 2% -> 9% of each run, Pallas kernels for 0% -> 0%
where the time goes in v10:
time: 192 us; the launch traced here: 191 us
  waiting for transfers between devices  113 us (59%)
  starting transfers between devices  35.4 us (18%)
  local copies, waits for them, and re-layouts  23.4 us (12%)
  matrix products  9.71 us (5%)
  other arithmetic  7.86 us (4%)
    all_to_all x1, waiting for transfers between devices, body(): lax.all_to_all(outgoing, 'zs', split_axis=0, concat_axis=0, tiled=True)  103 us
    all_to_all x1, starting transfers between devices, body(): lax.all_to_all(outgoing, 'zs', split_axis=0, concat_axis=0, tiled=True)  16.1 us
    ppermute x1, waiting for transfers between devices, body(): next1 = lax.ppermute(along_y, 'zs', pairs(-1, None))  8.31 us
    convert_element_type x2, local copies, waits for them, and re-layouts, body(): field = gradient.astype(jnp.bfloat16)  7.75 us
    ppermute x2, starting transfers between devices, shifted(): return lax.ppermute(x, axis, pairs)  7.38 us
    ppermute x1, starting transfers between devices, body(): prev1 = lax.ppermute(along_y, 'zs', pairs(1, None))  6.06 us
    transpose x1, local copies, waits for them, and re-layouts, body(): assembled.reshape(2, YBLOCKS, BLK, BLK, BLK).transpose(0, 2, 4, 1, 3)  5.24 us
    convert_element_type x2, other arithmetic, body(): field = gradient.astype(jnp.bfloat16)  4.97 us
  transfers between devices with their start and end apart: 8, of which 4 were waited for; matrix products, arithmetic and copies ran while one was open for 9% of the time, Pallas kernels for 0%

profile of v10, /device:TPU:7, one launch (start us, length us, event | category | flops | bytes accessed | tf_op | source)
XLA Modules:
  0.0 190.7 jit_solution(642097582314147382)
XLA Ops:
  0.6 0.8 fusion.36
  1.5 0.1 select_reduce_fusion
  1.6 0.7 copy-done
  2.2 0.7 fusion.6
  2.9 0.1 broadcast_in_dim.29
  3.0 0.2 pad_maximum_fusion
  3.2 2.2 %copy.13 = bf16[32,272,128]{2,1,0:T(8,128)(2,1)} copy(bf16[32,272,128]{2,0,1:T(8,128)(2,1)S(1)} %pad_maximum_fusion) | data formatting | bytes 4456448 | tf_op jit(solution)/shard_map/concatenate | solution.py:44
  5.5 16.1 %all-to-all-start = ((bf16[32,272,128]{2,1,0:T(8,128)(2,1)}), bf16[32,272,128]{2,1,0:T(8,128)(2,1)}, u32[]{:S(2)}, u32[]{:S(2)}) async-start(bf16[32,272,128]{2,1,0:T(8,128)(2,1)} %copy.13), calls=%async_computation | async-start | bytes 4456448 | tf_op jit(solution)/shard_map/all_to_all | solution.py:45
  21.6 0.1 multiply_reduce_fusion
  21.7 0.1 divide_convert_fusion
  21.9 0.2 reshape.54
  22.1 0.1 pad_slice_fusion.1
  22.2 0.3 reshape.58
  22.6 103.0 %all-to-all-done = bf16[32,272,128]{2,1,0:T(8,128)(2,1)} async-done(((bf16[32,272,128]{2,1,0:T(8,128)(2,1)}), bf16[32,272,128]{2,1,0:T(8,128)(2,1)}, u32[]{:S(2)}, u32[]{:S(2)}) %all-to-all-start) | async-done | bytes 2228256 | tf_op jit(solution)/shard_map/all_to_all | solution.py:45
  125.5 1.5 fusion.27
  127.0 2.1 %fusion.1 = f32[8,272,128]{2,0,1:T(8,128)S(1)} fusion(bf16[32,272,128]{2,1,0:T(8,128)(2,1)} %all-to-all-done, s32[32]{0:T(128)S(1)} %fusion.27), kind=kOutput, calls=%fused_computation.4 | convolution fusion | flops 17826048 | bytes 3342464 | tf_op jit(solution)/shard_map/bs,skc->bkc/dot_general | solution.py:48
  129.1 0.1 slice.97
  129.2 0.2 copy.15
  129.4 2.4 %reshape.52 = f32[2,4,32,32,32]{4,3,2,1,0:T(8,128)} reshape(f32[8,256,128]{2,1,0:T(8,128)S(1)} %copy.15) | data formatting | bytes 2097152 | tf_op jit(solution)/shard_map/reshape | solution.py:50
  131.8 5.2 %copy.16 = f32[2,32,32,4,32]{4,3,2,1,0:T(4,128)} copy(f32[2,32,32,4,32]{2,4,1,3,0:T(8,128)} %bitcast.66) | data formatting | bytes 2097152 | tf_op jit(solution)/shard_map/transpose | solution.py:50
  137.1 3.7 %reshape.53 = f32[64,32,128]{2,1,0:T(8,128)S(1)} reshape(f32[2,32,32,4,32]{4,3,2,1,0:T(4,128)} %copy.16) | data formatting | bytes 2097152 | tf_op jit(solution)/shard_map/reshape | solution.py:51
  140.8 1.0 convert_element_type.52
  141.7 3.2 %collective-permute-start = (bf16[64,32,128]{2,1,0:T(8,128)(2,1)}, bf16[64,32,128]{2,1,0:T(8,128)(2,1)}, u32[]{:S(2)}, u32[]{:S(2)}) collective-permute-start(bf16[64,32,128]{2,1,0:T(8,128)(2,1)} %convert_element_type.52), channel_id=1, source_target_pairs={{0,32},{32,64},{64,96},{96,128},{128,160},{160,192},{192,224},{224... | collective-permute-start | bytes 1572872 | tf_op jit(solution)/shard_map/ppermute | solution.py:18
  144.9 4.2 %collective-permute-start.1 = (bf16[64,32,128]{2,1,0:T(8,128)(2,1)}, bf16[64,32,128]{2,1,0:T(8,128)(2,1)}, u32[]{:S(2)}, u32[]{:S(2)}) collective-permute-start(bf16[64,32,128]{2,1,0:T(8,128)(2,1)} %convert_element_type.52), channel_id=1, source_target_pairs={{32,0},{64,32},{96,64},{128,96},{160,128},{192,160},{224,192},{256... | collective-permute-start | bytes 1572872 | tf_op jit(solution)/shard_map/ppermute | solution.py:18
  149.1 4.0 %bitcast_convert_fusion = bf16[2,32,32,4,32]{2,4,1,3,0:T(8,128)(2,1)} fusion(f32[2,4,32,32,32]{4,3,2,1,0:T(8,128)} %reshape.52), kind=kLoop, calls=%fused_computation.67 | loop fusion | flops 262144 | bytes 1572864 | tf_op jit(solution)/shard_map/convert_element_type | solution.py:54
  153.2 4.3 %copy.17 = bf16[2,32,32,4,32]{4,3,2,1,0:T(4,128)(2,1)} copy(bf16[2,32,32,4,32]{2,4,1,3,0:T(8,128)(2,1)} %bitcast_convert_fusion) | data formatting | bytes 1048576 | tf_op jit(solution)/shard_map/convert_element_type | solution.py:54
  157.4 3.5 %convert_element_type.51 = bf16[64,4096]{1,0:T(8,128)(2,1)S(1)} reshape(bf16[2,32,32,4,32]{4,3,2,1,0:T(4,128)(2,1)} %copy.17) | data formatting | bytes 1048576 | tf_op jit(solution)/shard_map/convert_element_type | solution.py:54
  160.9 0.3 fusion.25
  161.3 1.3 convolution_add_fusion.1
  162.6 1.3 fusion.12
  164.0 0.1 copy.22
  164.1 0.3 convolution_convert_fusion
  164.4 6.1 %collective-permute-start.2 = (bf16[64,32,128]{2,1,0:T(8,128)(2,1)S(1)}, bf16[64,32,128]{2,1,0:T(8,128)(2,1)}, u32[]{:S(2)}, u32[]{:S(2)}) collective-permute-start(bf16[64,32,128]{2,1,0:T(8,128)(2,1)S(1)} %convolution_convert_fusion), channel_id=1, source_target_pairs={{0,1},{1,2},{2,3},{3,4},{4,5},{5,6},{6,7},{7,8},{8,9},{9,10},{10,1... | collective-permute-start | bytes 1572872 | tf_op jit(solution)/shard_map/ppermute | solution.py:75
  170.5 1.9 %collective-permute-start.3 = (bf16[64,32,128]{2,1,0:T(8,128)(2,1)S(1)}, bf16[64,32,128]{2,1,0:T(8,128)(2,1)S(1)}, u32[]{:S(2)}, u32[]{:S(2)}) collective-permute-start(bf16[64,32,128]{2,1,0:T(8,128)(2,1)S(1)} %convolution_convert_fusion), channel_id=1, source_target_pairs={{1,0},{2,1},{3,2},{4,3},{5,4},{6,5},{7,6},{8,7},{9,8},{10,9},{11,1... | collective-permute-start | bytes 1572872 | tf_op jit(solution)/shard_map/ppermute | solution.py:76
  172.4 0.1 tile.32
  172.5 0.1 reshape.59
  172.7 1.3 collective-permute-start.6
  174.0 0.7 collective-permute-start.4
  174.7 1.9 collective-permute-done.2
  176.6 8.3 %collective-permute-done.3 = bf16[64,32,128]{2,1,0:T(8,128)(2,1)S(1)} collective-permute-done((bf16[64,32,128]{2,1,0:T(8,128)(2,1)S(1)}, bf16[64,32,128]{2,1,0:T(8,128)(2,1)S(1)}, u32[]{:S(2)}, u32[]{:S(2)}) %collective-permute-start.3) | collective-permute-done | bytes 524320 | tf_op jit(solution)/shard_map/ppermute | solution.py:76
  184.9 0.1 broadcast_select_fusion
  184.9 1.9 %collective-permute-start.5 = (bf16[64,32,128]{2,1,0:T(8,128)(2,1)S(1)}, bf16[64,32,128]{2,1,0:T(8,128)(2,1)S(1)}, u32[]{:S(2)}, u32[]{:S(2)}) collective-permute-start(bf16[64,32,128]{2,1,0:T(8,128)(2,1)S(1)} %broadcast_select_fusion), channel_id=1, source_target_pairs={{0,1},{1,0},{2,3},{3,2},{4,5},{5,4},{6,7},{7,6},{8,9},{9,8},{10,11... | collective-permute-start | bytes 1572872 | tf_op jit(solution)/shard_map/ppermute | solution.py:80
  186.9 0.3 fusion.30
  187.2 1.4 convolution_add_fusion.3
  188.6 0.1 collective-permute-done.5
  188.7 0.3 fusion.17
  189.0 0.3 fusion.19
  189.3 1.3 fusion.11
  (22 shorter events, 0.2 us)
Async XLA Ops:
  0.6 1.6 copy-start
  5.5 16.1 %copy-start.2 = (f32[3,129]{1,0:T(4,128)S(1)}, f32[3,129]{1,0:T(4,128)}, u32[]{:S(2)}) copy-start(f32[3,129]{1,0:T(4,128)} %param.5) | copy-start | bytes 4648
  5.5 120.1 %all-to-all-start = ((bf16[32,272,128]{2,1,0:T(8,128)(2,1)}), bf16[32,272,128]{2,1,0:T(8,128)(2,1)}, u32[]{:S(2)}, u32[]{:S(2)}) async-start(bf16[32,272,128]{2,1,0:T(8,128)(2,1)} %copy.13), calls=%async_computation | async-start | bytes 4456448 | tf_op jit(solution)/shard_map/all_to_all | solution.py:45
  140.8 12.4 %copy-start.1 = (f32[64,32,128]{2,1,0:T(8,128)}, f32[64,32,128]{2,1,0:T(8,128)S(1)}, u32[]{:S(2)}) copy-start(f32[64,32,128]{2,1,0:T(8,128)S(1)} %reshape.53) | copy-start | bytes 3145732
  141.7 19.5 %collective-permute-start = (bf16[64,32,128]{2,1,0:T(8,128)(2,1)}, bf16[64,32,128]{2,1,0:T(8,128)(2,1)}, u32[]{:S(2)}, u32[]{:S(2)}) collective-permute-start(bf16[64,32,128]{2,1,0:T(8,128)(2,1)} %convert_element_type.52), channel_id=1, source_target_pairs={{0,32},{32,64},{64,96},{96,128},{128,160},{160,192},{192,224},{224... | collective-permute-start | bytes 1572872 | tf_op jit(solution)/shard_map/ppermute | solution.py:18
  144.9 17.7 %collective-permute-start.1 = (bf16[64,32,128]{2,1,0:T(8,128)(2,1)}, bf16[64,32,128]{2,1,0:T(8,128)(2,1)}, u32[]{:S(2)}, u32[]{:S(2)}) collective-permute-start(bf16[64,32,128]{2,1,0:T(8,128)(2,1)} %convert_element_type.52), channel_id=1, source_target_pairs={{32,0},{64,32},{96,64},{128,96},{160,128},{192,160},{224,192},{256... | collective-permute-start | bytes 1572872 | tf_op jit(solution)/shard_map/ppermute | solution.py:18
  164.4 12.2 %collective-permute-start.2 = (bf16[64,32,128]{2,1,0:T(8,128)(2,1)S(1)}, bf16[64,32,128]{2,1,0:T(8,128)(2,1)}, u32[]{:S(2)}, u32[]{:S(2)}) collective-permute-start(bf16[64,32,128]{2,1,0:T(8,128)(2,1)S(1)} %convolution_convert_fusion), channel_id=1, source_target_pairs={{0,1},{1,2},{2,3},{3,4},{4,5},{5,6},{6,7},{7,8},{8,9},{9,10},{10,1... | collective-permute-start | bytes 1572872 | tf_op jit(solution)/shard_map/ppermute | solution.py:75
  170.5 14.4 %collective-permute-start.3 = (bf16[64,32,128]{2,1,0:T(8,128)(2,1)S(1)}, bf16[64,32,128]{2,1,0:T(8,128)(2,1)S(1)}, u32[]{:S(2)}, u32[]{:S(2)}) collective-permute-start(bf16[64,32,128]{2,1,0:T(8,128)(2,1)S(1)} %convolution_convert_fusion), channel_id=1, source_target_pairs={{1,0},{2,1},{3,2},{4,3},{5,4},{6,5},{7,6},{8,7},{9,8},{10,9},{11,1... | collective-permute-start | bytes 1572872 | tf_op jit(solution)/shard_map/ppermute | solution.py:76
  172.7 15.9 %collective-permute-start.6 = (bf16[64,32,128]{2,1,0:T(8,128)(2,1)S(1)}, bf16[64,32,128]{2,1,0:T(8,128)(2,1)S(1)}, u32[]{:S(2)}, u32[]{:S(2)}) collective-permute-start(bf16[64,32,128]{2,1,0:T(8,128)(2,1)S(1)} %convolution_convert_fusion), channel_id=1, source_target_pairs={{3,1},{5,3},{7,5},{9,7},{11,9},{13,11},{15,13},{17,15},{19,17},{21... | collective-permute-start | bytes 1572872 | tf_op jit(solution)/shard_map/ppermute | solution.py:78
  174.0 15.1 %collective-permute-start.4 = (bf16[64,32,128]{2,1,0:T(8,128)(2,1)S(1)}, bf16[64,32,128]{2,1,0:T(8,128)(2,1)S(1)}, u32[]{:S(2)}, u32[]{:S(2)}) collective-permute-start(bf16[64,32,128]{2,1,0:T(8,128)(2,1)S(1)} %convolution_convert_fusion), channel_id=1, source_target_pairs={{0,2},{2,4},{4,6},{6,8},{8,10},{10,12},{12,14},{14,16},{16,18},{18... | collective-permute-start | bytes 1572872 | tf_op jit(solution)/shard_map/ppermute | solution.py:77
  184.9 3.8 %collective-permute-start.5 = (bf16[64,32,128]{2,1,0:T(8,128)(2,1)S(1)}, bf16[64,32,128]{2,1,0:T(8,128)(2,1)S(1)}, u32[]{:S(2)}, u32[]{:S(2)}) collective-permute-start(bf16[64,32,128]{2,1,0:T(8,128)(2,1)S(1)} %broadcast_select_fusion), channel_id=1, source_target_pairs={{0,1},{1,0},{2,3},{3,2},{4,5},{5,4},{6,7},{7,6},{8,9},{9,8},{10,11... | collective-permute-start | bytes 1572872 | tf_op jit(solution)/shard_map/ppermute | solution.py:80

commit v11 on v9

--- a/solution.py
+++ b/solution.py
@@ -48,11 +48,15 @@
     placing = (arrived_ids[None, :] == jnp.arange(blocks_local)[:, None]).astype(jnp.bfloat16)
     assembled = jnp.einsum("bs,skc->bkc", placing, arrived, preferred_element_type=jnp.float32)
     assembled = lax.optimization_barrier(assembled)
-    assembled = assembled.reshape(2, YBLOCKS, BLK, BLK, BLK).transpose(0, 2, 4, 1, 3)
-    gradient = assembled.reshape(CX, CZ, NY)
+
+    def to_xzy(cubes):
+        cubes = cubes.reshape(2, YBLOCKS, BLK, BLK, BLK).transpose(0, 2, 4, 1, 3)
+        return cubes.reshape(CX, CZ, NY)
+
+    gradient = to_xzy(assembled)
+    field = to_xzy(lax.optimization_barrier(assembled.astype(jnp.bfloat16)))
     norms = jnp.sqrt(jnp.sum(taps * taps, axis=1, keepdims=True))
     kernel = (taps / norms).astype(jnp.bfloat16)
-    field = gradient.astype(jnp.bfloat16)
     padded = jnp.concatenate(
         [shifted(field, "xb", 1), field, shifted(field, "xb", -1)], axis=0
     )

time: 188 us -> 202 us (1.074); the launches traced: 184 us -> 201 us
  local copies, waits for them, and re-layouts: 17.4 us -> 39.6 us
  waiting for transfers between devices: 121 us -> 113 us
  matrix products: 6.5 us -> 9.21 us
    reshape x2 -> x4, local copies, waits for them, and re-layouts: 6.13 us -> 15.6 us  [the longest x2 8.32 us: to_xzy(): return cubes.reshape(CX, CZ, NY)]
    ppermute x1, waiting for transfers between devices: 6.56 us -> 0.01 us  [body(): next1 = lax.ppermute(along_y, 'zs', pairs(-1, None))]
    transpose x1 -> x2, local copies, waits for them, and re-layouts: 5.24 us -> 9.49 us  [to_xzy(): cubes = cubes.reshape(2, YBLOCKS, BLK, BLK, BLK).transpose(0, 2, 4, 1, 3)]
    concatenate x0 -> x1, local copies, waits for them, and re-layouts: none -> 4.22 us  [body(): jnp.concatenate([shifted(field, 'xb', 1), field, shifted(field, 'xb', -1)...]
    unnamed x11 -> x13, local copies, waits for them, and re-layouts: 0.87 us -> 3.36 us
    dot_general x5, matrix products: 3.63 us -> 5.73 us  [body(): jnp.einsum('zk,xky->xzy', z_matrix[:, k * CZ:(k + 1) * CZ], slab, preferr...]
  transfers between devices with their start and end apart: 8 -> 8, of which waited for: 6 -> 4; matrix products, arithmetic and copies ran while one was open for 2% -> 13% of each run, Pallas kernels for 0% -> 0%
where the time goes in v11:
time: 202 us; the launch traced here: 201 us
  waiting for transfers between devices  113 us (56%)
  local copies, waits for them, and re-layouts  39.6 us (20%)
  starting transfers between devices  34 us (17%)
  matrix products  9.21 us (5%)
  other arithmetic  4 us (2%)
    all_to_all x1, waiting for transfers between devices, body(): lax.all_to_all(outgoing, 'zs', split_axis=0, concat_axis=0, tiled=True)  104 us
    all_to_all x1, starting transfers between devices, body(): lax.all_to_all(outgoing, 'zs', split_axis=0, concat_axis=0, tiled=True)  16.1 us
    transpose x2, local copies, waits for them, and re-layouts, to_xzy(): cubes = cubes.reshape(2, YBLOCKS, BLK, BLK, BLK).transpose(0, 2, 4, 1, 3)  9.49 us
    ppermute x2, waiting for transfers between devices, shifted(): return lax.ppermute(x, axis, pairs)  8.4 us
    reshape x2, local copies, waits for them, and re-layouts, to_xzy(): return cubes.reshape(CX, CZ, NY)  8.32 us
    reshape x2, local copies, waits for them, and re-layouts, to_xzy(): cubes = cubes.reshape(2, YBLOCKS, BLK, BLK, BLK).transpose(0, 2, 4, 1, 3)  7.27 us
    ppermute x2, starting transfers between devices, shifted(): return lax.ppermute(x, axis, pairs)  6.82 us
    dot_general x5, matrix products, body(): jnp.einsum('zk,xky->xzy', z_matrix[:, k * CZ:(k + 1) * CZ], slab, preferr...  5.73 us
  transfers between devices with their start and end apart: 8, of which 4 were waited for; matrix products, arithmetic and copies ran while one was open for 13% of the time, Pallas kernels for 0%

profile of v11, /device:TPU:7, one launch (start us, length us, event | category | flops | bytes accessed | tf_op | source)
XLA Modules:
  0.0 200.9 jit_solution(9763067104621444851)
XLA Ops:
  0.6 0.8 fusion.35
  1.5 0.1 select_reduce_fusion
  1.6 0.7 copy-done
  2.2 0.7 fusion.5
  2.9 0.1 broadcast_in_dim.29
  3.0 0.2 pad_maximum_fusion
  3.2 2.2 %copy.18 = bf16[32,272,128]{2,1,0:T(8,128)(2,1)} copy(bf16[32,272,128]{2,0,1:T(8,128)(2,1)S(1)} %pad_maximum_fusion) | data formatting | bytes 4456448 | tf_op jit(solution)/shard_map/concatenate | solution.py:44
  5.5 16.1 %all-to-all-start = ((bf16[32,272,128]{2,1,0:T(8,128)(2,1)}), bf16[32,272,128]{2,1,0:T(8,128)(2,1)}, u32[]{:S(2)}, u32[]{:S(2)}) async-start(bf16[32,272,128]{2,1,0:T(8,128)(2,1)} %copy.18), calls=%async_computation | async-start | bytes 4456448 | tf_op jit(solution)/shard_map/all_to_all | solution.py:45
  21.6 0.1 multiply_reduce_fusion
  21.8 103.7 %all-to-all-done = bf16[32,272,128]{2,1,0:T(8,128)(2,1)} async-done(((bf16[32,272,128]{2,1,0:T(8,128)(2,1)}), bf16[32,272,128]{2,1,0:T(8,128)(2,1)}, u32[]{:S(2)}, u32[]{:S(2)}) %all-to-all-start) | async-done | bytes 2228256 | tf_op jit(solution)/shard_map/all_to_all | solution.py:45
  125.5 1.5 fusion.26
  127.0 1.7 slice.85
  128.8 1.2 fusion.3
  130.1 0.9 copy.22
  131.0 3.5 %reshape.57 = bf16[2,4,32,32,32]{4,3,2,1,0:T(8,128)(2,1)} reshape(bf16[8,256,128]{2,1,0:T(8,128)(2,1)} %copy.22) | data formatting | bytes 1048576 | tf_op jit(solution)/shard_map/reshape | solution.py:53
  134.5 4.3 %copy.23 = bf16[2,32,32,4,32]{4,3,2,1,0:T(4,128)(2,1)} copy(bf16[2,32,32,4,32]{2,4,1,3,0:T(8,128)(2,1)} %bitcast.66) | data formatting | bytes 1048576 | tf_op jit(solution)/shard_map/transpose | solution.py:53
  138.7 3.8 %reshape.58 = bf16[64,32,128]{2,1,0:T(8,128)(2,1)} reshape(bf16[2,32,32,4,32]{4,3,2,1,0:T(4,128)(2,1)} %copy.23) | data formatting | bytes 1048576 | tf_op jit(solution)/shard_map/reshape | solution.py:54
  142.5 4.9 %collective-permute-start.1 = (bf16[64,32,128]{2,1,0:T(8,128)(2,1)}, bf16[64,32,128]{2,1,0:T(8,128)(2,1)}, u32[]{:S(2)}, u32[]{:S(2)}) collective-permute-start(bf16[64,32,128]{2,1,0:T(8,128)(2,1)} %reshape.58), channel_id=1, source_target_pairs={{32,0},{64,32},{96,64},{128,96},{160,128},{192,160},{224,192},{256... | collective-permute-start | bytes 1572872 | tf_op jit(solution)/shard_map/ppermute | solution.py:18
  147.4 1.9 collective-permute-start
  149.4 0.2 reshape.56
  149.6 0.1 pad_slice_fusion.1
  149.8 0.3 reshape.60
  150.1 4.2 %concatenate.25 = bf16[64,4096]{1,0:T(8,128)(2,1)} reshape(bf16[2,32,32,4,32]{4,3,2,1,0:T(4,128)(2,1)} %copy.23) | data formatting | bytes 1048576 | tf_op jit(solution)/shard_map/concatenate | solution.py:60
  154.3 3.7 %collective-permute-done.1 = bf16[64,32,128]{2,1,0:T(8,128)(2,1)} collective-permute-done((bf16[64,32,128]{2,1,0:T(8,128)(2,1)}, bf16[64,32,128]{2,1,0:T(8,128)(2,1)}, u32[]{:S(2)}, u32[]{:S(2)}) %collective-permute-start.1) | collective-permute-done | bytes 524320 | tf_op jit(solution)/shard_map/ppermute | solution.py:18
  158.0 1.3 copy.42
  159.3 4.7 %collective-permute-done = bf16[64,32,128]{2,1,0:T(8,128)(2,1)} collective-permute-done((bf16[64,32,128]{2,1,0:T(8,128)(2,1)}, bf16[64,32,128]{2,1,0:T(8,128)(2,1)}, u32[]{:S(2)}, u32[]{:S(2)}) %collective-permute-start) | collective-permute-done | bytes 524320 | tf_op jit(solution)/shard_map/ppermute | solution.py:18
  164.0 1.3 copy.43
  165.2 0.4 fusion.16
  165.6 0.1 copy.30
  165.7 1.2 convolution_convert_fusion.1
  166.9 4.0 %collective-permute-start.3 = (bf16[64,32,128]{2,1,0:T(8,128)(2,1)}, bf16[64,32,128]{2,1,0:T(8,128)(2,1)}, u32[]{:S(2)}, u32[]{:S(2)}) collective-permute-start(bf16[64,32,128]{2,1,0:T(8,128)(2,1)} %convolution_convert_fusion.1), channel_id=1, source_target_pairs={{1,0},{2,1},{3,2},{4,3},{5,4},{6,5},{7,6},{8,7},{9,8},{10,9},{11,1... | collective-permute-start | bytes 1572872 | tf_op jit(solution)/shard_map/ppermute | solution.py:80
  170.9 1.9 collective-permute-start.2
  172.9 0.1 tile.32
  173.0 0.1 reshape.61
  173.1 1.2 copy.20
  174.3 3.7 %reshape.54 = f32[2,4,32,32,32]{4,3,2,1,0:T(8,128)} reshape(f32[8,256,128]{2,1,0:T(8,128)} %copy.20) | data formatting | bytes 2097152 | tf_op jit(solution)/shard_map/reshape | solution.py:53
  178.0 5.2 %copy.21 = f32[2,32,32,4,32]{4,3,2,1,0:T(4,128)} copy(f32[2,32,32,4,32]{2,4,1,3,0:T(8,128)} %bitcast.65) | data formatting | bytes 2097152 | tf_op jit(solution)/shard_map/transpose | solution.py:53
  183.3 4.5 %reshape.55 = f32[64,32,128]{2,1,0:T(8,128)} reshape(f32[2,32,32,4,32]{4,3,2,1,0:T(4,128)} %copy.21) | data formatting | bytes 2097152 | tf_op jit(solution)/shard_map/reshape | solution.py:54
  187.8 1.3 collective-permute-start.6
  189.1 0.7 collective-permute-start.4
  189.8 1.1 broadcast_select_fusion
  190.9 3.2 %collective-permute-start.5 = (bf16[64,32,128]{2,1,0:T(8,128)(2,1)S(1)}, bf16[64,32,128]{2,1,0:T(8,128)(2,1)S(1)}, u32[]{:S(2)}, u32[]{:S(2)}) collective-permute-start(bf16[64,32,128]{2,1,0:T(8,128)(2,1)S(1)} %broadcast_select_fusion), channel_id=1, source_target_pairs={{0,1},{1,0},{2,3},{3,2},{4,5},{5,4},{6,7},{7,6},{8,9},{9,8},{10,11... | collective-permute-start | bytes 1572872 | tf_op jit(solution)/shard_map/ppermute | solution.py:84
  194.1 1.4 fusion.29
  195.5 1.4 convolution_add_fusion.1
  196.9 1.0 collective-permute-done.6
  197.9 0.3 fusion.19
  198.2 0.3 fusion.21
  198.5 2.4 %fusion.15 = f32[64,32,128]{2,1,0:T(8,128)} fusion(f32[64,128,32]{1,2,0:T(8,128)S(1)} %fusion.19, f32[64,128,32]{1,2,0:T(8,128)S(1)} %fusion.21, f32[64,128,32]{1,2,0:T(8,128)S(1)} %convolution_add_fusion.1, bf16[64,32,128]{2,1,0:T(8,128)(2,1)} %collective-permute-done.3, bf16[32,191]{1,0:T(8,128)(2,1)S(1)} %reshape.61), kind=kOutput, calls=%fused_computation.17 | convolution fusion | flops 17563648 | bytes 4726784 | tf_op jit(solution)/shard_map/zk,xky->xzy/dot_general | solution.py:91
  (24 shorter events, 0.3 us)
Async XLA Ops:
  0.6 1.6 copy-start
  5.5 16.1 %copy-start.2 = (f32[3,129]{1,0:T(4,128)S(1)}, f32[3,129]{1,0:T(4,128)}, u32[]{:S(2)}) copy-start(f32[3,129]{1,0:T(4,128)} %param.5) | copy-start | bytes 4648
  5.5 120.1 %all-to-all-start = ((bf16[32,272,128]{2,1,0:T(8,128)(2,1)}), bf16[32,272,128]{2,1,0:T(8,128)(2,1)}, u32[]{:S(2)}, u32[]{:S(2)}) async-start(bf16[32,272,128]{2,1,0:T(8,128)(2,1)} %copy.18), calls=%async_computation | async-start | bytes 4456448 | tf_op jit(solution)/shard_map/all_to_all | solution.py:45
  142.5 15.5 %collective-permute-start.1 = (bf16[64,32,128]{2,1,0:T(8,128)(2,1)}, bf16[64,32,128]{2,1,0:T(8,128)(2,1)}, u32[]{:S(2)}, u32[]{:S(2)}) collective-permute-start(bf16[64,32,128]{2,1,0:T(8,128)(2,1)} %reshape.58), channel_id=1, source_target_pairs={{32,0},{64,32},{96,64},{128,96},{160,128},{192,160},{224,192},{256... | collective-permute-start | bytes 1572872 | tf_op jit(solution)/shard_map/ppermute | solution.py:18
  147.4 16.5 %collective-permute-start = (bf16[64,32,128]{2,1,0:T(8,128)(2,1)}, bf16[64,32,128]{2,1,0:T(8,128)(2,1)}, u32[]{:S(2)}, u32[]{:S(2)}) collective-permute-start(bf16[64,32,128]{2,1,0:T(8,128)(2,1)} %reshape.58), channel_id=1, source_target_pairs={{0,32},{32,64},{64,96},{96,128},{128,160},{160,192},{192,224},{224... | collective-permute-start | bytes 1572872 | tf_op jit(solution)/shard_map/ppermute | solution.py:18
  154.3 10.9 %copy-start.1 = (bf16[64,4096]{1,0:T(8,128)(2,1)S(1)}, bf16[64,4096]{1,0:T(8,128)(2,1)}, u32[]{:S(2)}) copy-start(bf16[64,4096]{1,0:T(8,128)(2,1)} %concatenate.25) | copy-start | bytes 1572868
  166.9 22.9 %collective-permute-start.3 = (bf16[64,32,128]{2,1,0:T(8,128)(2,1)}, bf16[64,32,128]{2,1,0:T(8,128)(2,1)}, u32[]{:S(2)}, u32[]{:S(2)}) collective-permute-start(bf16[64,32,128]{2,1,0:T(8,128)(2,1)} %convolution_convert_fusion.1), channel_id=1, source_target_pairs={{1,0},{2,1},{3,2},{4,3},{5,4},{6,5},{7,6},{8,7},{9,8},{10,9},{11,1... | collective-permute-start | bytes 1572872 | tf_op jit(solution)/shard_map/ppermute | solution.py:80
  170.9 18.9 %collective-permute-start.2 = (bf16[64,32,128]{2,1,0:T(8,128)(2,1)}, bf16[64,32,128]{2,1,0:T(8,128)(2,1)}, u32[]{:S(2)}, u32[]{:S(2)}) collective-permute-start(bf16[64,32,128]{2,1,0:T(8,128)(2,1)} %convolution_convert_fusion.1), channel_id=1, source_target_pairs={{0,1},{1,2},{2,3},{3,4},{4,5},{5,6},{6,7},{7,8},{8,9},{9,10},{10,1... | collective-permute-start | bytes 1572872 | tf_op jit(solution)/shard_map/ppermute | solution.py:79
  187.8 10.1 %collective-permute-start.6 = (bf16[64,32,128]{2,1,0:T(8,128)(2,1)}, bf16[64,32,128]{2,1,0:T(8,128)(2,1)S(1)}, u32[]{:S(2)}, u32[]{:S(2)}) collective-permute-start(bf16[64,32,128]{2,1,0:T(8,128)(2,1)} %convolution_convert_fusion.1), channel_id=1, source_target_pairs={{3,1},{5,3},{7,5},{9,7},{11,9},{13,11},{15,13},{17,15},{19,17},{21... | collective-permute-start | bytes 1572872 | tf_op jit(solution)/shard_map/ppermute | solution.py:82
  189.1 9.1 %collective-permute-start.4 = (bf16[64,32,128]{2,1,0:T(8,128)(2,1)}, bf16[64,32,128]{2,1,0:T(8,128)(2,1)S(1)}, u32[]{:S(2)}, u32[]{:S(2)}) collective-permute-start(bf16[64,32,128]{2,1,0:T(8,128)(2,1)} %convolution_convert_fusion.1), channel_id=1, source_target_pairs={{0,2},{2,4},{4,6},{6,8},{8,10},{10,12},{12,14},{14,16},{16,18},{18... | collective-permute-start | bytes 1572872 | tf_op jit(solution)/shard_map/ppermute | solution.py:81
  190.9 7.0 %collective-permute-start.5 = (bf16[64,32,128]{2,1,0:T(8,128)(2,1)S(1)}, bf16[64,32,128]{2,1,0:T(8,128)(2,1)S(1)}, u32[]{:S(2)}, u32[]{:S(2)}) collective-permute-start(bf16[64,32,128]{2,1,0:T(8,128)(2,1)S(1)} %broadcast_select_fusion), channel_id=1, source_target_pairs={{0,1},{1,0},{2,3},{3,2},{4,5},{5,4},{6,7},{7,6},{8,9},{9,8},{10,11... | collective-permute-start | bytes 1572872 | tf_op jit(solution)/shard_map/ppermute | solution.py:84

commit v12 on v9

--- a/solution.py
+++ b/solution.py
@@ -43,11 +43,10 @@
     id_rows = jnp.broadcast_to(packed_ids[:, None, None], (owners_count, 16, 128))
     outgoing = jnp.concatenate([packed, id_rows], axis=1)
     arrived_all = lax.all_to_all(outgoing, "zs", split_axis=0, concat_axis=0, tiled=True)
-    arrived = arrived_all[:, : CELLS // 128]
     arrived_ids = arrived_all[:, CELLS // 128, 0].astype(jnp.int32)
     placing = (arrived_ids[None, :] == jnp.arange(blocks_local)[:, None]).astype(jnp.bfloat16)
-    assembled = jnp.einsum("bs,skc->bkc", placing, arrived, preferred_element_type=jnp.float32)
-    assembled = lax.optimization_barrier(assembled)
+    assembled = jnp.einsum("bs,skc->bkc", placing, arrived_all, preferred_element_type=jnp.float32)
+    assembled = lax.optimization_barrier(assembled)[:, : CELLS // 128]
     assembled = assembled.reshape(2, YBLOCKS, BLK, BLK, BLK).transpose(0, 2, 4, 1, 3)
     gradient = assembled.reshape(CX, CZ, NY)
     norms = jnp.sqrt(jnp.sum(taps * taps, axis=1, keepdims=True))

time: 188 us -> 187 us (level)
  no operation moved by 1% of the time
where the time goes in v12:
time: 187 us; the launch traced here: 184 us
  waiting for transfers between devices  121 us (65%)
  starting transfers between devices  33.5 us (18%)
  local copies, waits for them, and re-layouts  15.7 us (8%)
  matrix products  7.33 us (4%)
  other arithmetic  5.37 us (3%)
    all_to_all x1, waiting for transfers between devices, body(): lax.all_to_all(outgoing, 'zs', split_axis=0, concat_axis=0, tiled=True)  104 us
    all_to_all x1, starting transfers between devices, body(): lax.all_to_all(outgoing, 'zs', split_axis=0, concat_axis=0, tiled=True)  16.1 us
    ppermute x2, waiting for transfers between devices, shifted(): return lax.ppermute(x, axis, pairs)  9.57 us
    ppermute x2, starting transfers between devices, shifted(): return lax.ppermute(x, axis, pairs)  7.38 us
    ppermute x1, waiting for transfers between devices, body(): next1 = lax.ppermute(along_y, 'zs', pairs(-1, None))  6.58 us
    transpose x1, local copies, waits for them, and re-layouts, body(): assembled.reshape(2, YBLOCKS, BLK, BLK, BLK).transpose(0, 2, 4, 1, 3)  5.24 us
  transfers between devices with their start and end apart: 8, of which 6 were waited for; matrix products, arithmetic and copies ran while one was open for 2% of the time, Pallas kernels for 0%

profile of v12, /device:TPU:7, one launch (start us, length us, event | category | flops | bytes accessed | tf_op | source)
XLA Modules:
  0.0 183.7 jit_solution(16038314362658892143)
XLA Ops:
  0.6 0.0 copy-start
  0.6 0.8 fusion.32
  1.5 0.1 select_reduce_fusion
  1.6 0.7 copy-done
  2.2 0.7 fusion.5
  2.9 0.1 broadcast_in_dim.29
  3.0 0.2 pad_maximum_fusion
  3.2 2.2 %copy.12 = bf16[32,272,128]{2,1,0:T(8,128)(2,1)} copy(bf16[32,272,128]{2,0,1:T(8,128)(2,1)S(1)} %pad_maximum_fusion) | data formatting | bytes 4456448 | tf_op jit(solution)/shard_map/concatenate | solution.py:44
  5.5 16.1 %all-to-all-start = ((bf16[32,272,128]{2,1,0:T(8,128)(2,1)}), bf16[32,272,128]{2,1,0:T(8,128)(2,1)}, u32[]{:S(2)}, u32[]{:S(2)}) async-start(bf16[32,272,128]{2,1,0:T(8,128)(2,1)} %copy.12), calls=%async_computation | async-start | bytes 4456448 | tf_op jit(solution)/shard_map/all_to_all | solution.py:45
  21.6 0.1 multiply_reduce_fusion
  21.7 0.1 divide_convert_fusion
  21.8 103.7 %all-to-all-done = bf16[32,272,128]{2,1,0:T(8,128)(2,1)} async-done(((bf16[32,272,128]{2,1,0:T(8,128)(2,1)}), bf16[32,272,128]{2,1,0:T(8,128)(2,1)}, u32[]{:S(2)}, u32[]{:S(2)}) %all-to-all-start) | async-done | bytes 2228256 | tf_op jit(solution)/shard_map/all_to_all | solution.py:45
  125.5 1.5 fusion.23
  127.0 2.1 %fusion = f32[8,272,128]{2,0,1:T(8,128)S(1)} fusion(bf16[32,272,128]{2,1,0:T(8,128)(2,1)} %all-to-all-done, s32[32]{0:T(128)S(1)} %fusion.23), kind=kOutput, calls=%fused_computation.2 | convolution fusion | flops 17826048 | bytes 3342464 | tf_op jit(solution)/shard_map/bs,skc->bkc/dot_general | solution.py:48
  129.1 0.1 slice.85
  129.2 0.2 copy.14
  129.4 2.4 %reshape.46 = f32[2,4,32,32,32]{4,3,2,1,0:T(8,128)} reshape(f32[8,256,128]{2,1,0:T(8,128)S(1)} %copy.14) | data formatting | bytes 2097152 | tf_op jit(solution)/shard_map/reshape | solution.py:50
  131.8 5.2 %copy.15 = f32[2,32,32,4,32]{4,3,2,1,0:T(4,128)} copy(f32[2,32,32,4,32]{2,4,1,3,0:T(8,128)} %bitcast.62) | data formatting | bytes 2097152 | tf_op jit(solution)/shard_map/transpose | solution.py:50
  137.1 3.7 %reshape.47 = f32[64,32,128]{2,1,0:T(8,128)S(1)} reshape(f32[2,32,32,4,32]{4,3,2,1,0:T(4,128)} %copy.15) | data formatting | bytes 2097152 | tf_op jit(solution)/shard_map/reshape | solution.py:51
  140.8 1.0 convert_element_type.44
  141.7 3.2 %collective-permute-start = (bf16[64,32,128]{2,1,0:T(8,128)(2,1)}, bf16[64,32,128]{2,1,0:T(8,128)(2,1)}, u32[]{:S(2)}, u32[]{:S(2)}) collective-permute-start(bf16[64,32,128]{2,1,0:T(8,128)(2,1)} %convert_element_type.44), channel_id=1, source_target_pairs={{0,32},{32,64},{64,96},{96,128},{128,160},{160,192},{192,224},{224... | collective-permute-start | bytes 1572872 | tf_op jit(solution)/shard_map/ppermute | solution.py:18
  144.9 4.2 %collective-permute-start.1 = (bf16[64,32,128]{2,1,0:T(8,128)(2,1)}, bf16[64,32,128]{2,1,0:T(8,128)(2,1)}, u32[]{:S(2)}, u32[]{:S(2)}) collective-permute-start(bf16[64,32,128]{2,1,0:T(8,128)(2,1)} %convert_element_type.44), channel_id=1, source_target_pairs={{32,0},{64,32},{96,64},{128,96},{160,128},{192,160},{224,192},{256... | collective-permute-start | bytes 1572872 | tf_op jit(solution)/shard_map/ppermute | solution.py:18
  149.2 0.2 reshape.48
  149.4 0.1 pad_slice_fusion.1
  149.5 0.1 copy.20
  149.6 0.3 reshape.51
  149.9 8.7 %collective-permute-done = bf16[64,32,128]{2,1,0:T(8,128)(2,1)} collective-permute-done((bf16[64,32,128]{2,1,0:T(8,128)(2,1)}, bf16[64,32,128]{2,1,0:T(8,128)(2,1)}, u32[]{:S(2)}, u32[]{:S(2)}) %collective-permute-start) | collective-permute-done | bytes 524320 | tf_op jit(solution)/shard_map/ppermute | solution.py:18
  158.5 0.9 collective-permute-done.1
  159.4 1.5 pad_maximum_fusion.1
  161.0 0.6 fusion.13
  161.6 0.1 copy.19
  161.7 0.3 convolution_convert_fusion.1
  162.0 3.2 %collective-permute-start.2 = (bf16[64,32,128]{2,1,0:T(8,128)(2,1)S(1)}, bf16[64,32,128]{2,1,0:T(8,128)(2,1)}, u32[]{:S(2)}, u32[]{:S(2)}) collective-permute-start(bf16[64,32,128]{2,1,0:T(8,128)(2,1)S(1)} %convolution_convert_fusion.1), channel_id=1, source_target_pairs={{0,1},{1,2},{2,3},{3,4},{4,5},{5,6},{6,7},{7,8},{8,9},{9,10},{10,1... | collective-permute-start | bytes 1572872 | tf_op jit(solution)/shard_map/ppermute | solution.py:74
  165.2 2.9 %collective-permute-start.3 = (bf16[64,32,128]{2,1,0:T(8,128)(2,1)S(1)}, bf16[64,32,128]{2,1,0:T(8,128)(2,1)S(1)}, u32[]{:S(2)}, u32[]{:S(2)}) collective-permute-start(bf16[64,32,128]{2,1,0:T(8,128)(2,1)S(1)} %convolution_convert_fusion.1), channel_id=1, source_target_pairs={{1,0},{2,1},{3,2},{4,3},{5,4},{6,5},{7,6},{8,7},{9,8},{10,9},{11,1... | collective-permute-start | bytes 1572872 | tf_op jit(solution)/shard_map/ppermute | solution.py:75
  168.2 0.1 tile.32
  168.3 0.1 reshape.52
  168.5 0.7 collective-permute-start.4
  169.2 1.3 collective-permute-start.6
  170.5 0.9 collective-permute-done.2
  171.3 6.6 %collective-permute-done.3 = bf16[64,32,128]{2,1,0:T(8,128)(2,1)S(1)} collective-permute-done((bf16[64,32,128]{2,1,0:T(8,128)(2,1)S(1)}, bf16[64,32,128]{2,1,0:T(8,128)(2,1)S(1)}, u32[]{:S(2)}, u32[]{:S(2)}) %collective-permute-start.3) | collective-permute-done | bytes 524320 | tf_op jit(solution)/shard_map/ppermute | solution.py:75
  177.9 0.1 broadcast_select_fusion
  178.0 1.9 %collective-permute-start.5 = (bf16[64,32,128]{2,1,0:T(8,128)(2,1)S(1)}, bf16[64,32,128]{2,1,0:T(8,128)(2,1)S(1)}, u32[]{:S(2)}, u32[]{:S(2)}) collective-permute-start(bf16[64,32,128]{2,1,0:T(8,128)(2,1)S(1)} %broadcast_select_fusion), channel_id=1, source_target_pairs={{0,1},{1,0},{2,3},{3,2},{4,5},{5,4},{6,7},{7,6},{8,9},{9,8},{10,11... | collective-permute-start | bytes 1572872 | tf_op jit(solution)/shard_map/ppermute | solution.py:79
  179.9 0.3 fusion.26
  180.2 1.4 convolution_add_fusion.1
  181.6 0.1 collective-permute-done.5
  181.8 0.3 fusion.18
  182.1 0.3 fusion.16
  182.4 1.3 fusion.12
  (18 shorter events, 0.2 us)
Async XLA Ops:
  0.6 1.6 copy-start
  5.5 16.1 %copy-start.2 = (f32[3,129]{1,0:T(4,128)S(1)}, f32[3,129]{1,0:T(4,128)}, u32[]{:S(2)}) copy-start(f32[3,129]{1,0:T(4,128)} %param.5) | copy-start | bytes 4648
  5.5 120.1 %all-to-all-start = ((bf16[32,272,128]{2,1,0:T(8,128)(2,1)}), bf16[32,272,128]{2,1,0:T(8,128)(2,1)}, u32[]{:S(2)}, u32[]{:S(2)}) async-start(bf16[32,272,128]{2,1,0:T(8,128)(2,1)} %copy.12), calls=%async_computation | async-start | bytes 4456448 | tf_op jit(solution)/shard_map/all_to_all | solution.py:45
  140.8 20.2 %copy-start.1 = (f32[64,32,128]{2,1,0:T(8,128)}, f32[64,32,128]{2,1,0:T(8,128)S(1)}, u32[]{:S(2)}) copy-start(f32[64,32,128]{2,1,0:T(8,128)S(1)} %reshape.47) | copy-start | bytes 3145732
  141.7 16.8 %collective-permute-start = (bf16[64,32,128]{2,1,0:T(8,128)(2,1)}, bf16[64,32,128]{2,1,0:T(8,128)(2,1)}, u32[]{:S(2)}, u32[]{:S(2)}) collective-permute-start(bf16[64,32,128]{2,1,0:T(8,128)(2,1)} %convert_element_type.44), channel_id=1, source_target_pairs={{0,32},{32,64},{64,96},{96,128},{128,160},{160,192},{192,224},{224... | collective-permute-start | bytes 1572872 | tf_op jit(solution)/shard_map/ppermute | solution.py:18
  144.9 14.5 %collective-permute-start.1 = (bf16[64,32,128]{2,1,0:T(8,128)(2,1)}, bf16[64,32,128]{2,1,0:T(8,128)(2,1)}, u32[]{:S(2)}, u32[]{:S(2)}) collective-permute-start(bf16[64,32,128]{2,1,0:T(8,128)(2,1)} %convert_element_type.44), channel_id=1, source_target_pairs={{32,0},{64,32},{96,64},{128,96},{160,128},{192,160},{224,192},{256... | collective-permute-start | bytes 1572872 | tf_op jit(solution)/shard_map/ppermute | solution.py:18
  162.0 9.3 %collective-permute-start.2 = (bf16[64,32,128]{2,1,0:T(8,128)(2,1)S(1)}, bf16[64,32,128]{2,1,0:T(8,128)(2,1)}, u32[]{:S(2)}, u32[]{:S(2)}) collective-permute-start(bf16[64,32,128]{2,1,0:T(8,128)(2,1)S(1)} %convolution_convert_fusion.1), channel_id=1, source_target_pairs={{0,1},{1,2},{2,3},{3,4},{4,5},{5,6},{6,7},{7,8},{8,9},{9,10},{10,1... | collective-permute-start | bytes 1572872 | tf_op jit(solution)/shard_map/ppermute | solution.py:74
  165.2 12.7 %collective-permute-start.3 = (bf16[64,32,128]{2,1,0:T(8,128)(2,1)S(1)}, bf16[64,32,128]{2,1,0:T(8,128)(2,1)S(1)}, u32[]{:S(2)}, u32[]{:S(2)}) collective-permute-start(bf16[64,32,128]{2,1,0:T(8,128)(2,1)S(1)} %convolution_convert_fusion.1), channel_id=1, source_target_pairs={{1,0},{2,1},{3,2},{4,3},{5,4},{6,5},{7,6},{8,7},{9,8},{10,9},{11,1... | collective-permute-start | bytes 1572872 | tf_op jit(solution)/shard_map/ppermute | solution.py:75
  168.5 13.2 %collective-permute-start.4 = (bf16[64,32,128]{2,1,0:T(8,128)(2,1)S(1)}, bf16[64,32,128]{2,1,0:T(8,128)(2,1)S(1)}, u32[]{:S(2)}, u32[]{:S(2)}) collective-permute-start(bf16[64,32,128]{2,1,0:T(8,128)(2,1)S(1)} %convolution_convert_fusion.1), channel_id=1, source_target_pairs={{0,2},{2,4},{4,6},{6,8},{8,10},{10,12},{12,14},{14,16},{16,18},{18... | collective-permute-start | bytes 1572872 | tf_op jit(solution)/shard_map/ppermute | solution.py:76
  169.2 12.9 %collective-permute-start.6 = (bf16[64,32,128]{2,1,0:T(8,128)(2,1)S(1)}, bf16[64,32,128]{2,1,0:T(8,128)(2,1)S(1)}, u32[]{:S(2)}, u32[]{:S(2)}) collective-permute-start(bf16[64,32,128]{2,1,0:T(8,128)(2,1)S(1)} %convolution_convert_fusion.1), channel_id=1, source_target_pairs={{3,1},{5,3},{7,5},{9,7},{11,9},{13,11},{15,13},{17,15},{19,17},{21... | collective-permute-start | bytes 1572872 | tf_op jit(solution)/shard_map/ppermute | solution.py:77
  178.0 3.8 %collective-permute-start.5 = (bf16[64,32,128]{2,1,0:T(8,128)(2,1)S(1)}, bf16[64,32,128]{2,1,0:T(8,128)(2,1)S(1)}, u32[]{:S(2)}, u32[]{:S(2)}) collective-permute-start(bf16[64,32,128]{2,1,0:T(8,128)(2,1)S(1)} %broadcast_select_fusion), channel_id=1, source_target_pairs={{0,1},{1,0},{2,3},{3,2},{4,5},{5,4},{6,7},{7,6},{8,9},{9,8},{10,11... | collective-permute-start | bytes 1572872 | tf_op jit(solution)/shard_map/ppermute | solution.py:79

commit v13 on v12

--- a/solution.py
+++ b/solution.py
@@ -75,12 +75,10 @@
     next1 = lax.ppermute(along_y, "zs", pairs(-1, None))
     prev2_even = lax.ppermute(along_y, "zs", pairs(2, 0))
     next2_odd = lax.ppermute(along_y, "zs", pairs(-2, 1))
-    even = lax.axis_index("zs") % 2 == 0
-    relayed = lax.ppermute(
-        jnp.where(even, prev1, next1), "zs", [(i, i ^ 1) for i in range(zs_count)]
-    )
-    prev2 = jnp.where(even, prev2_even, relayed)
-    next2 = jnp.where(even, relayed, next2_odd)
+    to_odd = lax.ppermute(prev1, "zs", [(i, i + 1) for i in range(0, zs_count, 2)])
+    to_even = lax.ppermute(next1, "zs", [(i, i - 1) for i in range(1, zs_count, 2)])
+    prev2 = prev2_even + to_odd
+    next2 = next2_odd + to_even
     z_matrix = band_matrix(kernel[2], CZ, CZ + 2 * REACH, 0)
     smoothed = sum(
         jnp.einsum(

time: 187 us -> 184 us (0.984)
  waiting for transfers between devices: 121 us -> 118 us
    ppermute x1, waiting for transfers between devices: 6.58 us -> 1.98 us  [body(): next1 = lax.ppermute(along_y, 'zs', pairs(-1, None))]
  transfers between devices with their start and end apart: 8 -> 9, of which waited for: 6 -> 6; matrix products, arithmetic and copies ran while one was open for 2% -> 2% of each run, Pallas kernels for 0% -> 0%
where the time goes in v13:
time: 184 us; the launch traced here: 182 us
  waiting for transfers between devices  118 us (64%)
  starting transfers between devices  34 us (18%)
  local copies, waits for them, and re-layouts  15.7 us (9%)
  matrix products  7.36 us (4%)
  other arithmetic  5.32 us (3%)
    all_to_all x1, waiting for transfers between devices, body(): lax.all_to_all(outgoing, 'zs', split_axis=0, concat_axis=0, tiled=True)  104 us
    all_to_all x1, starting transfers between devices, body(): lax.all_to_all(outgoing, 'zs', split_axis=0, concat_axis=0, tiled=True)  16.1 us
    ppermute x2, waiting for transfers between devices, shifted(): return lax.ppermute(x, axis, pairs)  9.57 us
    ppermute x2, starting transfers between devices, shifted(): return lax.ppermute(x, axis, pairs)  7.38 us
    transpose x1, local copies, waits for them, and re-layouts, body(): assembled.reshape(2, YBLOCKS, BLK, BLK, BLK).transpose(0, 2, 4, 1, 3)  5.24 us
    ppermute x1, starting transfers between devices, body(): next1 = lax.ppermute(along_y, 'zs', pairs(-1, None))  4.05 us
    reshape x1, local copies, waits for them, and re-layouts, body(): gradient = assembled.reshape(CX, CZ, NY)  3.71 us
  transfers between devices with their start and end apart: 9, of which 6 were waited for; matrix products, arithmetic and copies ran while one was open for 2% of the time, Pallas kernels for 0%

profile of v13, /device:TPU:7, one launch (start us, length us, event | category | flops | bytes accessed | tf_op | source)
XLA Modules:
  0.0 181.6 jit_solution(18379793776038047334)
XLA Ops:
  0.6 0.0 copy-start
  0.6 0.8 fusion.28
  1.5 0.1 select_reduce_fusion
  1.6 0.7 copy-done
  2.2 0.7 fusion.5
  2.9 0.1 broadcast_in_dim.29
  3.0 0.2 pad_maximum_fusion
  3.2 2.2 %copy.12 = bf16[32,272,128]{2,1,0:T(8,128)(2,1)} copy(bf16[32,272,128]{2,0,1:T(8,128)(2,1)S(1)} %pad_maximum_fusion) | data formatting | bytes 4456448 | tf_op jit(solution)/shard_map/concatenate | solution.py:44
  5.5 16.1 %all-to-all-start = ((bf16[32,272,128]{2,1,0:T(8,128)(2,1)}), bf16[32,272,128]{2,1,0:T(8,128)(2,1)}, u32[]{:S(2)}, u32[]{:S(2)}) async-start(bf16[32,272,128]{2,1,0:T(8,128)(2,1)} %copy.12), calls=%async_computation | async-start | bytes 4456448 | tf_op jit(solution)/shard_map/all_to_all | solution.py:45
  21.6 0.1 multiply_reduce_fusion
  21.7 0.1 divide_convert_fusion
  21.8 103.7 %all-to-all-done = bf16[32,272,128]{2,1,0:T(8,128)(2,1)} async-done(((bf16[32,272,128]{2,1,0:T(8,128)(2,1)}), bf16[32,272,128]{2,1,0:T(8,128)(2,1)}, u32[]{:S(2)}, u32[]{:S(2)}) %all-to-all-start) | async-done | bytes 2228256 | tf_op jit(solution)/shard_map/all_to_all | solution.py:45
  125.5 1.5 fusion.19
  127.0 2.1 %fusion = f32[8,272,128]{2,0,1:T(8,128)S(1)} fusion(bf16[32,272,128]{2,1,0:T(8,128)(2,1)} %all-to-all-done, s32[32]{0:T(128)S(1)} %fusion.19), kind=kOutput, calls=%fused_computation.2 | convolution fusion | flops 17826048 | bytes 3342464 | tf_op jit(solution)/shard_map/bs,skc->bkc/dot_general | solution.py:48
  129.1 0.1 slice.85
  129.2 0.2 copy.14
  129.4 2.4 %reshape.46 = f32[2,4,32,32,32]{4,3,2,1,0:T(8,128)} reshape(f32[8,256,128]{2,1,0:T(8,128)S(1)} %copy.14) | data formatting | bytes 2097152 | tf_op jit(solution)/shard_map/reshape | solution.py:50
  131.8 5.2 %copy.15 = f32[2,32,32,4,32]{4,3,2,1,0:T(4,128)} copy(f32[2,32,32,4,32]{2,4,1,3,0:T(8,128)} %bitcast.62) | data formatting | bytes 2097152 | tf_op jit(solution)/shard_map/transpose | solution.py:50
  137.1 3.7 %reshape.47 = f32[64,32,128]{2,1,0:T(8,128)S(1)} reshape(f32[2,32,32,4,32]{4,3,2,1,0:T(4,128)} %copy.15) | data formatting | bytes 2097152 | tf_op jit(solution)/shard_map/reshape | solution.py:51
  140.8 1.0 convert_element_type.44
  141.7 3.2 %collective-permute-start = (bf16[64,32,128]{2,1,0:T(8,128)(2,1)}, bf16[64,32,128]{2,1,0:T(8,128)(2,1)}, u32[]{:S(2)}, u32[]{:S(2)}) collective-permute-start(bf16[64,32,128]{2,1,0:T(8,128)(2,1)} %convert_element_type.44), channel_id=1, source_target_pairs={{0,32},{32,64},{64,96},{96,128},{128,160},{160,192},{192,224},{224... | collective-permute-start | bytes 1572872 | tf_op jit(solution)/shard_map/ppermute | solution.py:18
  144.9 4.2 %collective-permute-start.1 = (bf16[64,32,128]{2,1,0:T(8,128)(2,1)}, bf16[64,32,128]{2,1,0:T(8,128)(2,1)}, u32[]{:S(2)}, u32[]{:S(2)}) collective-permute-start(bf16[64,32,128]{2,1,0:T(8,128)(2,1)} %convert_element_type.44), channel_id=1, source_target_pairs={{32,0},{64,32},{96,64},{128,96},{160,128},{192,160},{224,192},{256... | collective-permute-start | bytes 1572872 | tf_op jit(solution)/shard_map/ppermute | solution.py:18
  149.2 0.2 reshape.48
  149.4 0.1 pad_slice_fusion.1
  149.5 0.1 copy.20
  149.6 0.3 reshape.51
  149.9 8.7 %collective-permute-done = bf16[64,32,128]{2,1,0:T(8,128)(2,1)} collective-permute-done((bf16[64,32,128]{2,1,0:T(8,128)(2,1)}, bf16[64,32,128]{2,1,0:T(8,128)(2,1)}, u32[]{:S(2)}, u32[]{:S(2)}) %collective-permute-start) | collective-permute-done | bytes 524320 | tf_op jit(solution)/shard_map/ppermute | solution.py:18
  158.5 0.9 collective-permute-done.1
  159.4 1.5 pad_maximum_fusion.1
  161.0 0.6 fusion.12
  161.6 0.1 copy.19
  161.7 0.3 convolution_convert_fusion.1
  162.0 4.0 %collective-permute-start.3 = (bf16[64,32,128]{2,1,0:T(8,128)(2,1)S(1)}, bf16[64,32,128]{2,1,0:T(8,128)(2,1)}, u32[]{:S(2)}, u32[]{:S(2)}) collective-permute-start(bf16[64,32,128]{2,1,0:T(8,128)(2,1)S(1)} %convolution_convert_fusion.1), channel_id=1, source_target_pairs={{1,0},{2,1},{3,2},{4,3},{5,4},{6,5},{7,6},{8,7},{9,8},{10,9},{11,1... | collective-permute-start | bytes 1572872 | tf_op jit(solution)/shard_map/ppermute | solution.py:75
  166.1 1.9 %collective-permute-start.2 = (bf16[64,32,128]{2,1,0:T(8,128)(2,1)S(1)}, bf16[64,32,128]{2,1,0:T(8,128)(2,1)S(1)}, u32[]{:S(2)}, u32[]{:S(2)}) collective-permute-start(bf16[64,32,128]{2,1,0:T(8,128)(2,1)S(1)} %convolution_convert_fusion.1), channel_id=1, source_target_pairs={{0,1},{1,2},{2,3},{3,4},{4,5},{5,6},{6,7},{7,8},{8,9},{9,10},{10,1... | collective-permute-start | bytes 1572872 | tf_op jit(solution)/shard_map/ppermute | solution.py:74
  168.1 0.1 tile.32
  168.2 0.1 reshape.52
  168.3 1.3 collective-permute-start.6
  169.6 0.7 collective-permute-start.4
  170.3 0.4 fusion.22
  170.7 2.0 %collective-permute-done.3 = bf16[64,32,128]{2,1,0:T(8,128)(2,1)} collective-permute-done((bf16[64,32,128]{2,1,0:T(8,128)(2,1)S(1)}, bf16[64,32,128]{2,1,0:T(8,128)(2,1)}, u32[]{:S(2)}, u32[]{:S(2)}) %collective-permute-start.3) | collective-permute-done | bytes 524320 | tf_op jit(solution)/shard_map/ppermute | solution.py:75
  172.6 1.3 collective-permute-start.7
  174.0 2.6 %collective-permute-done.2 = bf16[64,32,128]{2,1,0:T(8,128)(2,1)S(1)} collective-permute-done((bf16[64,32,128]{2,1,0:T(8,128)(2,1)S(1)}, bf16[64,32,128]{2,1,0:T(8,128)(2,1)S(1)}, u32[]{:S(2)}, u32[]{:S(2)}) %collective-permute-start.2) | collective-permute-done | bytes 524320 | tf_op jit(solution)/shard_map/ppermute | solution.py:74
  176.6 1.3 collective-permute-start.5
  177.9 0.4 convolution_add_fusion.2
  178.2 1.4 convolution_add_fusion.1
  179.7 0.3 fusion.15
  180.0 0.4 collective-permute-done.5
  180.4 1.3 fusion.11
  (19 shorter events, 0.2 us)
Async XLA Ops:
  0.6 1.6 copy-start
  5.5 16.1 %copy-start.2 = (f32[3,129]{1,0:T(4,128)S(1)}, f32[3,129]{1,0:T(4,128)}, u32[]{:S(2)}) copy-start(f32[3,129]{1,0:T(4,128)} %param.5) | copy-start | bytes 4648
  5.5 120.1 %all-to-all-start = ((bf16[32,272,128]{2,1,0:T(8,128)(2,1)}), bf16[32,272,128]{2,1,0:T(8,128)(2,1)}, u32[]{:S(2)}, u32[]{:S(2)}) async-start(bf16[32,272,128]{2,1,0:T(8,128)(2,1)} %copy.12), calls=%async_computation | async-start | bytes 4456448 | tf_op jit(solution)/shard_map/all_to_all | solution.py:45
  140.8 20.2 %copy-start.1 = (f32[64,32,128]{2,1,0:T(8,128)}, f32[64,32,128]{2,1,0:T(8,128)S(1)}, u32[]{:S(2)}) copy-start(f32[64,32,128]{2,1,0:T(8,128)S(1)} %reshape.47) | copy-start | bytes 3145732
  141.7 16.8 %collective-permute-start = (bf16[64,32,128]{2,1,0:T(8,128)(2,1)}, bf16[64,32,128]{2,1,0:T(8,128)(2,1)}, u32[]{:S(2)}, u32[]{:S(2)}) collective-permute-start(bf16[64,32,128]{2,1,0:T(8,128)(2,1)} %convert_element_type.44), channel_id=1, source_target_pairs={{0,32},{32,64},{64,96},{96,128},{128,160},{160,192},{192,224},{224... | collective-permute-start | bytes 1572872 | tf_op jit(solution)/shard_map/ppermute | solution.py:18
  144.9 14.5 %collective-permute-start.1 = (bf16[64,32,128]{2,1,0:T(8,128)(2,1)}, bf16[64,32,128]{2,1,0:T(8,128)(2,1)}, u32[]{:S(2)}, u32[]{:S(2)}) collective-permute-start(bf16[64,32,128]{2,1,0:T(8,128)(2,1)} %convert_element_type.44), channel_id=1, source_target_pairs={{32,0},{64,32},{96,64},{128,96},{160,128},{192,160},{224,192},{256... | collective-permute-start | bytes 1572872 | tf_op jit(solution)/shard_map/ppermute | solution.py:18
  162.0 10.6 %collective-permute-start.3 = (bf16[64,32,128]{2,1,0:T(8,128)(2,1)S(1)}, bf16[64,32,128]{2,1,0:T(8,128)(2,1)}, u32[]{:S(2)}, u32[]{:S(2)}) collective-permute-start(bf16[64,32,128]{2,1,0:T(8,128)(2,1)S(1)} %convolution_convert_fusion.1), channel_id=1, source_target_pairs={{1,0},{2,1},{3,2},{4,3},{5,4},{6,5},{7,6},{8,7},{9,8},{10,9},{11,1... | collective-permute-start | bytes 1572872 | tf_op jit(solution)/shard_map/ppermute | solution.py:75
  166.1 10.5 %collective-permute-start.2 = (bf16[64,32,128]{2,1,0:T(8,128)(2,1)S(1)}, bf16[64,32,128]{2,1,0:T(8,128)(2,1)S(1)}, u32[]{:S(2)}, u32[]{:S(2)}) collective-permute-start(bf16[64,32,128]{2,1,0:T(8,128)(2,1)S(1)} %convolution_convert_fusion.1), channel_id=1, source_target_pairs={{0,1},{1,2},{2,3},{3,4},{4,5},{5,6},{6,7},{7,8},{8,9},{9,10},{10,1... | collective-permute-start | bytes 1572872 | tf_op jit(solution)/shard_map/ppermute | solution.py:74
  168.3 11.4 %collective-permute-start.6 = (bf16[64,32,128]{2,1,0:T(8,128)(2,1)S(1)}, bf16[64,32,128]{2,1,0:T(8,128)(2,1)S(1)}, u32[]{:S(2)}, u32[]{:S(2)}) collective-permute-start(bf16[64,32,128]{2,1,0:T(8,128)(2,1)S(1)} %convolution_convert_fusion.1), channel_id=1, source_target_pairs={{3,1},{5,3},{7,5},{9,7},{11,9},{13,11},{15,13},{17,15},{19,17},{21... | collective-permute-start | bytes 1572872 | tf_op jit(solution)/shard_map/ppermute | solution.py:77
  169.6 10.4 %collective-permute-start.4 = (bf16[64,32,128]{2,1,0:T(8,128)(2,1)S(1)}, bf16[64,32,128]{2,1,0:T(8,128)(2,1)S(1)}, u32[]{:S(2)}, u32[]{:S(2)}) collective-permute-start(bf16[64,32,128]{2,1,0:T(8,128)(2,1)S(1)} %convolution_convert_fusion.1), channel_id=1, source_target_pairs={{0,2},{2,4},{4,6},{6,8},{8,10},{10,12},{12,14},{14,16},{16,18},{18... | collective-permute-start | bytes 1572872 | tf_op jit(solution)/shard_map/ppermute | solution.py:76
  172.6 7.0 %collective-permute-start.7 = (bf16[64,32,128]{2,1,0:T(8,128)(2,1)}, bf16[64,32,128]{2,1,0:T(8,128)(2,1)S(1)}, u32[]{:S(2)}, u32[]{:S(2)}) collective-permute-start(bf16[64,32,128]{2,1,0:T(8,128)(2,1)} %collective-permute-done.3), channel_id=1, source_target_pairs={{1,0},{3,2},{5,4},{7,6},{9,8},{11,10},{13,12},{15,14},{17,16},{19,... | collective-permute-start | bytes 1572872 | tf_op jit(solution)/shard_map/ppermute | solution.py:79
  176.6 3.8 %collective-permute-start.5 = (bf16[64,32,128]{2,1,0:T(8,128)(2,1)S(1)}, bf16[64,32,128]{2,1,0:T(8,128)(2,1)S(1)}, u32[]{:S(2)}, u32[]{:S(2)}) collective-permute-start(bf16[64,32,128]{2,1,0:T(8,128)(2,1)S(1)} %collective-permute-done.2), channel_id=1, source_target_pairs={{0,1},{2,3},{4,5},{6,7},{8,9},{10,11},{12,13},{14,15},{16,17},{18,... | collective-permute-start | bytes 1572872 | tf_op jit(solution)/shard_map/ppermute | solution.py:78
